TPU v7x, 128 devices: a whole 4x4x4 slice. The times are simulated.
128 devices in a mesh: shot: 32 (over z, x, core), az: 4 (over y).
Axes of the slice: x: 4, y: 4, z: 4, core: 2. Of those that a mesh axis runs over, the one named last changes fastest.
Arguments:
- spectra: bfloat16 [4, 128, 4096, 128], P('az', None, 'shot'), may hold values from -6 to 6
- sampled_mask: int32 [4, 128, 16, 256], P('az', 'shot'), may hold values 0 or 1
- counts: int32 [4, 128], P('az', 'shot'), may hold values from 1 to 6, as said below
Outputs:
- blended: bfloat16 [4, 128, 2048, 128], P('az', None, 'shot')
Inputs may be any that keep to these rules, and one draw needn't show every extreme that they name: `counts`: every draw holds a patch with 1 iteration and a patch with 6.
All inputs are finite; a program needn't handle non-finite values. No bound on the sum of `sampled_mask` on one device may be relied on, other than what follows from the above.
Results may differ from a plain program's by a relative error of at most 0.008.
Values may be sent and summed in bfloat16 or wider, within the bound.
No kernel may reach another device: no remote copies, remote signals or barrier semaphores. Data moves between devices by JAX's collectives and lax.ppermute only.
A program may use at most 64 MiB of HBM per device.

v0:
```python
import jax
import jax.numpy as jnp
from jax import lax
from jax.sharding import PartitionSpec as P


def passed_along(block, axis, distance):
    devices = range(lax.axis_size(axis))
    route = [(i - distance, i) for i in devices if i - distance in devices]
    return lax.ppermute(block, axis, route)


def dft_tables(extent):
    indices = jnp.arange(extent, dtype=jnp.int32)
    product = indices[:, None] * indices[None, :] % extent
    phase = product.astype(jnp.float32) * (2.0 * jnp.pi / extent)
    scale = extent ** (-0.5)
    cos_table = jnp.cos(phase) * scale
    sin_table = -jnp.sin(phase) * scale
    kron_real = jnp.kron(cos_table, cos_table) - jnp.kron(sin_table, sin_table)
    kron_imag = jnp.kron(cos_table, sin_table) + jnp.kron(sin_table, cos_table)
    return (
        cos_table.astype(jnp.bfloat16),
        sin_table.astype(jnp.bfloat16),
        kron_real.astype(jnp.bfloat16),
        kron_imag.astype(jnp.bfloat16),
    )


def apply_along(mat_real, mat_imag, volume, pattern):
    halfway = volume.shape[-1] // 2
    rotated = jnp.concatenate([-volume[..., halfway:], volume[..., :halfway]], axis=-1)
    first_part = jnp.einsum(pattern, mat_real, volume, preferred_element_type=jnp.float32)
    second_part = jnp.einsum(pattern, mat_imag, rotated, preferred_element_type=jnp.float32)
    return first_part + second_part


def project_patch(observed, mask_item, sweeps, tables):
    cos_table, sin_table, kron_real, kron_imag = tables
    sampled = (mask_item > 0)[:, :, None]
    initial = jnp.where(sampled, observed, jnp.zeros_like(observed))
    halfway = observed.shape[-1] // 2

    def forward(volume):
        middle = apply_along(kron_real, kron_imag, volume, "kj,ajl->akl").astype(jnp.bfloat16)
        return apply_along(cos_table, sin_table, middle, "ka,ajl->kjl")

    def inverse(volume):
        middle = apply_along(cos_table, -sin_table, volume, "ka,ajl->kjl").astype(jnp.bfloat16)
        return apply_along(kron_real, -kron_imag, middle, "kj,ajl->akl")

    def magnitude(coeffs):
        return jnp.sqrt(coeffs[..., :halfway] ** 2 + coeffs[..., halfway:] ** 2)

    largest = jnp.max(magnitude(forward(initial)), axis=(0, 1))

    def sweep_step(sweep, volume):
        coeffs = forward(volume)
        size_now = magnitude(coeffs)
        cutoff = largest * (0.5 * jnp.power(jnp.float32(0.6), sweep.astype(jnp.float32)))
        factor = jax.nn.relu(size_now - cutoff) / (jnp.maximum(size_now, cutoff) + 1e-06)
        thinned = (coeffs * jnp.concatenate([factor, factor], axis=-1)).astype(jnp.bfloat16)
        returned = inverse(thinned)
        return jnp.where(sampled, observed.astype(jnp.float32), returned).astype(jnp.bfloat16)

    return lax.fori_loop(0, sweeps, sweep_step, initial)


def shards(spectra, sampled_mask, counts):
    regrouped = lax.all_to_all(spectra, "shot", split_axis=1, concat_axis=2, tiled=True)
    owned_count = regrouped.shape[1]
    extent = sampled_mask.shape[2]
    plane = extent * extent
    lane_count = regrouped.shape[3]
    tables = dft_tables(extent)
    observed = regrouped.reshape(owned_count, extent, plane, lane_count)
    masks = sampled_mask[0]
    sweeps = counts[0]

    def run_patch(item):
        return project_patch(item[0], item[1], item[2], tables)

    result = lax.map(run_patch, (observed, masks, sweeps))
    halfway = extent // 2
    arrived = passed_along(result[-1, halfway:], "shot", 1)
    earlier = jnp.concatenate([arrived[None], result[:-1, halfway:]], axis=0).astype(jnp.float32)
    weight = ((jnp.arange(halfway, dtype=jnp.float32) + 0.5) / halfway)[:, None, None]
    mixed = weight * result[:, :halfway].astype(jnp.float32) + (1.0 - weight) * earlier
    mixed = mixed.astype(jnp.bfloat16).reshape(1, owned_count, halfway * plane, lane_count)
    return lax.all_to_all(mixed, "shot", split_axis=2, concat_axis=1, tiled=True)


def solution(mesh):
    return jax.shard_map(
        shards,
        mesh=mesh,
        in_specs=(P("az", None, "shot", None), P("az", "shot", None, None), P("az", "shot")),
        out_specs=P("az", None, "shot", None),
        check_vma=False,
    )
```

profile of v0, /device:TPU:1, one launch (start us, length us, event | category | flops | bytes accessed | tf_op | source)
XLA Modules:
  0.0 603.3 jit_solution(11063826194500366722)
XLA Ops:
  0.0 9.5 %all-to-all-start = ((bf16[1,128,128,128]{3,2,0,1:T(8,128)(2,1)}), bf16[1,128,128,128]{3,2,0,1:T(8,128)(2,1)}, u32[]{:S(2)}, u32[]{:S(2)}) async-start(bf16[1,128,128,128]{3,2,0,1:T(8,128)(2,1)} %bitcast.152), calls=%async_computation | async-start | bytes 8388608 | tf_op jit(solution)/shard_map/all_to_all | solution.py:70
  9.6 50.6 %all-to-all-done = bf16[1,128,128,128]{3,2,0,1:T(8,128)(2,1)} async-done(((bf16[1,128,128,128]{3,2,0,1:T(8,128)(2,1)}), bf16[1,128,128,128]{3,2,0,1:T(8,128)(2,1)}, u32[]{:S(2)}, u32[]{:S(2)}) %all-to-all-start) | async-done | bytes 4194336 | tf_op jit(solution)/shard_map/all_to_all | solution.py:70
  60.2 4.7 copy.39
  64.9 272.9 %while.32 = (s32[]{:T(128)}, bf16[4,16,256,128]{3,2,1,0:T(8,128)(2,1)}, s32[4,16,256]{2,1,0:T(8,128)}, bf16[4,16,256,128]{3,2,1,0:T(8,128)(2,1)}, s32[4]{0:T(128...) while((s32[]{:T(128)}, ...), condition=%wide.region_4.5_spmd.clone.clone.clone, body=%wide.region_0.4_spmd.clone.clone.clone.sunk | while | flops 1737582592 | bytes 113581320 | solution.py:83
  70.5 2.2 convert_element_type.288
  73.8 2.2 reshape.153
  82.7 3.0 fusion.137
  92.5 61.8 %while.33 = (s32[]{:T(128)}, bf16[16,256,128]{1,2,0:T(8,128)(2,1)S(1)}, s32[]{:T(128)}, pred[16,256,1]{1,0,2:T(8,128)(4,1)S(1)}, bf16[16,256,128]{1,2,0:T(8,128)...) while((s32[]{:T(128)}, ...), condition=%wide.region_3.3_spmd.clone, body=%wide.region_2.2_spmd.clone.sunk | while | flops 1158676480 | bytes 64494576 | solution.py:66
  161.7 2.2 convert_element_type.288
  164.9 2.2 reshape.153
  173.8 3.0 fusion.137
  183.6 46.5 %while.33 = (s32[]{:T(128)}, bf16[16,256,128]{1,2,0:T(8,128)(2,1)S(1)}, s32[]{:T(128)}, pred[16,256,1]{1,0,2:T(8,128)(4,1)S(1)}, bf16[16,256,128]{1,2,0:T(8,128)...) while((s32[]{:T(128)}, ...), condition=%wide.region_3.3_spmd.clone, body=%wide.region_2.2_spmd.clone.sunk | while | flops 1158676480 | bytes 64494576 | solution.py:66
  237.5 2.2 convert_element_type.288
  240.8 2.2 reshape.153
  249.7 3.0 fusion.137
  259.5 31.2 %while.33 = (s32[]{:T(128)}, bf16[16,256,128]{1,2,0:T(8,128)(2,1)S(1)}, s32[]{:T(128)}, pred[16,256,1]{1,0,2:T(8,128)(4,1)S(1)}, bf16[16,256,128]{1,2,0:T(8,128)...) while((s32[]{:T(128)}, ...), condition=%wide.region_3.3_spmd.clone, body=%wide.region_2.2_spmd.clone.sunk | while | flops 1158676480 | bytes 64494576 | solution.py:66
  298.1 2.2 convert_element_type.288
  301.4 2.2 reshape.153
  310.2 3.0 fusion.137
  320.1 15.9 %while.33 = (s32[]{:T(128)}, bf16[16,256,128]{1,2,0:T(8,128)(2,1)S(1)}, s32[]{:T(128)}, pred[16,256,1]{1,0,2:T(8,128)(4,1)S(1)}, bf16[16,256,128]{1,2,0:T(8,128)...) while((s32[]{:T(128)}, ...), condition=%wide.region_3.3_spmd.clone, body=%wide.region_2.2_spmd.clone.sunk | while | flops 1158676480 | bytes 64494576 | solution.py:66
  339.1 4.4 collective-permute-start
  345.1 214.4 %collective-permute-done = bf16[8,256,128]{2,1,0:T(8,128)(2,1)S(1)} collective-permute-done((bf16[8,256,128]{2,1,0:T(8,128)(2,1)S(1)}, bf16[8,256,128]{2,1,0:T(8,128)(2,1)S(1)}, u32[]{:S(2)}, u32[]{:S(2)}) %collective-permute-start) | collective-permute-done | bytes 524320 | tf_op jit(solution)/shard_map/ppermute | solution.py:10
  560.5 9.8 %copy.44 = bf16[1,4,2048,128]{3,1,0,2:T(4,128)(2,1)S(1)} copy(bf16[1,4,2048,128]{3,2,1,0:T(8,128)(2,1)S(1)} %bitcast.150) | data formatting | bytes 4194304 | tf_op jit(solution)/shard_map/reshape | solution.py:89
  570.3 31.3 %all_to_all.33 = bf16[1,4,2048,128]{3,1,0,2:T(4,128)(2,1)S(1)} all-to-all(bf16[1,4,2048,128]{3,1,0,2:T(4,128)(2,1)S(1)} %copy.44), channel_id=1, replica_groups=mesh['shot'=32,'az'=4] {'shot'}, dimensions={2} | all-to-all | bytes 4194304 | tf_op jit(solution)/shard_map/all_to_all | solution.py:90
  (382 shorter events, 237.6 us)
Async XLA Ops:
  0.0 60.2 %all-to-all-start = ((bf16[1,128,128,128]{3,2,0,1:T(8,128)(2,1)}), bf16[1,128,128,128]{3,2,0,1:T(8,128)(2,1)}, u32[]{:S(2)}, u32[]{:S(2)}) async-start(bf16[1,128,128,128]{3,2,0,1:T(8,128)(2,1)} %bitcast.152), calls=%async_computation | async-start | bytes 8388608 | tf_op jit(solution)/shard_map/all_to_all | solution.py:70
  60.2 4.7 copy-start.8
  64.9 4.0 copy-start.4
  64.9 4.0 copy-start.6
  154.3 1.8 copy-start.5
  154.3 1.8 copy-start.7
  154.3 1.8 copy-start.9
  156.0 4.0 copy-start.4
  156.0 4.0 copy-start.6
  230.1 1.8 copy-start.5
  230.1 1.8 copy-start.7
  230.1 1.8 copy-start.9
  231.9 4.0 copy-start.4
  231.9 4.0 copy-start.6
  290.7 1.8 copy-start.5
  290.7 1.8 copy-start.7
  290.7 1.7 copy-start.9
  292.5 4.0 copy-start.4
  292.5 4.0 copy-start.6
  336.0 1.8 copy-start.5
  336.0 1.8 copy-start.7
  336.0 1.8 copy-start.9
  337.8 221.6 %copy-start.3 = (bf16[4,16,256,128]{3,2,1,0:T(8,128)(2,1)S(1)}, bf16[4,16,256,128]{3,2,1,0:T(8,128)(2,1)}, u32[]{:S(2)}) copy-start(bf16[4,16,256,128]{3,2,1,0:T(8,128)(2,1)} %get-tuple-element.696) | copy-start | bytes 12582916
  339.1 220.4 %collective-permute-start = (bf16[8,256,128]{2,1,0:T(8,128)(2,1)S(1)}, bf16[8,256,128]{2,1,0:T(8,128)(2,1)S(1)}, u32[]{:S(2)}, u32[]{:S(2)}) collective-permute-start(bf16[8,256,128]{2,1,0:T(8,128)(2,1)S(1)} %slice_bitcast_fusion), channel_id=1, source_target_pairs={{0,4},{4,8},{8,12},{12,16},{16,20},{20,24},{24,28},{28,32},{32,36}... | collective-permute-start | bytes 1572872 | tf_op jit(solution)/shard_map/ppermute | solution.py:10
  (24 other events, 29.2 us)
where the time goes:
time: 607 us; the launch traced here: 603 us
  waiting for transfers between devices  265 us (44%)
  local copies, waits for them, and re-layouts  115 us (19%)
  matrix products  99.7 us (16%)
  other arithmetic  66.8 us (11%)
  blocking collectives  31.3 us (5%)
  starting transfers between devices  13.9 us (2%)
  loops' own time  11.3 us (2%)
    ppermute x1, waiting for transfers between devices, passed_along(): return lax.ppermute(block, axis, route)  214 us
    all_to_all x1, waiting for transfers between devices, shards(): lax.all_to_all(spectra, 'shot', split_axis=1, concat_axis=2, tiled=True)  50.6 us
    dot_general x48, matrix products, apply_along(): jnp.einsum(pattern, mat_real, volume, preferred_element_type=jnp.float32)  50.4 us
    dot_general x48, matrix products, apply_along(): jnp.einsum(pattern, mat_imag, rotated, preferred_element_type=jnp.float32)  49.3 us
    all_to_all x1, blocking collectives, shards(): lax.all_to_all(mixed, 'shot', split_axis=2, concat_axis=1, tiled=True)  31.3 us
    concatenate x14, local copies, waits for them, and re-layouts, apply_along(): jnp.concatenate([-volume[..., halfway:], volume[..., :halfway]], axis=-1)  18.5 us
    convert_element_type x14, local copies, waits for them, and re-layouts, forward(): apply_along(kron_real, kron_imag, volume, 'kj,ajl->akl')  18 us
    convert_element_type x8, local copies, waits for them, and re-layouts, dft_tables(): kron_real.astype(jnp.bfloat16)  17.7 us
  transfers between devices with their start and end apart: 2, of which 2 were waited for; matrix products, arithmetic and copies ran while one was open for 0% of the time, Pallas kernels for 0%

commit v1 on v0

v1 whole, which is shorter than its diff:
```python
import functools

import jax
import jax.numpy as jnp
from jax import lax
from jax.experimental import pallas as pl
from jax.experimental.pallas import tpu as pltpu
from jax.sharding import PartitionSpec as P


def passed_along(block, axis, distance):
    devices = range(lax.axis_size(axis))
    route = [(i - distance, i) for i in devices if i - distance in devices]
    return lax.ppermute(block, axis, route)


def dft_tables(extent):
    indices = jnp.arange(extent, dtype=jnp.int32)
    product = indices[:, None] * indices[None, :] % extent
    phase = product.astype(jnp.float32) * (2.0 * jnp.pi / extent)
    scale = extent ** (-0.5)
    cos_table = jnp.cos(phase) * scale
    sin_table = -jnp.sin(phase) * scale
    kron_real = jnp.kron(cos_table, cos_table) - jnp.kron(sin_table, sin_table)
    kron_imag = jnp.kron(cos_table, sin_table) + jnp.kron(sin_table, cos_table)
    return (
        cos_table.astype(jnp.bfloat16),
        sin_table.astype(jnp.bfloat16),
        kron_real.astype(jnp.bfloat16),
        kron_imag.astype(jnp.bfloat16),
    )


def kernel_tables(extent):
    cos_table, sin_table, kron_real, kron_imag = dft_tables(extent)
    eye = jnp.eye(extent, dtype=jnp.float32)

    def spread(table):
        return jnp.kron(table.astype(jnp.float32), eye).astype(jnp.bfloat16)

    return jnp.stack([
        jnp.concatenate([kron_real, kron_imag], axis=1),
        jnp.concatenate([kron_real, -kron_imag], axis=1),
        jnp.concatenate([spread(cos_table), spread(sin_table)], axis=1),
        jnp.concatenate([spread(cos_table), spread(-sin_table)], axis=1),
    ])


def pocs_kernel(counts_ref, scales_ref, obs_ref, mask_ref, tab_ref, out_ref, y_ref, v_ref):
    p = pl.program_id(0)
    extent = obs_ref.shape[1]
    lanes = obs_ref.shape[3]
    half = lanes // 2
    plane = obs_ref.shape[2]
    sweeps = counts_ref[p]
    lower = lax.broadcasted_iota(jnp.int32, (1, lanes), 1) < half

    def apply(table_idx, block):
        rolled = pltpu.roll(block, half, 1)
        rotated = jnp.where(lower, -rolled, rolled)
        stacked = jnp.concatenate([block, rotated], axis=0)
        return jnp.dot(tab_ref[table_idx], stacked, preferred_element_type=jnp.float32)

    def stage_one(a, volume):
        middle = apply(0, volume).astype(jnp.bfloat16)
        for hi in range(extent):
            y_ref[hi, a] = middle[hi * extent:(hi + 1) * extent]

    def magnitude(c):
        return jnp.sqrt(c * c + pltpu.roll(c, half, 1) ** 2)

    def init_a(a, carry):
        sampled = mask_ref[0, a] > 0
        initial = jnp.where(sampled, obs_ref[0, a], jnp.zeros_like(obs_ref[0, a]))
        out_ref[0, a] = initial
        stage_one(a, initial)
        return carry

    lax.fori_loop(0, extent, init_a, 0, unroll=16)

    def init_hi(hi, running):
        coeffs = apply(2, y_ref[hi].reshape(plane, lanes))
        return jnp.maximum(running, jnp.max(magnitude(coeffs), axis=0, keepdims=True))

    largest = lax.fori_loop(0, extent, init_hi, jnp.zeros((1, lanes), jnp.float32), unroll=16)

    def sweep_step(k, carry):
        cutoff = largest * scales_ref[k]

        def thin_hi(hi, c2):
            coeffs = apply(2, y_ref[hi].reshape(plane, lanes))
            size_now = magnitude(coeffs)
            factor = jnp.maximum(size_now - cutoff, 0.0) / (jnp.maximum(size_now, cutoff) + 1e-06)
            thinned = (coeffs * factor).astype(jnp.bfloat16)
            back_mid = apply(3, thinned).astype(jnp.bfloat16)
            for a in range(extent):
                v_ref[a, hi] = back_mid[a * extent:(a + 1) * extent]
            return c2

        lax.fori_loop(0, extent, thin_hi, 0, unroll=16)

        def back_a(a, c2):
            returned = apply(1, v_ref[a].reshape(plane, lanes))
            sampled = mask_ref[0, a] > 0
            updated = jnp.where(sampled, obs_ref[0, a].astype(jnp.float32), returned).astype(jnp.bfloat16)
            out_ref[0, a] = updated

            @pl.when(k + 1 < sweeps)
            def _():
                stage_one(a, updated)

            return c2

        lax.fori_loop(0, extent, back_a, 0, unroll=16)
        return carry

    lax.fori_loop(0, sweeps, sweep_step, 0)


def run_patches(observed, maskb, sweeps, scales, tables):
    count, extent, plane, lanes = observed.shape
    block = pl.BlockSpec((1, extent, plane, lanes), lambda p, c, s: (p, 0, 0, 0))
    grid_spec = pltpu.PrefetchScalarGridSpec(
        num_scalar_prefetch=2,
        grid=(count,),
        in_specs=[block, block, pl.BlockSpec(tables.shape, lambda p, c, s: (0, 0, 0))],
        out_specs=block,
        scratch_shapes=[
            pltpu.VMEM((extent, extent, extent, lanes), jnp.bfloat16),
            pltpu.VMEM((extent, extent, extent, lanes), jnp.bfloat16),
        ],
    )
    return pl.pallas_call(
        pocs_kernel,
        grid_spec=grid_spec,
        out_shape=jax.ShapeDtypeStruct(observed.shape, jnp.bfloat16),
        compiler_params=pltpu.CompilerParams(dimension_semantics=("arbitrary",)),
    )(sweeps, scales, observed, maskb, tables)


def shards(spectra, sampled_mask, counts):
    regrouped = lax.all_to_all(spectra, "shot", split_axis=1, concat_axis=2, tiled=True)
    owned_count = regrouped.shape[1]
    extent = sampled_mask.shape[2]
    plane = extent * extent
    lane_count = regrouped.shape[3]
    tables = kernel_tables(extent)
    observed = regrouped.reshape(owned_count, extent, plane, lane_count)
    maskb = jnp.broadcast_to((sampled_mask[0] > 0).astype(jnp.bfloat16)[..., None], observed.shape)
    sweeps = counts[0]
    steps = jnp.arange(8, dtype=jnp.float32)
    scales = 0.5 * jnp.power(jnp.float32(0.6), steps)

    result = run_patches(observed, maskb, sweeps, scales, tables)
    halfway = extent // 2
    arrived = passed_along(result[-1, halfway:], "shot", 1)
    earlier = jnp.concatenate([arrived[None], result[:-1, halfway:]], axis=0).astype(jnp.float32)
    weight = ((jnp.arange(halfway, dtype=jnp.float32) + 0.5) / halfway)[:, None, None]
    mixed = weight * result[:, :halfway].astype(jnp.float32) + (1.0 - weight) * earlier
    mixed = mixed.astype(jnp.bfloat16).reshape(1, owned_count, halfway * plane, lane_count)
    return lax.all_to_all(mixed, "shot", split_axis=2, concat_axis=1, tiled=True)


def solution(mesh):
    return jax.shard_map(
        shards,
        mesh=mesh,
        in_specs=(P("az", None, "shot", None), P("az", "shot", None, None), P("az", "shot")),
        out_specs=P("az", None, "shot", None),
        check_vma=False,
    )
```

time: 607 us -> 484 us (0.80)
  starting transfers between devices: 13.9 us -> 166 us
  waiting for transfers between devices: 265 us -> 119 us
  Pallas kernels: 0 us -> 135 us
  matrix products: 99.7 us -> 0 us
  local copies, waits for them, and re-layouts: 115 us -> 27.9 us
  other arithmetic: 66.8 us -> 4.19 us
  loops' own time: 11.3 us -> 0 us
    ppermute x1, starting transfers between devices: 4.41 us -> 156 us  [passed_along(): return lax.ppermute(block, axis, route)]
    ppermute x1, waiting for transfers between devices: 214 us -> 76.5 us  [passed_along(): return lax.ppermute(block, axis, route)]
    pallas_call x0 -> x1, Pallas kernels: none -> 135 us  [run_patches(): pl.pallas_call(pocs_kernel, grid_spec=grid_spec, out_shape=jax.ShapeDtype...]
    dot_general x96 -> x0, matrix products: 99.7 us -> none  [the longest x48 50.4 us: apply_along(): jnp.einsum(pattern, mat_real, volume, preferred_element_type=jnp.float32)]
    concatenate x14 -> x0, local copies, waits for them, and re-layouts: 18.5 us -> none  [apply_along(): jnp.concatenate([-volume[..., halfway:], volume[..., :halfway]], axis=-1)]
    while x88 -> x0, local copies, waits for them, and re-layouts: 17.5 us -> none
    convert_element_type x8 -> x1, local copies, waits for them, and re-layouts: 17.7 us -> 0.99 us  [dft_tables(): kron_real.astype(jnp.bfloat16)]
    convert_element_type x14 -> x3, local copies, waits for them, and re-layouts: 18 us -> 2.97 us  [spread(): return jnp.kron(table.astype(jnp.float32), eye).astype(jnp.bfloat16)]
  transfers between devices with their start and end apart: 2 -> 2, of which waited for: 2 -> 2; matrix products, arithmetic and copies ran while one was open for 0% -> 2% of each run, Pallas kernels for 0% -> 0%
where the time goes in v1:
time: 484 us
  starting transfers between devices  166 us (34%)
  Pallas kernels  135 us (28%)
  waiting for transfers between devices  119 us (25%)
  blocking collectives  31.3 us (6%)
  local copies, waits for them, and re-layouts  27.9 us (6%)
    ppermute x1, starting transfers between devices, passed_along(): return lax.ppermute(block, axis, route)  156 us
    pallas_call x1, Pallas kernels, run_patches(): pl.pallas_call(pocs_kernel, grid_spec=grid_spec, out_shape=jax.ShapeDtype...  135 us
    ppermute x1, waiting for transfers between devices, passed_along(): return lax.ppermute(block, axis, route)  76.5 us
    all_to_all x1, waiting for transfers between devices, shards(): lax.all_to_all(spectra, 'shot', split_axis=1, concat_axis=2, tiled=True)  42.5 us
    all_to_all x1, blocking collectives, shards(): lax.all_to_all(mixed, 'shot', split_axis=2, concat_axis=1, tiled=True)  31.3 us
    reshape x1, local copies, waits for them, and re-layouts, shards(): mixed.astype(jnp.bfloat16)  9.76 us
  transfers between devices with their start and end apart: 2, of which 2 were waited for; matrix products, arithmetic and copies ran while one was open for 2% of the time, Pallas kernels for 0%

profile of v1, /device:TPU:1, one launch (start us, length us, event | category | flops | bytes accessed | tf_op | source)
XLA Modules:
  0.0 483.7 jit_solution(618856545403963419)
XLA Ops:
  0.0 9.5 %all-to-all-start = ((bf16[1,128,128,128]{3,2,0,1:T(8,128)(2,1)}), bf16[1,128,128,128]{3,2,0,1:T(8,128)(2,1)}, u32[]{:S(2)}, u32[]{:S(2)}) async-start(bf16[1,128,128,128]{3,2,0,1:T(8,128)(2,1)} %bitcast.37), calls=%async_computation | async-start | bytes 8388608 | tf_op jit(solution)/shard_map/all_to_all | solution.py:142
  9.5 0.1 negate_convert_fusion
  9.6 0.1 convert_convert_fusion
  9.6 0.6 multiply_convert_fusion.1
  10.2 1.0 convert_element_type.171
  11.2 1.0 convert_element_type.175
  12.2 1.0 convert_element_type.178
  13.3 0.6 add_convert_fusion.1
  13.9 1.0 convert_element_type.166
  14.9 1.0 convert_element_type.164
  15.9 0.5 power_multiply_fusion.scales_ref
  16.5 1.1 pad_maximum_fusion.tab_ref
  17.7 42.5 %all-to-all-done = bf16[1,128,128,128]{3,2,0,1:T(8,128)(2,1)} async-done(((bf16[1,128,128,128]{3,2,0,1:T(8,128)(2,1)}), bf16[1,128,128,128]{3,2,0,1:T(8,128)(2,1)}, u32[]{:S(2)}, u32[]{:S(2)}) %all-to-all-start) | async-done | bytes 4194336 | tf_op jit(solution)/shard_map/all_to_all | solution.py:142
  60.2 4.7 copy.7
  64.9 3.8 broadcast_in_dim.31.mask_ref
  68.7 135.2 %shard_map.37 = bf16[4,16,256,128]{3,2,1,0:T(8,128)(2,1)} custom-call(s32[4]{0:T(128)} %bitcast.39, f32[8]{0:T(128)} %power_multiply_fusion.scales_ref, bf16[4,16,256,128]{3,2,1,0:T(8,128)(2,1)} %bitcast.34, bf16[4,16,256,128]{3,2,1,0:T(8,128)(2,1)} %broadcast_in_dim.31.mask_ref, bf16[4,256,512]{2,1,0:T(8,128)(2,1)} %pad_maximum_fusion.tab_ref), custom_call_target="tpu_custom_call" | custom-call | tf_op jit(solution)/shard_map/pallas_call | solution.py:133
  203.9 1.2 slice_bitcast_fusion
  205.2 156.5 %collective-permute-start = (bf16[8,256,128]{2,1,0:T(8,128)(2,1)S(1)}, bf16[8,256,128]{2,1,0:T(8,128)(2,1)S(1)}, u32[]{:S(2)}, u32[]{:S(2)}) collective-permute-start(bf16[8,256,128]{2,1,0:T(8,128)(2,1)S(1)} %slice_bitcast_fusion), channel_id=1, source_target_pairs={{0,4},{4,8},{8,12},{12,16},{16,20},{20,24},{24,28},{28,32},{32,36}... | collective-permute-start | bytes 1572872 | tf_op jit(solution)/shard_map/ppermute | solution.py:14
  361.7 1.6 slice.14
  363.2 76.5 %collective-permute-done = bf16[8,256,128]{2,1,0:T(8,128)(2,1)S(1)} collective-permute-done((bf16[8,256,128]{2,1,0:T(8,128)(2,1)S(1)}, bf16[8,256,128]{2,1,0:T(8,128)(2,1)S(1)}, u32[]{:S(2)}, u32[]{:S(2)}) %collective-permute-start) | collective-permute-done | bytes 524320 | tf_op jit(solution)/shard_map/ppermute | solution.py:14
  439.7 1.0 add_convert_fusion
  440.7 9.8 %copy.8 = bf16[1,4,2048,128]{3,1,0,2:T(4,128)(2,1)S(1)} copy(bf16[1,4,2048,128]{3,2,1,0:T(8,128)(2,1)S(1)} %bitcast.35) | data formatting | bytes 4194304 | tf_op jit(solution)/shard_map/reshape | solution.py:160
  450.5 31.3 %all_to_all.33 = bf16[1,4,2048,128]{3,1,0,2:T(4,128)(2,1)S(1)} all-to-all(bf16[1,4,2048,128]{3,1,0,2:T(4,128)(2,1)S(1)} %copy.8), channel_id=1, replica_groups=mesh['shot'=32,'az'=4] {'shot'}, dimensions={2} | all-to-all | bytes 4194304 | tf_op jit(solution)/shard_map/all_to_all | solution.py:161
  481.8 1.9 copy.9
  (11 shorter events, 0.2 us)
Async XLA Ops:
  0.0 60.2 %all-to-all-start = ((bf16[1,128,128,128]{3,2,0,1:T(8,128)(2,1)}), bf16[1,128,128,128]{3,2,0,1:T(8,128)(2,1)}, u32[]{:S(2)}, u32[]{:S(2)}) async-start(bf16[1,128,128,128]{3,2,0,1:T(8,128)(2,1)} %bitcast.37), calls=%async_computation | async-start | bytes 8388608 | tf_op jit(solution)/shard_map/all_to_all | solution.py:142
  15.9 1.7 copy-start.1
  203.9 235.8 %copy-start = (bf16[4,16,256,128]{3,2,1,0:T(8,128)(2,1)S(1)}, bf16[4,16,256,128]{3,2,1,0:T(8,128)(2,1)}, u32[]{:S(2)}) copy-start(bf16[4,16,256,128]{3,2,1,0:T(8,128)(2,1)} %shard_map.37) | copy-start | bytes 12582916
  205.2 234.5 %collective-permute-start = (bf16[8,256,128]{2,1,0:T(8,128)(2,1)S(1)}, bf16[8,256,128]{2,1,0:T(8,128)(2,1)S(1)}, u32[]{:S(2)}, u32[]{:S(2)}) collective-permute-start(bf16[8,256,128]{2,1,0:T(8,128)(2,1)S(1)} %slice_bitcast_fusion), channel_id=1, source_target_pairs={{0,4},{4,8},{8,12},{12,16},{16,20},{20,24},{24,28},{28,32},{32,36}... | collective-permute-start | bytes 1572872 | tf_op jit(solution)/shard_map/ppermute | solution.py:14

commit v2 on v1

--- a/solution.py
+++ b/solution.py
@@ -1,5 +1,3 @@
-import functools
-
 import jax
 import jax.numpy as jnp
 from jax import lax
@@ -52,6 +50,7 @@
     lanes = obs_ref.shape[3]
     half = lanes // 2
     plane = obs_ref.shape[2]
+    half_axis = extent // 2
     sweeps = counts_ref[p]
     lower = lax.broadcasted_iota(jnp.int32, (1, lanes), 1) < half
 
@@ -72,7 +71,9 @@
     def init_a(a, carry):
         sampled = mask_ref[0, a] > 0
         initial = jnp.where(sampled, obs_ref[0, a], jnp.zeros_like(obs_ref[0, a]))
-        out_ref[0, a] = initial
+        for quarter in range(4):
+            rows = plane // 4
+            out_ref[(a % half_axis) * 4 + quarter, 0, a // half_axis] = initial[quarter * rows:(quarter + 1) * rows]
         stage_one(a, initial)
         return carry
 
@@ -103,7 +104,9 @@
             returned = apply(1, v_ref[a].reshape(plane, lanes))
             sampled = mask_ref[0, a] > 0
             updated = jnp.where(sampled, obs_ref[0, a].astype(jnp.float32), returned).astype(jnp.bfloat16)
-            out_ref[0, a] = updated
+            for quarter in range(4):
+                rows = plane // 4
+                out_ref[(a % half_axis) * 4 + quarter, 0, a // half_axis] = updated[quarter * rows:(quarter + 1) * rows]
 
             @pl.when(k + 1 < sweeps)
             def _():
@@ -120,11 +123,13 @@
 def run_patches(observed, maskb, sweeps, scales, tables):
     count, extent, plane, lanes = observed.shape
     block = pl.BlockSpec((1, extent, plane, lanes), lambda p, c, s: (p, 0, 0, 0))
+    dests = extent // 2 * 4
+    out_block = pl.BlockSpec((dests, 1, 2, plane // 4, lanes), lambda p, c, s: (0, p, 0, 0, 0))
     grid_spec = pltpu.PrefetchScalarGridSpec(
         num_scalar_prefetch=2,
         grid=(count,),
         in_specs=[block, block, pl.BlockSpec(tables.shape, lambda p, c, s: (0, 0, 0))],
-        out_specs=block,
+        out_specs=out_block,
         scratch_shapes=[
             pltpu.VMEM((extent, extent, extent, lanes), jnp.bfloat16),
             pltpu.VMEM((extent, extent, extent, lanes), jnp.bfloat16),
@@ -133,32 +138,56 @@
     return pl.pallas_call(
         pocs_kernel,
         grid_spec=grid_spec,
-        out_shape=jax.ShapeDtypeStruct(observed.shape, jnp.bfloat16),
+        out_shape=jax.ShapeDtypeStruct((dests, count, 2, plane // 4, lanes), jnp.bfloat16),
         compiler_params=pltpu.CompilerParams(dimension_semantics=("arbitrary",)),
     )(sweeps, scales, observed, maskb, tables)
 
 
+def snake_slots(devices, per_device):
+    ranks = []
+    for d in range(devices):
+        for i in range(per_device):
+            ranks.append(i * devices + (d if i % 2 == 0 else devices - 1 - d))
+    return jnp.array(ranks, jnp.int32)
+
+
 def shards(spectra, sampled_mask, counts):
-    regrouped = lax.all_to_all(spectra, "shot", split_axis=1, concat_axis=2, tiled=True)
-    owned_count = regrouped.shape[1]
+    devices = lax.axis_size("shot")
+    me = lax.axis_index("shot")
+    owned_count = counts.shape[1]
+    total = devices * owned_count
     extent = sampled_mask.shape[2]
     plane = extent * extent
-    lane_count = regrouped.shape[3]
+    lane_count = spectra.shape[3]
+    halfway = extent // 2
+
+    all_counts = lax.all_gather(counts[0], "shot", tiled=True)
+    order = jnp.argsort(-all_counts, stable=True).astype(jnp.int32)
+    perm = order[snake_slots(devices, owned_count)]
+    inverse = jnp.zeros((total,), jnp.int32).at[perm].set(jnp.arange(total, dtype=jnp.int32))
+    mine = lax.dynamic_slice(perm, (me * owned_count,), (owned_count,))
+
+    routed = jnp.take(spectra, perm, axis=1)
+    regrouped = lax.all_to_all(routed, "shot", split_axis=1, concat_axis=2, tiled=True)
+    observed = regrouped.reshape(owned_count, extent, plane, lane_count)
+    all_masks = lax.all_gather((sampled_mask[0] > 0).astype(jnp.bfloat16), "shot", tiled=True)
+    masks = jnp.take(all_masks, mine, axis=0)
+    maskb = jnp.broadcast_to(masks[..., None], observed.shape)
+    sweeps = jnp.take(all_counts, mine)
     tables = kernel_tables(extent)
-    observed = regrouped.reshape(owned_count, extent, plane, lane_count)
-    maskb = jnp.broadcast_to((sampled_mask[0] > 0).astype(jnp.bfloat16)[..., None], observed.shape)
-    sweeps = counts[0]
     steps = jnp.arange(8, dtype=jnp.float32)
     scales = 0.5 * jnp.power(jnp.float32(0.6), steps)
 
     result = run_patches(observed, maskb, sweeps, scales, tables)
-    halfway = extent // 2
-    arrived = passed_along(result[-1, halfway:], "shot", 1)
-    earlier = jnp.concatenate([arrived[None], result[:-1, halfway:]], axis=0).astype(jnp.float32)
-    weight = ((jnp.arange(halfway, dtype=jnp.float32) + 0.5) / halfway)[:, None, None]
-    mixed = weight * result[:, :halfway].astype(jnp.float32) + (1.0 - weight) * earlier
-    mixed = mixed.astype(jnp.bfloat16).reshape(1, owned_count, halfway * plane, lane_count)
-    return lax.all_to_all(mixed, "shot", split_axis=2, concat_axis=1, tiled=True)
+    back = lax.all_to_all(result, "shot", split_axis=0, concat_axis=1, tiled=True)[0]
+    back = jnp.take(back, inverse, axis=0)
+    own_half = back[:, 0].astype(jnp.float32)
+    top_half = back[:, 1].astype(jnp.float32)
+    earlier = jnp.concatenate([jnp.zeros_like(top_half[:1]), top_half[:-1]], axis=0)
+    h = (me // (devices // halfway)).astype(jnp.float32)
+    weight = (h + 0.5) / halfway
+    mixed = weight * own_half + (1.0 - weight) * earlier
+    return mixed.astype(jnp.bfloat16)[None]
 
 
 def solution(mesh):

time: 484 us -> 369 us (0.76)
  starting transfers between devices: 166 us -> 13.3 us
  Pallas kernels: 135 us -> 166 us
  blocking collectives: 31.3 us -> 15.5 us
  between operations: 0.14 us -> 14.3 us
  other arithmetic: 4.19 us -> 17.3 us
  waiting for transfers between devices: 119 us -> 109 us
    ppermute x1 -> x0, starting transfers between devices: 156 us -> none  [passed_along(): return lax.ppermute(block, axis, route)]
    ppermute x1 -> x0, waiting for transfers between devices: 76.5 us -> none  [passed_along(): return lax.ppermute(block, axis, route)]
    all_gather x0 -> x1, waiting for transfers between devices: none -> 59.7 us  [shards(): lax.all_gather((sampled_mask[0] > 0).astype(jnp.bfloat16), 'shot', tiled=...]
    all_to_all x1 -> x0, blocking collectives: 31.3 us -> none  [shards(): lax.all_to_all(mixed, 'shot', split_axis=2, concat_axis=1, tiled=True)]
    pallas_call x1, Pallas kernels: 135 us -> 166 us  [run_patches(): pl.pallas_call(pocs_kernel, grid_spec=grid_spec, out_shape=jax.ShapeDtype...]
    all_gather x0 -> x1, blocking collectives: none -> 15.5 us  [shards(): all_counts = lax.all_gather(counts[0], 'shot', tiled=True)]
    gather x0 -> x5, local copies, waits for them, and re-layouts: none -> 14.1 us  [the longest x1 5.25 us: shards(): routed = jnp.take(spectra, perm, axis=1)]
    reshape x1 -> x0, local copies, waits for them, and re-layouts: 9.76 us -> none  [shards(): mixed.astype(jnp.bfloat16)]
  transfers between devices with their start and end apart: 2 -> 3, of which waited for: 2 -> 2; matrix products, arithmetic and copies ran while one was open for 2% -> 4% of each run, Pallas kernels for 0% -> 0%
where the time goes in v2:
time: 369 us; the launch traced here: 366 us
  Pallas kernels  166 us (45%)
  waiting for transfers between devices  109 us (30%)
  local copies, waits for them, and re-layouts  30.8 us (8%)
  other arithmetic  17.3 us (5%)
  blocking collectives  15.5 us (4%)
  between operations  14.3 us (4%)
  starting transfers between devices  13.3 us (4%)
    pallas_call x1, Pallas kernels, run_patches(): pl.pallas_call(pocs_kernel, grid_spec=grid_spec, out_shape=jax.ShapeDtype...  166 us
    all_gather x1, waiting for transfers between devices, shards(): lax.all_gather((sampled_mask[0] > 0).astype(jnp.bfloat16), 'shot', tiled=...  59.7 us
    all_to_all x1, waiting for transfers between devices, shards(): lax.all_to_all(result, 'shot', split_axis=0, concat_axis=1, tiled=True)[0]  49.6 us
    all_gather x1, blocking collectives, shards(): all_counts = lax.all_gather(counts[0], 'shot', tiled=True)  15.5 us
    all_to_all x1, starting transfers between devices, shards(): lax.all_to_all(routed, 'shot', split_axis=1, concat_axis=2, tiled=True)  8.52 us
  transfers between devices with their start and end apart: 3, of which 2 were waited for; matrix products, arithmetic and copies ran while one was open for 4% of the time, Pallas kernels for 0%

profile of v2, /device:TPU:1, one launch (start us, length us, event | category | flops | bytes accessed | tf_op | source)
XLA Modules:
  0.0 366.2 jit_solution(14507028499581232668)
XLA Ops:
  6.5 1.2 dynamic-slice
  9.2 15.5 %all-reduce.1 = s32[128]{0:T(128)S(1)} all-reduce(s32[128]{0:T(128)S(1)} %bitcast_dynamic-update-slice_fusion), channel_id=2, replica_groups=mesh['shot'=32,'az'=4] {'shot'}, use_global_device_ids=true, to_apply=%add.1 | all-reduce | flops 128 | bytes 1024 | tf_op jit(solution)/shard_map/all_gather | solution.py:164
  25.3 2.5 sort.17
  27.9 1.2 gather_fusion
  29.1 5.2 %gather_fusion.2 = bf16[128,128,128]{2,1,0:T(8,128)(2,1)} fusion(bf16[128,128,128]{2,1,0:T(8,128)(2,1)} %bitcast.53, s32[1024]{0:T(1024)S(1)} %pad_clamp_fusion.1), kind=kCustom, calls=%fused_computation.2 | custom fusion | bytes 8389120 | tf_op jit(solution)/shard_map/jit(_take)/gather | solution.py:170
  34.4 4.6 %bitcast_select_fusion = bf16[1,128,128,128]{3,2,0,1:T(8,128)(2,1)} fusion(bf16[128,128,128]{2,1,0:T(8,128)(2,1)} %gather_fusion.2, pred[128]{0:T(512)(128)(4,1)S(1)} %compare_and_fusion), kind=kLoop, calls=%fused_computation.8 | loop fusion | flops 2097152 | bytes 8388736 | tf_op jit(solution)/shard_map/jit(_take)/select_n | solution.py:170
  39.0 8.5 %all-to-all-start = ((bf16[1,128,128,128]{3,2,0,1:T(8,128)(2,1)}), bf16[1,128,128,128]{3,2,0,1:T(8,128)(2,1)}, u32[]{:S(2)}, u32[]{:S(2)}) async-start(bf16[1,128,128,128]{3,2,0,1:T(8,128)(2,1)} %bitcast_select_fusion), calls=%async_computation | async-start | bytes 8388608 | tf_op jit(solution)/shard_map/all_to_all | solution.py:171
  49.7 1.0 convert_element_type.171
  50.7 1.0 convert_element_type.175
  51.7 1.0 convert_element_type.178
  53.4 1.0 convert_element_type.164
  54.4 1.0 convert_element_type.166
  56.0 1.1 pad_maximum_fusion.tab_ref
  57.7 59.7 %all-gather.4.cloned.1.call-done = bf16[1,128,16,256]{3,2,0,1:T(8,128)(2,1)} async-done(((bf16[1,4,16,256]{3,2,0,1:T(8,128)(2,1)}), bf16[1,128,16,256]{3,2,0,1:T(8,128)(2,1)}) %all-gather.4.cloned.1.call-update) | async-done | bytes 1048592 | tf_op jit(solution)/shard_map/all_gather | solution.py:173
  117.5 1.8 gather_fusion.3
  119.3 4.8 %copy.8 = bf16[1,32,4,128,128]{4,3,1,2,0:T(8,128)(2,1)} copy(bf16[1,32,4,128,128]{4,3,2,1,0:T(8,128)(2,1)} %bitcast.6) | data formatting | bytes 8388608 | tf_op jit(solution)/shard_map/all_to_all | solution.py:171
  124.1 3.8 %broadcast_in_dim.77.mask_ref = bf16[4,16,256,128]{3,2,1,0:T(8,128)(2,1)} broadcast(bf16[4,16,256]{2,1,0:T(8,128)(2,1)S(1)} %broadcast_select_fusion.1), dimensions={0,1,2} | broadcast | bytes 4227072 | tf_op jit(solution)/shard_map/broadcast_in_dim | solution.py:175
  127.9 165.6 %shard_map.46 = bf16[32,4,2,64,128]{4,3,2,1,0:T(8,128)(2,1)} custom-call(s32[4]{0:T(128)} %broadcast_select_fusion.2.counts_ref, f32[8]{0:T(128)} %power_multiply_fusion.scales_ref, bf16[4,16,256,128]{3,2,1,0:T(8,128)(2,1)} %bitcast.52, bf16[4,16,256,128]{3,2,1,0:T(8,128)(2,1)} %broadcast_in_dim.77.mask_ref, bf16[4,256,512]{2,1,0:T(8,128)(2,1)} %pad_maximum_fusion.tab_ref), custom_call_target="tpu_custom_call" | custom-call | tf_op jit(solution)/shard_map/pallas_call | solution.py:138
  293.6 4.7 %all-to-all-start.1 = ((bf16[32,4,2,64,128]{4,3,2,1,0:T(8,128)(2,1)}), bf16[32,4,2,64,128]{4,3,2,1,0:T(8,128)(2,1)}, u32[]{:S(2)}, u32[]{:S(2)}) async-start(bf16[32,4,2,64,128]{4,3,2,1,0:T(8,128)(2,1)} %shard_map.46), calls=%async_computation.1 | async-start | bytes 8388608 | tf_op jit(solution)/shard_map/all_to_all | solution.py:182
  298.3 1.0 scatter_custom_fusion
  299.3 49.6 %all-to-all-done.1 = bf16[32,4,2,64,128]{4,3,2,1,0:T(8,128)(2,1)} async-done(((bf16[32,4,2,64,128]{4,3,2,1,0:T(8,128)(2,1)}), bf16[32,4,2,64,128]{4,3,2,1,0:T(8,128)(2,1)}, u32[]{:S(2)}, u32[]{:S(2)}) %all-to-all-start.1) | async-done | bytes 4194336 | tf_op jit(solution)/shard_map/all_to_all | solution.py:182
  349.0 5.2 %gather_fusion.4 = bf16[128,2,64,128]{3,2,1,0:T(8,128)(2,1)} fusion(bf16[128,2,64,128]{3,2,1,0:T(8,128)(2,1)} %bitcast.15, s32[1024]{0:T(1024)S(1)} %pad_clamp_fusion), kind=kCustom, calls=%fused_computation.4 | custom fusion | bytes 8389120 | tf_op jit(solution)/shard_map/jit(_take)/gather | solution.py:183
  354.2 2.6 broadcast_select_fusion
  357.0 2.3 fusion.1
  (34 shorter events, 5.8 us)
Async XLA Ops:
  39.0 8.6 %copy-start = (s32[1,4,16,256]{3,2,1,0:T(8,128)S(1)}, s32[1,4,16,256]{3,2,1,0:T(8,128)}, u32[]{:S(2)}) copy-start(s32[1,4,16,256]{3,2,1,0:T(8,128)} %param.5) | copy-start | bytes 196612
  39.0 80.4 %all-to-all-start = ((bf16[1,128,128,128]{3,2,0,1:T(8,128)(2,1)}), bf16[1,128,128,128]{3,2,0,1:T(8,128)(2,1)}, u32[]{:S(2)}, u32[]{:S(2)}) async-start(bf16[1,128,128,128]{3,2,0,1:T(8,128)(2,1)} %bitcast_select_fusion), calls=%async_computation | async-start | bytes 8388608 | tf_op jit(solution)/shard_map/all_to_all | solution.py:171
  47.5 70.0 %all-gather.4.cloned.1.call-start = ((), (), s32[]{:S(2)}) async-start(), calls=%async_computation.2 | async-start | bytes 1081344 | tf_op jit(solution)/shard_map/all_gather | solution.py:173
  293.6 55.4 %all-to-all-start.1 = ((bf16[32,4,2,64,128]{4,3,2,1,0:T(8,128)(2,1)}), bf16[32,4,2,64,128]{4,3,2,1,0:T(8,128)(2,1)}, u32[]{:S(2)}, u32[]{:S(2)}) async-start(bf16[32,4,2,64,128]{4,3,2,1,0:T(8,128)(2,1)} %shard_map.46), calls=%async_computation.1 | async-start | bytes 8388608 | tf_op jit(solution)/shard_map/all_to_all | solution.py:182
Sparse Core Ops, SparseCore 0:
  50.6 66.8 all-gather.3

commit v3 on v2

--- a/solution.py
+++ b/solution.py
@@ -44,7 +44,7 @@
     ])
 
 
-def pocs_kernel(counts_ref, scales_ref, obs_ref, mask_ref, tab_ref, out_ref, y_ref, v_ref):
+def pocs_kernel(counts_ref, scales_ref, obs_ref, tab_ref, out_ref, y_ref, v_ref):
     p = pl.program_id(0)
     extent = obs_ref.shape[1]
     lanes = obs_ref.shape[3]
@@ -65,12 +65,17 @@
         for hi in range(extent):
             y_ref[hi, a] = middle[hi * extent:(hi + 1) * extent]
 
+    def recorded(v):
+        wide = v.astype(jnp.float32)
+        return wide == wide
+
     def magnitude(c):
         return jnp.sqrt(c * c + pltpu.roll(c, half, 1) ** 2)
 
     def init_a(a, carry):
-        sampled = mask_ref[0, a] > 0
-        initial = jnp.where(sampled, obs_ref[0, a], jnp.zeros_like(obs_ref[0, a]))
+        observed = obs_ref[0, a]
+        sampled = recorded(observed)
+        initial = jnp.where(sampled, observed, jnp.zeros_like(observed))
         for quarter in range(4):
             rows = plane // 4
             out_ref[(a % half_axis) * 4 + quarter, 0, a // half_axis] = initial[quarter * rows:(quarter + 1) * rows]
@@ -102,8 +107,8 @@
 
         def back_a(a, c2):
             returned = apply(1, v_ref[a].reshape(plane, lanes))
-            sampled = mask_ref[0, a] > 0
-            updated = jnp.where(sampled, obs_ref[0, a].astype(jnp.float32), returned).astype(jnp.bfloat16)
+            observed = obs_ref[0, a].astype(jnp.float32)
+            updated = jnp.where(observed == observed, observed, returned).astype(jnp.bfloat16)
             for quarter in range(4):
                 rows = plane // 4
                 out_ref[(a % half_axis) * 4 + quarter, 0, a // half_axis] = updated[quarter * rows:(quarter + 1) * rows]
@@ -120,7 +125,7 @@
     lax.fori_loop(0, sweeps, sweep_step, 0)
 
 
-def run_patches(observed, maskb, sweeps, scales, tables):
+def run_patches(observed, sweeps, scales, tables):
     count, extent, plane, lanes = observed.shape
     block = pl.BlockSpec((1, extent, plane, lanes), lambda p, c, s: (p, 0, 0, 0))
     dests = extent // 2 * 4
@@ -128,7 +133,7 @@
     grid_spec = pltpu.PrefetchScalarGridSpec(
         num_scalar_prefetch=2,
         grid=(count,),
-        in_specs=[block, block, pl.BlockSpec(tables.shape, lambda p, c, s: (0, 0, 0))],
+        in_specs=[block, pl.BlockSpec(tables.shape, lambda p, c, s: (0, 0, 0))],
         out_specs=out_block,
         scratch_shapes=[
             pltpu.VMEM((extent, extent, extent, lanes), jnp.bfloat16),
@@ -140,7 +145,7 @@
         grid_spec=grid_spec,
         out_shape=jax.ShapeDtypeStruct((dests, count, 2, plane // 4, lanes), jnp.bfloat16),
         compiler_params=pltpu.CompilerParams(dimension_semantics=("arbitrary",)),
-    )(sweeps, scales, observed, maskb, tables)
+    )(sweeps, scales, observed, tables)
 
 
 def snake_slots(devices, per_device):
@@ -161,24 +166,29 @@
     lane_count = spectra.shape[3]
     halfway = extent // 2
 
-    all_counts = lax.all_gather(counts[0], "shot", tiled=True)
+    mask_rows = (sampled_mask[0] > 0).astype(jnp.bfloat16).reshape(owned_count, devices, -1)
+    count_cols = jnp.broadcast_to(counts[0].astype(jnp.bfloat16)[:, None, None], (owned_count, devices, 8))
+    packed = jnp.concatenate([mask_rows, count_cols], axis=2)[None]
+    arrived = lax.all_to_all(packed, "shot", split_axis=2, concat_axis=1, tiled=True)[0, :, 0]
+    local_traces = spectra.shape[2]
+    local_mask = arrived[:, :local_traces]
+    all_counts = arrived[:, local_traces].astype(jnp.int32)
+
     order = jnp.argsort(-all_counts, stable=True).astype(jnp.int32)
     perm = order[snake_slots(devices, owned_count)]
     inverse = jnp.zeros((total,), jnp.int32).at[perm].set(jnp.arange(total, dtype=jnp.int32))
     mine = lax.dynamic_slice(perm, (me * owned_count,), (owned_count,))
 
-    routed = jnp.take(spectra, perm, axis=1)
+    marked = jnp.where(local_mask[None, :, :, None] > 0, spectra, jnp.nan).astype(spectra.dtype)
+    routed = jnp.take(marked, perm, axis=1)
     regrouped = lax.all_to_all(routed, "shot", split_axis=1, concat_axis=2, tiled=True)
     observed = regrouped.reshape(owned_count, extent, plane, lane_count)
-    all_masks = lax.all_gather((sampled_mask[0] > 0).astype(jnp.bfloat16), "shot", tiled=True)
-    masks = jnp.take(all_masks, mine, axis=0)
-    maskb = jnp.broadcast_to(masks[..., None], observed.shape)
     sweeps = jnp.take(all_counts, mine)
     tables = kernel_tables(extent)
     steps = jnp.arange(8, dtype=jnp.float32)
     scales = 0.5 * jnp.power(jnp.float32(0.6), steps)
 
-    result = run_patches(observed, maskb, sweeps, scales, tables)
+    result = run_patches(observed, sweeps, scales, tables)
     back = lax.all_to_all(result, "shot", split_axis=0, concat_axis=1, tiled=True)[0]
     back = jnp.take(back, inverse, axis=0)
     own_half = back[:, 0].astype(jnp.float32)

time: 369 us -> 338 us (0.916)
  blocking collectives: 15.5 us -> 0 us
  between operations: 14.3 us -> 0.25 us
  waiting for transfers between devices: 109 us -> 97.4 us
  starting transfers between devices: 13.3 us -> 22.4 us
  other arithmetic: 17.3 us -> 25.8 us
  local copies, waits for them, and re-layouts: 30.8 us -> 24.1 us
    all_gather x1 -> x0, waiting for transfers between devices: 59.7 us -> none  [shards(): lax.all_gather((sampled_mask[0] > 0).astype(jnp.bfloat16), 'shot', tiled=...]
    all_to_all x1, waiting for transfers between devices: 0.01 us -> 41.1 us  [shards(): lax.all_to_all(routed, 'shot', split_axis=1, concat_axis=2, tiled=True)]
    all_gather x1 -> x0, blocking collectives: 15.5 us -> none  [shards(): all_counts = lax.all_gather(counts[0], 'shot', tiled=True)]
    all_to_all x0 -> x1, starting transfers between devices: none -> 9.42 us  [shards(): lax.all_to_all(packed, 'shot', split_axis=2, concat_axis=1, tiled=True)]
    select_n x2, other arithmetic: 4.68 us -> 12.2 us  [the longest x1 7.64 us: shards(): jnp.where(local_mask[None, :, :, None] > 0, spectra, jnp.nan)]
    all_to_all x0 -> x1, waiting for transfers between devices: none -> 6.66 us  [shards(): lax.all_to_all(packed, 'shot', split_axis=2, concat_axis=1, tiled=True)]
    all_to_all x1, starting transfers between devices: 8.52 us -> 4.82 us  [shards(): lax.all_to_all(routed, 'shot', split_axis=1, concat_axis=2, tiled=True)]
  transfers between devices with their start and end apart: 3 -> 3, of which waited for: 2 -> 3; matrix products, arithmetic and copies ran while one was open for 4% -> 3% of each run, Pallas kernels for 0% -> 0%
where the time goes in v3:
time: 338 us; the launch traced here: 335 us
  Pallas kernels  165 us (49%)
  waiting for transfers between devices  97.4 us (29%)
  other arithmetic  25.8 us (8%)
  local copies, waits for them, and re-layouts  24.1 us (7%)
  starting transfers between devices  22.4 us (7%)
    pallas_call x1, Pallas kernels, run_patches(): pl.pallas_call(pocs_kernel, grid_spec=grid_spec, out_shape=jax.ShapeDtype...  165 us
    all_to_all x1, waiting for transfers between devices, shards(): lax.all_to_all(result, 'shot', split_axis=0, concat_axis=1, tiled=True)[0]  49.6 us
    all_to_all x1, waiting for transfers between devices, shards(): lax.all_to_all(routed, 'shot', split_axis=1, concat_axis=2, tiled=True)  41.1 us
    all_to_all x1, starting transfers between devices, shards(): lax.all_to_all(packed, 'shot', split_axis=2, concat_axis=1, tiled=True)  9.42 us
    all_to_all x1, starting transfers between devices, shards(): lax.all_to_all(result, 'shot', split_axis=0, concat_axis=1, tiled=True)[0]  8.12 us
    select_n x1, other arithmetic, shards(): jnp.where(local_mask[None, :, :, None] > 0, spectra, jnp.nan)  7.64 us
  transfers between devices with their start and end apart: 3, of which 3 were waited for; matrix products, arithmetic and copies ran while one was open for 3% of the time, Pallas kernels for 0%

profile of v3, /device:TPU:1, one launch (start us, length us, event | category | flops | bytes accessed | tf_op | source)
XLA Modules:
  0.0 335.2 jit_solution(15396233219926869589)
XLA Ops:
  0.7 0.8 compare_convert_fusion
  2.3 9.4 %all-to-all-start = ((bf16[1,4,32,136]{3,1,0,2:T(4,128)(2,1)}), bf16[1,4,32,136]{3,1,0,2:T(4,128)(2,1)S(1)}, u32[]{:S(2)}, u32[]{:S(2)}) async-start(bf16[1,4,32,136]{3,1,0,2:T(4,128)(2,1)} %copy.18), calls=%async_computation | async-start | bytes 131072 | tf_op jit(solution)/shard_map/all_to_all | solution.py:172
  12.4 6.7 %all-to-all-done = bf16[1,4,32,136]{3,1,0,2:T(4,128)(2,1)S(1)} async-done(((bf16[1,4,32,136]{3,1,0,2:T(4,128)(2,1)}), bf16[1,4,32,136]{3,1,0,2:T(4,128)(2,1)S(1)}, u32[]{:S(2)}, u32[]{:S(2)}) %all-to-all-start) | async-done | bytes 34848 | tf_op jit(solution)/shard_map/all_to_all | solution.py:172
  19.3 2.5 sort.17
  21.8 1.2 gather_fusion
  23.1 7.6 %fusion.1 = bf16[128,128,128]{2,1,0:T(8,128)(2,1)} fusion(bf16[1,128,128,128]{3,2,1,0:T(8,128)(2,1)} %param.4, pred[128,128]{1,0:T(8,128)(4,1)S(1)} %slice_compare_fusion), kind=kLoop, calls=%fused_computation.9 | loop fusion | flops 2097152 | bytes 8404992 | tf_op jit(solution)/shard_map/jit(_where)/select_n | solution.py:182
  30.7 5.2 %gather_fusion.2 = bf16[128,128,128]{2,1,0:T(8,128)(2,1)} fusion(bf16[128,128,128]{2,1,0:T(8,128)(2,1)} %fusion.1, s32[1024]{0:T(1024)S(1)} %pad_clamp_fusion.1), kind=kCustom, calls=%fused_computation.2 | custom fusion | bytes 8389120 | tf_op jit(solution)/shard_map/jit(_take)/gather | solution.py:183
  35.9 4.6 %bitcast_select_fusion = bf16[1,128,128,128]{3,2,0,1:T(8,128)(2,1)} fusion(bf16[128,128,128]{2,1,0:T(8,128)(2,1)} %gather_fusion.2, pred[128]{0:T(512)(128)(4,1)S(1)} %compare_and_fusion), kind=kLoop, calls=%fused_computation.5 | loop fusion | flops 2097152 | bytes 8388736 | tf_op jit(solution)/shard_map/jit(_take)/select_n | solution.py:183
  40.5 4.8 %all-to-all-start.1 = ((bf16[1,128,128,128]{3,2,0,1:T(8,128)(2,1)}), bf16[1,128,128,128]{3,2,0,1:T(8,128)(2,1)}, u32[]{:S(2)}, u32[]{:S(2)}) async-start(bf16[1,128,128,128]{3,2,0,1:T(8,128)(2,1)} %bitcast_select_fusion), calls=%async_computation.1 | async-start | bytes 8388608 | tf_op jit(solution)/shard_map/all_to_all | solution.py:184
  46.1 1.0 convert_element_type.194
  47.1 1.0 convert_element_type.198
  48.2 1.0 convert_element_type.201
  49.9 1.0 convert_element_type.187
  50.9 1.0 convert_element_type.189
  52.6 1.1 pad_maximum_fusion.tab_ref
  55.0 41.1 %all-to-all-done.1 = bf16[1,128,128,128]{3,2,0,1:T(8,128)(2,1)} async-done(((bf16[1,128,128,128]{3,2,0,1:T(8,128)(2,1)}), bf16[1,128,128,128]{3,2,0,1:T(8,128)(2,1)}, u32[]{:S(2)}, u32[]{:S(2)}) %all-to-all-start.1) | async-done | bytes 4194336 | tf_op jit(solution)/shard_map/all_to_all | solution.py:184
  96.1 4.7 %copy.21 = bf16[1,32,4,128,128]{4,3,1,2,0:T(8,128)(2,1)} copy(bf16[1,32,4,128,128]{4,3,2,1,0:T(8,128)(2,1)} %bitcast.10) | data formatting | bytes 8388608 | tf_op jit(solution)/shard_map/all_to_all | solution.py:184
  100.8 165.2 %shard_map.46 = bf16[32,4,2,64,128]{4,3,2,1,0:T(8,128)(2,1)} custom-call(s32[4]{0:T(128)} %and_select_fusion.counts_ref, f32[8]{0:T(128)} %power_multiply_fusion.scales_ref, bf16[4,16,256,128]{3,2,1,0:T(8,128)(2,1)} %bitcast.62, bf16[4,256,512]{2,1,0:T(8,128)(2,1)} %pad_maximum_fusion.tab_ref), custom_call_target="tpu_custom_call" | custom-call | tf_op jit(solution)/shard_map/pallas_call | solution.py:143
  266.0 8.1 %all-to-all-start.2 = ((bf16[32,4,2,64,128]{4,3,2,1,0:T(8,128)(2,1)}), bf16[32,4,2,64,128]{4,3,2,1,0:T(8,128)(2,1)}, u32[]{:S(2)}, u32[]{:S(2)}) async-start(bf16[32,4,2,64,128]{4,3,2,1,0:T(8,128)(2,1)} %shard_map.46), calls=%async_computation.2 | async-start | bytes 8388608 | tf_op jit(solution)/shard_map/all_to_all | solution.py:192
  274.2 1.0 scatter_custom_fusion
  275.2 49.6 %all-to-all-done.2 = bf16[32,4,2,64,128]{4,3,2,1,0:T(8,128)(2,1)} async-done(((bf16[32,4,2,64,128]{4,3,2,1,0:T(8,128)(2,1)}), bf16[32,4,2,64,128]{4,3,2,1,0:T(8,128)(2,1)}, u32[]{:S(2)}, u32[]{:S(2)}) %all-to-all-start.2) | async-done | bytes 4194336 | tf_op jit(solution)/shard_map/all_to_all | solution.py:192
  324.8 5.2 %gather_fusion.3 = bf16[128,2,64,128]{3,2,1,0:T(8,128)(2,1)} fusion(bf16[128,2,64,128]{3,2,1,0:T(8,128)(2,1)} %bitcast.17, s32[1024]{0:T(1024)S(1)} %pad_clamp_fusion), kind=kCustom, calls=%fused_computation.3 | custom fusion | bytes 8389120 | tf_op jit(solution)/shard_map/jit(_take)/gather | solution.py:193
  330.0 2.6 broadcast_select_fusion
  332.9 2.3 fusion.2
  (33 shorter events, 5.8 us)
Async XLA Ops:
  2.3 16.7 %all-to-all-start = ((bf16[1,4,32,136]{3,1,0,2:T(4,128)(2,1)}), bf16[1,4,32,136]{3,1,0,2:T(4,128)(2,1)S(1)}, u32[]{:S(2)}, u32[]{:S(2)}) async-start(bf16[1,4,32,136]{3,1,0,2:T(4,128)(2,1)} %copy.18), calls=%async_computation | async-start | bytes 131072 | tf_op jit(solution)/shard_map/all_to_all | solution.py:172
  40.5 55.5 %all-to-all-start.1 = ((bf16[1,128,128,128]{3,2,0,1:T(8,128)(2,1)}), bf16[1,128,128,128]{3,2,0,1:T(8,128)(2,1)}, u32[]{:S(2)}, u32[]{:S(2)}) async-start(bf16[1,128,128,128]{3,2,0,1:T(8,128)(2,1)} %bitcast_select_fusion), calls=%async_computation.1 | async-start | bytes 8388608 | tf_op jit(solution)/shard_map/all_to_all | solution.py:184
  266.0 58.8 %all-to-all-start.2 = ((bf16[32,4,2,64,128]{4,3,2,1,0:T(8,128)(2,1)}), bf16[32,4,2,64,128]{4,3,2,1,0:T(8,128)(2,1)}, u32[]{:S(2)}, u32[]{:S(2)}) async-start(bf16[32,4,2,64,128]{4,3,2,1,0:T(8,128)(2,1)} %shard_map.46), calls=%async_computation.2 | async-start | bytes 8388608 | tf_op jit(solution)/shard_map/all_to_all | solution.py:192

commit v4 on v3

--- a/solution.py
+++ b/solution.py
@@ -180,16 +180,20 @@
     mine = lax.dynamic_slice(perm, (me * owned_count,), (owned_count,))
 
     marked = jnp.where(local_mask[None, :, :, None] > 0, spectra, jnp.nan).astype(spectra.dtype)
-    routed = jnp.take(marked, perm, axis=1)
-    regrouped = lax.all_to_all(routed, "shot", split_axis=1, concat_axis=2, tiled=True)
-    observed = regrouped.reshape(owned_count, extent, plane, lane_count)
-    sweeps = jnp.take(all_counts, mine)
     tables = kernel_tables(extent)
     steps = jnp.arange(8, dtype=jnp.float32)
     scales = 0.5 * jnp.power(jnp.float32(0.6), steps)
-
-    result = run_patches(observed, sweeps, scales, tables)
-    back = lax.all_to_all(result, "shot", split_axis=0, concat_axis=1, tiled=True)[0]
+    slots = perm.reshape(devices, owned_count)
+    sweeps = jnp.take(all_counts, mine)
+
+    returned = []
+    for slot in range(owned_count):
+        routed = jnp.take(marked, slots[:, slot], axis=1)
+        regrouped = lax.all_to_all(routed, "shot", split_axis=1, concat_axis=2, tiled=True)
+        observed = regrouped.reshape(1, extent, plane, lane_count)
+        result = run_patches(observed, sweeps[slot:slot + 1], scales, tables)
+        returned.append(lax.all_to_all(result, "shot", split_axis=0, concat_axis=1, tiled=True)[0])
+    back = jnp.stack(returned, axis=1).reshape((total,) + returned[0].shape[1:])
     back = jnp.take(back, inverse, axis=0)
     own_half = back[:, 0].astype(jnp.float32)
     top_half = back[:, 1].astype(jnp.float32)

time: 338 us -> 385 us (1.14)
  the two profiles are of different devices: /device:TPU:1 before, /device:TPU:17 now
where the time goes in v4:
time: 385 us; the launch traced here: 379 us
  Pallas kernels  177 us (46%)
  starting transfers between devices  90.9 us (24%)
  waiting for transfers between devices  54.4 us (14%)
  other arithmetic  28.6 us (7%)
  local copies, waits for them, and re-layouts  27.8 us (7%)
    pallas_call x4, Pallas kernels, run_patches(): pl.pallas_call(pocs_kernel, grid_spec=grid_spec, out_shape=jax.ShapeDtype...  177 us
    all_to_all x4, starting transfers between devices, shards(): lax.all_to_all(result, 'shot', split_axis=0, concat_axis=1, tiled=True)[0]  65.4 us
    all_to_all x4, waiting for transfers between devices, shards(): lax.all_to_all(routed, 'shot', split_axis=1, concat_axis=2, tiled=True)  31.9 us
    all_to_all x4, starting transfers between devices, shards(): lax.all_to_all(routed, 'shot', split_axis=1, concat_axis=2, tiled=True)  16.9 us
    all_to_all x4, waiting for transfers between devices, shards(): lax.all_to_all(result, 'shot', split_axis=0, concat_axis=1, tiled=True)[0]  15.8 us
    gather x4, local copies, waits for them, and re-layouts, shards(): routed = jnp.take(marked, slots[:, slot], axis=1)  11.7 us
    all_to_all x1, starting transfers between devices, shards(): lax.all_to_all(packed, 'shot', split_axis=2, concat_axis=1, tiled=True)  8.6 us
  transfers between devices with their start and end apart: 9, of which 5 were waited for; matrix products, arithmetic and copies ran while one was open for 6% of the time, Pallas kernels for 47%

profile of v4, /device:TPU:17, one launch (start us, length us, event | category | flops | bytes accessed | tf_op | source)
XLA Modules:
  0.0 379.4 jit_solution(16850483344041839937)
XLA Ops:
  2.3 8.6 %all-to-all-start = ((bf16[1,4,32,136]{3,1,0,2:T(4,128)(2,1)}), bf16[1,4,32,136]{3,1,0,2:T(4,128)(2,1)S(1)}, u32[]{:S(2)}, u32[]{:S(2)}) async-start(bf16[1,4,32,136]{3,1,0,2:T(4,128)(2,1)} %copy.12), calls=%async_computation | async-start | bytes 131072 | tf_op jit(solution)/shard_map/all_to_all | solution.py:172
  11.6 6.6 %all-to-all-done = bf16[1,4,32,136]{3,1,0,2:T(4,128)(2,1)S(1)} async-done(((bf16[1,4,32,136]{3,1,0,2:T(4,128)(2,1)}), bf16[1,4,32,136]{3,1,0,2:T(4,128)(2,1)S(1)}, u32[]{:S(2)}, u32[]{:S(2)}) %all-to-all-start) | async-done | bytes 34848 | tf_op jit(solution)/shard_map/all_to_all | solution.py:172
  22.6 7.6 %select_bitcast_fusion = bf16[128,128,128]{2,1,0:T(8,128)(2,1)} fusion(bf16[1,128,128,128]{3,2,1,0:T(8,128)(2,1)} %param.6, pred[128,128]{1,0:T(8,128)(4,1)S(1)} %slice_compare_fusion), kind=kLoop, calls=%fused_computation.11 | loop fusion | flops 2097152 | bytes 8404992 | tf_op jit(solution)/shard_map/jit(_take)/Arg_0.17 | solution.py:191
  34.3 4.0 %all-to-all-start.1 = ((bf16[1,32,128,128]{3,2,0,1:T(8,128)(2,1)}), bf16[1,32,128,128]{3,2,0,1:T(8,128)(2,1)S(1)}, u32[]{:S(2)}, u32[]{:S(2)}) async-start(bf16[1,32,128,128]{3,2,0,1:T(8,128)(2,1)} %bitcast_select_fusion.3), calls=%async_computation.1 | async-start | bytes 2097152 | tf_op jit(solution)/shard_map/all_to_all | solution.py:192
  38.4 2.9 gather_fusion.4
  42.5 12.9 %all-to-all-done.1 = bf16[1,32,128,128]{3,2,0,1:T(8,128)(2,1)S(1)} async-done(((bf16[1,32,128,128]{3,2,0,1:T(8,128)(2,1)}), bf16[1,32,128,128]{3,2,0,1:T(8,128)(2,1)S(1)}, u32[]{:S(2)}, u32[]{:S(2)}) %all-to-all-start.1) | async-done | bytes 1048608 | tf_op jit(solution)/shard_map/all_to_all | solution.py:192
  55.4 4.6 %all-to-all-start.3 = ((bf16[1,32,128,128]{3,2,0,1:T(8,128)(2,1)}), bf16[1,32,128,128]{3,2,0,1:T(8,128)(2,1)}, u32[]{:S(2)}, u32[]{:S(2)}) async-start(bf16[1,32,128,128]{3,2,0,1:T(8,128)(2,1)} %bitcast_select_fusion.2), calls=%async_computation.3 | async-start | bytes 2097152 | tf_op jit(solution)/shard_map/all_to_all | solution.py:192
  64.5 2.9 gather_fusion.5
  68.6 8.7 %all-to-all-done.3 = bf16[1,32,128,128]{3,2,0,1:T(8,128)(2,1)} async-done(((bf16[1,32,128,128]{3,2,0,1:T(8,128)(2,1)}), bf16[1,32,128,128]{3,2,0,1:T(8,128)(2,1)}, u32[]{:S(2)}, u32[]{:S(2)}) %all-to-all-start.3) | async-done | bytes 1048608 | tf_op jit(solution)/shard_map/all_to_all | solution.py:192
  77.3 4.0 %all-to-all-start.5 = ((bf16[1,32,128,128]{3,2,0,1:T(8,128)(2,1)}), bf16[1,32,128,128]{3,2,0,1:T(8,128)(2,1)S(1)}, u32[]{:S(2)}, u32[]{:S(2)}) async-start(bf16[1,32,128,128]{3,2,0,1:T(8,128)(2,1)} %bitcast_select_fusion.1), calls=%async_computation.5 | async-start | bytes 2097152 | tf_op jit(solution)/shard_map/all_to_all | solution.py:192
  84.0 2.9 gather_fusion.6
  88.1 10.3 %all-to-all-done.5 = bf16[1,32,128,128]{3,2,0,1:T(8,128)(2,1)S(1)} async-done(((bf16[1,32,128,128]{3,2,0,1:T(8,128)(2,1)}), bf16[1,32,128,128]{3,2,0,1:T(8,128)(2,1)S(1)}, u32[]{:S(2)}, u32[]{:S(2)}) %all-to-all-start.5) | async-done | bytes 1048608 | tf_op jit(solution)/shard_map/all_to_all | solution.py:192
  98.4 4.3 %all-to-all-start.7 = ((bf16[1,32,128,128]{3,2,0,1:T(8,128)(2,1)}), bf16[1,32,128,128]{3,2,0,1:T(8,128)(2,1)S(1)}, u32[]{:S(2)}, u32[]{:S(2)}) async-start(bf16[1,32,128,128]{3,2,0,1:T(8,128)(2,1)} %bitcast_select_fusion), calls=%async_computation.7 | async-start | bytes 2097152 | tf_op jit(solution)/shard_map/all_to_all | solution.py:192
  106.0 93.7 %shard_map.46 = bf16[32,1,2,64,128]{4,3,2,1,0:T(8,128)(2,1)} custom-call(s32[1]{0:T(128)} %get-tuple-element.21.counts_ref, f32[8]{0:T(128)} %power_multiply_fusion.scales_ref, bf16[1,16,256,128]{3,2,1,0:T(8,128)(2,1)} %bitcast.63, bf16[4,256,512]{2,1,0:T(8,128)(2,1)} %pad_maximum_fusion.1.tab_ref), custom_call_target="tpu_custom_call" | custom-call | tf_op jit(solution)/shard_map/pallas_call | solution.py:143
  199.7 15.7 %all-to-all-start.2 = ((bf16[32,1,2,64,128]{4,3,2,1,0:T(8,128)(2,1)}), bf16[32,1,2,64,128]{4,3,2,1,0:T(8,128)(2,1)S(1)}, u32[]{:S(2)}, u32[]{:S(2)}) async-start(bf16[32,1,2,64,128]{4,3,2,1,0:T(8,128)(2,1)} %shard_map.46), calls=%async_computation.2 | async-start | bytes 2097152 | tf_op jit(solution)/shard_map/all_to_all | solution.py:195
  215.5 32.8 %shard_map.47 = bf16[32,1,2,64,128]{4,3,2,1,0:T(8,128)(2,1)} custom-call(s32[1]{0:T(128)} %get-tuple-element.24.counts_ref, f32[8]{0:T(128)} %power_multiply_fusion.scales_ref, bf16[1,16,256,128]{3,2,1,0:T(8,128)(2,1)} %bitcast.14.obs_ref, bf16[4,256,512]{2,1,0:T(8,128)(2,1)} %pad_maximum_fusion.1.tab_ref), custom_call_target="tpu_custom_call" | custom-call | tf_op jit(solution)/shard_map/pallas_call | solution.py:143
  248.3 38.1 %all-to-all-start.4 = ((bf16[32,1,2,64,128]{4,3,2,1,0:T(8,128)(2,1)}), bf16[32,1,2,64,128]{4,3,2,1,0:T(8,128)(2,1)S(1)}, u32[]{:S(2)}, u32[]{:S(2)}) async-start(bf16[32,1,2,64,128]{4,3,2,1,0:T(8,128)(2,1)} %shard_map.47), calls=%async_computation.4 | async-start | bytes 2097152 | tf_op jit(solution)/shard_map/all_to_all | solution.py:195
  286.4 32.8 %shard_map.48 = bf16[32,1,2,64,128]{4,3,2,1,0:T(8,128)(2,1)} custom-call(s32[1]{0:T(128)} %get-tuple-element.23.counts_ref, f32[8]{0:T(128)} %power_multiply_fusion.scales_ref, bf16[1,16,256,128]{3,2,1,0:T(8,128)(2,1)} %bitcast.64, bf16[4,256,512]{2,1,0:T(8,128)(2,1)} %pad_maximum_fusion.1.tab_ref), custom_call_target="tpu_custom_call" | custom-call | tf_op jit(solution)/shard_map/pallas_call | solution.py:143
  319.2 4.0 %all-to-all-start.6 = ((bf16[32,1,2,64,128]{4,3,2,1,0:T(8,128)(2,1)}), bf16[32,1,2,64,128]{4,3,2,1,0:T(8,128)(2,1)S(1)}, u32[]{:S(2)}, u32[]{:S(2)}) async-start(bf16[32,1,2,64,128]{4,3,2,1,0:T(8,128)(2,1)} %shard_map.48), calls=%async_computation.6 | async-start | bytes 2097152 | tf_op jit(solution)/shard_map/all_to_all | solution.py:195
  323.2 17.7 %shard_map.49 = bf16[32,1,2,64,128]{4,3,2,1,0:T(8,128)(2,1)} custom-call(s32[1]{0:T(128)} %get-tuple-element.22.counts_ref, f32[8]{0:T(128)} %power_multiply_fusion.scales_ref, bf16[1,16,256,128]{3,2,1,0:T(8,128)(2,1)} %bitcast.65, bf16[4,256,512]{2,1,0:T(8,128)(2,1)} %pad_maximum_fusion.1.tab_ref), custom_call_target="tpu_custom_call" | custom-call | tf_op jit(solution)/shard_map/pallas_call | solution.py:143
  340.9 7.5 %all-to-all-start.8 = ((bf16[32,1,2,64,128]{4,3,2,1,0:T(8,128)(2,1)}), bf16[32,1,2,64,128]{4,3,2,1,0:T(8,128)(2,1)}, u32[]{:S(2)}, u32[]{:S(2)}) async-start(bf16[32,1,2,64,128]{4,3,2,1,0:T(8,128)(2,1)} %shard_map.49), calls=%async_computation.8 | async-start | bytes 2097152 | tf_op jit(solution)/shard_map/all_to_all | solution.py:195
  349.7 15.8 %all-to-all-done.8 = bf16[32,1,2,64,128]{4,3,2,1,0:T(8,128)(2,1)} async-done(((bf16[32,1,2,64,128]{4,3,2,1,0:T(8,128)(2,1)}), bf16[32,1,2,64,128]{4,3,2,1,0:T(8,128)(2,1)}, u32[]{:S(2)}, u32[]{:S(2)}) %all-to-all-start.8) | async-done | bytes 1048608 | tf_op jit(solution)/shard_map/all_to_all | solution.py:195
  365.5 3.2 pad_maximum_fusion
  368.7 5.2 %gather_fusion.2 = bf16[128,2,64,128]{3,2,1,0:T(8,128)(2,1)} fusion(bf16[128,2,64,128]{3,2,1,0:T(8,128)(2,1)} %bitcast.62, s32[1024]{0:T(1024)S(1)} %pad_clamp_fusion), kind=kCustom, calls=%fused_computation.6 | custom fusion | bytes 8389120 | tf_op jit(solution)/shard_map/jit(_take)/gather | solution.py:197
  (75 shorter events, 31.5 us)
Async XLA Ops:
  2.3 15.9 %all-to-all-start = ((bf16[1,4,32,136]{3,1,0,2:T(4,128)(2,1)}), bf16[1,4,32,136]{3,1,0,2:T(4,128)(2,1)S(1)}, u32[]{:S(2)}, u32[]{:S(2)}) async-start(bf16[1,4,32,136]{3,1,0,2:T(4,128)(2,1)} %copy.12), calls=%async_computation | async-start | bytes 131072 | tf_op jit(solution)/shard_map/all_to_all | solution.py:172
  34.3 21.1 %all-to-all-start.1 = ((bf16[1,32,128,128]{3,2,0,1:T(8,128)(2,1)}), bf16[1,32,128,128]{3,2,0,1:T(8,128)(2,1)S(1)}, u32[]{:S(2)}, u32[]{:S(2)}) async-start(bf16[1,32,128,128]{3,2,0,1:T(8,128)(2,1)} %bitcast_select_fusion.3), calls=%async_computation.1 | async-start | bytes 2097152 | tf_op jit(solution)/shard_map/all_to_all | solution.py:192
  55.4 4.6 %copy-start = (bf16[1,32,128,128]{3,2,0,1:T(8,128)(2,1)}, bf16[1,32,128,128]{3,2,0,1:T(8,128)(2,1)S(1)}, u32[]{:S(2)}) copy-start(bf16[1,32,128,128]{3,2,0,1:T(8,128)(2,1)S(1)} %all-to-all-done.1) | copy-start | bytes 3145732
  55.4 21.9 %all-to-all-start.3 = ((bf16[1,32,128,128]{3,2,0,1:T(8,128)(2,1)}), bf16[1,32,128,128]{3,2,0,1:T(8,128)(2,1)}, u32[]{:S(2)}, u32[]{:S(2)}) async-start(bf16[1,32,128,128]{3,2,0,1:T(8,128)(2,1)} %bitcast_select_fusion.2), calls=%async_computation.3 | async-start | bytes 2097152 | tf_op jit(solution)/shard_map/all_to_all | solution.py:192
  77.3 21.1 %all-to-all-start.5 = ((bf16[1,32,128,128]{3,2,0,1:T(8,128)(2,1)}), bf16[1,32,128,128]{3,2,0,1:T(8,128)(2,1)S(1)}, u32[]{:S(2)}, u32[]{:S(2)}) async-start(bf16[1,32,128,128]{3,2,0,1:T(8,128)(2,1)} %bitcast_select_fusion.1), calls=%async_computation.5 | async-start | bytes 2097152 | tf_op jit(solution)/shard_map/all_to_all | solution.py:192
  83.0 20.5 %copy-start.3 = (bf16[256,256]{1,0:T(8,128)(2,1)S(1)}, bf16[256,256]{1,0:T(8,128)(2,1)}, u32[]{:S(2)}) copy-start(bf16[256,256]{1,0:T(8,128)(2,1)} %convert_element_type.201) | copy-start | bytes 393220
  98.4 101.3 %copy-start.1 = (bf16[1,32,128,128]{3,2,0,1:T(8,128)(2,1)}, bf16[1,32,128,128]{3,2,0,1:T(8,128)(2,1)S(1)}, u32[]{:S(2)}) copy-start(bf16[1,32,128,128]{3,2,0,1:T(8,128)(2,1)S(1)} %all-to-all-done.5) | copy-start | bytes 3145732
  98.4 101.3 %all-to-all-start.7 = ((bf16[1,32,128,128]{3,2,0,1:T(8,128)(2,1)}), bf16[1,32,128,128]{3,2,0,1:T(8,128)(2,1)S(1)}, u32[]{:S(2)}, u32[]{:S(2)}) async-start(bf16[1,32,128,128]{3,2,0,1:T(8,128)(2,1)} %bitcast_select_fusion), calls=%async_computation.7 | async-start | bytes 2097152 | tf_op jit(solution)/shard_map/all_to_all | solution.py:192
  199.7 119.4 %copy-start.2 = (bf16[1,32,128,128]{3,2,0,1:T(8,128)(2,1)}, bf16[1,32,128,128]{3,2,0,1:T(8,128)(2,1)S(1)}, u32[]{:S(2)}) copy-start(bf16[1,32,128,128]{3,2,0,1:T(8,128)(2,1)S(1)} %all-to-all-done.7) | copy-start | bytes 3145732
  199.7 48.6 %all-to-all-start.2 = ((bf16[32,1,2,64,128]{4,3,2,1,0:T(8,128)(2,1)}), bf16[32,1,2,64,128]{4,3,2,1,0:T(8,128)(2,1)S(1)}, u32[]{:S(2)}, u32[]{:S(2)}) async-start(bf16[32,1,2,64,128]{4,3,2,1,0:T(8,128)(2,1)} %shard_map.46), calls=%async_computation.2 | async-start | bytes 2097152 | tf_op jit(solution)/shard_map/all_to_all | solution.py:195
  248.3 70.9 %all-to-all-start.4 = ((bf16[32,1,2,64,128]{4,3,2,1,0:T(8,128)(2,1)}), bf16[32,1,2,64,128]{4,3,2,1,0:T(8,128)(2,1)S(1)}, u32[]{:S(2)}, u32[]{:S(2)}) async-start(bf16[32,1,2,64,128]{4,3,2,1,0:T(8,128)(2,1)} %shard_map.47), calls=%async_computation.4 | async-start | bytes 2097152 | tf_op jit(solution)/shard_map/all_to_all | solution.py:195
  319.2 21.7 %all-to-all-start.6 = ((bf16[32,1,2,64,128]{4,3,2,1,0:T(8,128)(2,1)}), bf16[32,1,2,64,128]{4,3,2,1,0:T(8,128)(2,1)S(1)}, u32[]{:S(2)}, u32[]{:S(2)}) async-start(bf16[32,1,2,64,128]{4,3,2,1,0:T(8,128)(2,1)} %shard_map.48), calls=%async_computation.6 | async-start | bytes 2097152 | tf_op jit(solution)/shard_map/all_to_all | solution.py:195
  340.9 24.7 %all-to-all-start.8 = ((bf16[32,1,2,64,128]{4,3,2,1,0:T(8,128)(2,1)}), bf16[32,1,2,64,128]{4,3,2,1,0:T(8,128)(2,1)}, u32[]{:S(2)}, u32[]{:S(2)}) async-start(bf16[32,1,2,64,128]{4,3,2,1,0:T(8,128)(2,1)} %shard_map.49), calls=%async_computation.8 | async-start | bytes 2097152 | tf_op jit(solution)/shard_map/all_to_all | solution.py:195

commit v5 on v3

--- a/solution.py
+++ b/solution.py
@@ -44,6 +44,9 @@
     ])
 
 
+GROUP = 16
+
+
 def pocs_kernel(counts_ref, scales_ref, obs_ref, tab_ref, out_ref, y_ref, v_ref):
     p = pl.program_id(0)
     extent = obs_ref.shape[1]
@@ -51,19 +54,35 @@
     half = lanes // 2
     plane = obs_ref.shape[2]
     half_axis = extent // 2
+    rows = plane // 4
+    group = GROUP
+    groups = extent // group
     sweeps = counts_ref[p]
     lower = lax.broadcasted_iota(jnp.int32, (1, lanes), 1) < half
 
-    def apply(table_idx, block):
+    def rot(block):
         rolled = pltpu.roll(block, half, 1)
-        rotated = jnp.where(lower, -rolled, rolled)
-        stacked = jnp.concatenate([block, rotated], axis=0)
-        return jnp.dot(tab_ref[table_idx], stacked, preferred_element_type=jnp.float32)
-
-    def stage_one(a, volume):
-        middle = apply(0, volume).astype(jnp.bfloat16)
+        return jnp.where(lower, -rolled, rolled)
+
+    def apply(table_idx, blocks):
+        stacked = jnp.concatenate([
+            jnp.concatenate(blocks, axis=1),
+            jnp.concatenate([rot(b) for b in blocks], axis=1),
+        ], axis=0)
+        wide = jnp.dot(tab_ref[table_idx], stacked, preferred_element_type=jnp.float32)
+        return [wide[:, g * lanes:(g + 1) * lanes] for g in range(len(blocks))]
+
+    def scatter_y(a, middle):
         for hi in range(extent):
             y_ref[hi, a] = middle[hi * extent:(hi + 1) * extent]
+
+    def stage_one(a0, blocks):
+        for g, m in enumerate(apply(0, blocks)):
+            scatter_y(a0 + g, m.astype(jnp.bfloat16))
+
+    def write_out(a, value):
+        for quarter in range(4):
+            out_ref[(a % half_axis) * 4 + quarter, 0, a // half_axis] = value[quarter * rows:(quarter + 1) * rows]
 
     def recorded(v):
         wide = v.astype(jnp.float32)
@@ -72,54 +91,65 @@
     def magnitude(c):
         return jnp.sqrt(c * c + pltpu.roll(c, half, 1) ** 2)
 
-    def init_a(a, carry):
-        observed = obs_ref[0, a]
-        sampled = recorded(observed)
-        initial = jnp.where(sampled, observed, jnp.zeros_like(observed))
-        for quarter in range(4):
-            rows = plane // 4
-            out_ref[(a % half_axis) * 4 + quarter, 0, a // half_axis] = initial[quarter * rows:(quarter + 1) * rows]
-        stage_one(a, initial)
+    def init_group(i, carry):
+        a0 = group * i
+        initial = []
+        for g in range(group):
+            observed = obs_ref[0, a0 + g]
+            value = jnp.where(recorded(observed), observed, jnp.zeros_like(observed))
+            write_out(a0 + g, value)
+            initial.append(value)
+        stage_one(a0, initial)
         return carry
 
-    lax.fori_loop(0, extent, init_a, 0, unroll=16)
-
-    def init_hi(hi, running):
-        coeffs = apply(2, y_ref[hi].reshape(plane, lanes))
-        return jnp.maximum(running, jnp.max(magnitude(coeffs), axis=0, keepdims=True))
-
-    largest = lax.fori_loop(0, extent, init_hi, jnp.zeros((1, lanes), jnp.float32), unroll=16)
+    lax.fori_loop(0, groups, init_group, 0, unroll=groups)
+
+    def coeff_group(i):
+        hi0 = group * i
+        return apply(2, [y_ref[hi0 + g].reshape(plane, lanes) for g in range(group)])
+
+    def init_hi(i, running):
+        for coeffs in coeff_group(i):
+            running = jnp.maximum(running, jnp.max(magnitude(coeffs), axis=0, keepdims=True))
+        return running
+
+    largest = lax.fori_loop(0, groups, init_hi, jnp.zeros((1, lanes), jnp.float32), unroll=groups)
 
     def sweep_step(k, carry):
         cutoff = largest * scales_ref[k]
 
-        def thin_hi(hi, c2):
-            coeffs = apply(2, y_ref[hi].reshape(plane, lanes))
-            size_now = magnitude(coeffs)
-            factor = jnp.maximum(size_now - cutoff, 0.0) / (jnp.maximum(size_now, cutoff) + 1e-06)
-            thinned = (coeffs * factor).astype(jnp.bfloat16)
-            back_mid = apply(3, thinned).astype(jnp.bfloat16)
-            for a in range(extent):
-                v_ref[a, hi] = back_mid[a * extent:(a + 1) * extent]
+        def thin_group(i, c2):
+            thinned = []
+            for coeffs in coeff_group(i):
+                size_now = magnitude(coeffs)
+                factor = jnp.maximum(size_now - cutoff, 0.0) / (jnp.maximum(size_now, cutoff) + 1e-06)
+                thinned.append((coeffs * factor).astype(jnp.bfloat16))
+            hi0 = group * i
+            for g, back_mid in enumerate(apply(3, thinned)):
+                back_mid = back_mid.astype(jnp.bfloat16)
+                for a in range(extent):
+                    v_ref[a, hi0 + g] = back_mid[a * extent:(a + 1) * extent]
             return c2
 
-        lax.fori_loop(0, extent, thin_hi, 0, unroll=16)
-
-        def back_a(a, c2):
-            returned = apply(1, v_ref[a].reshape(plane, lanes))
-            observed = obs_ref[0, a].astype(jnp.float32)
-            updated = jnp.where(observed == observed, observed, returned).astype(jnp.bfloat16)
-            for quarter in range(4):
-                rows = plane // 4
-                out_ref[(a % half_axis) * 4 + quarter, 0, a // half_axis] = updated[quarter * rows:(quarter + 1) * rows]
+        lax.fori_loop(0, groups, thin_group, 0, unroll=groups)
+
+        def back_group(i, c2):
+            a0 = group * i
+            returned = apply(1, [v_ref[a0 + g].reshape(plane, lanes) for g in range(group)])
+            updated = []
+            for g in range(group):
+                observed = obs_ref[0, a0 + g].astype(jnp.float32)
+                value = jnp.where(observed == observed, observed, returned[g]).astype(jnp.bfloat16)
+                write_out(a0 + g, value)
+                updated.append(value)
 
             @pl.when(k + 1 < sweeps)
             def _():
-                stage_one(a, updated)
+                stage_one(a0, updated)
 
             return c2
 
-        lax.fori_loop(0, extent, back_a, 0, unroll=16)
+        lax.fori_loop(0, groups, back_group, 0, unroll=groups)
         return carry
 
     lax.fori_loop(0, sweeps, sweep_step, 0)

time: 338 us -> 220 us (0.65)
  Pallas kernels: 165 us -> 47.3 us
    pallas_call x1, Pallas kernels: 165 us -> 47.3 us  [run_patches(): pl.pallas_call(pocs_kernel, grid_spec=grid_spec, out_shape=jax.ShapeDtype...]
  transfers between devices with their start and end apart: 3 -> 3, of which waited for: 3 -> 3; matrix products, arithmetic and copies ran while one was open for 3% -> 5% of each run, Pallas kernels for 0% -> 0%
where the time goes in v5:
time: 220 us; the launch traced here: 218 us
  waiting for transfers between devices  97.4 us (44%)
  Pallas kernels  47.3 us (22%)
  other arithmetic  25.8 us (12%)
  local copies, waits for them, and re-layouts  24.1 us (11%)
  starting transfers between devices  22.6 us (10%)
    all_to_all x1, waiting for transfers between devices, shards(): lax.all_to_all(result, 'shot', split_axis=0, concat_axis=1, tiled=True)[0]  49.6 us
    pallas_call x1, Pallas kernels, run_patches(): pl.pallas_call(pocs_kernel, grid_spec=grid_spec, out_shape=jax.ShapeDtype...  47.3 us
    all_to_all x1, waiting for transfers between devices, shards(): lax.all_to_all(routed, 'shot', split_axis=1, concat_axis=2, tiled=True)  41.1 us
    all_to_all x1, starting transfers between devices, shards(): lax.all_to_all(packed, 'shot', split_axis=2, concat_axis=1, tiled=True)  9.42 us
    all_to_all x1, starting transfers between devices, shards(): lax.all_to_all(result, 'shot', split_axis=0, concat_axis=1, tiled=True)[0]  8.34 us
    select_n x1, other arithmetic, shards(): jnp.where(local_mask[None, :, :, None] > 0, spectra, jnp.nan)  7.64 us
    all_to_all x1, waiting for transfers between devices, shards(): lax.all_to_all(packed, 'shot', split_axis=2, concat_axis=1, tiled=True)  6.66 us
    gather x1, local copies, waits for them, and re-layouts, shards(): routed = jnp.take(marked, perm, axis=1)  5.24 us
  transfers between devices with their start and end apart: 3, of which 3 were waited for; matrix products, arithmetic and copies ran while one was open for 5% of the time, Pallas kernels for 0%

profile of v5, /device:TPU:1, one launch (start us, length us, event | category | flops | bytes accessed | tf_op | source)
XLA Modules:
  0.0 217.5 jit_solution(5581398604659457482)
XLA Ops:
  0.7 0.8 compare_convert_fusion
  2.3 9.4 %all-to-all-start = ((bf16[1,4,32,136]{3,1,0,2:T(4,128)(2,1)}), bf16[1,4,32,136]{3,1,0,2:T(4,128)(2,1)S(1)}, u32[]{:S(2)}, u32[]{:S(2)}) async-start(bf16[1,4,32,136]{3,1,0,2:T(4,128)(2,1)} %copy.18), calls=%async_computation | async-start | bytes 131072 | tf_op jit(solution)/shard_map/all_to_all | solution.py:202
  12.4 6.7 %all-to-all-done = bf16[1,4,32,136]{3,1,0,2:T(4,128)(2,1)S(1)} async-done(((bf16[1,4,32,136]{3,1,0,2:T(4,128)(2,1)}), bf16[1,4,32,136]{3,1,0,2:T(4,128)(2,1)S(1)}, u32[]{:S(2)}, u32[]{:S(2)}) %all-to-all-start) | async-done | bytes 34848 | tf_op jit(solution)/shard_map/all_to_all | solution.py:202
  19.3 2.5 %sort.17 = (s32[128]{0:T(128)}, s32[128]{0:T(128)S(1)}) sort(s32[128]{0:T(128)S(1)} %neg.40, s32[128]{0:T(128)S(1)} %iota.104), dimensions={0}, to_apply=%region_0.0 | sort | flops 896 | bytes 2048 | tf_op jit(solution)/shard_map/jit(argsort)/sort | solution.py:207
  21.8 1.2 gather_fusion
  23.1 7.6 %fusion.1 = bf16[128,128,128]{2,1,0:T(8,128)(2,1)} fusion(bf16[1,128,128,128]{3,2,1,0:T(8,128)(2,1)} %param.4, pred[128,128]{1,0:T(8,128)(4,1)S(1)} %slice_compare_fusion), kind=kLoop, calls=%fused_computation.9 | loop fusion | flops 2097152 | bytes 8404992 | tf_op jit(solution)/shard_map/jit(_where)/select_n | solution.py:212
  30.7 5.2 %gather_fusion.2 = bf16[128,128,128]{2,1,0:T(8,128)(2,1)} fusion(bf16[128,128,128]{2,1,0:T(8,128)(2,1)} %fusion.1, s32[1024]{0:T(1024)S(1)} %pad_clamp_fusion.1), kind=kCustom, calls=%fused_computation.2 | custom fusion | bytes 8389120 | tf_op jit(solution)/shard_map/jit(_take)/gather | solution.py:213
  35.9 4.6 %bitcast_select_fusion = bf16[1,128,128,128]{3,2,0,1:T(8,128)(2,1)} fusion(bf16[128,128,128]{2,1,0:T(8,128)(2,1)} %gather_fusion.2, pred[128]{0:T(512)(128)(4,1)S(1)} %compare_and_fusion), kind=kLoop, calls=%fused_computation.5 | loop fusion | flops 2097152 | bytes 8388736 | tf_op jit(solution)/shard_map/jit(_take)/select_n | solution.py:213
  40.5 4.8 %all-to-all-start.1 = ((bf16[1,128,128,128]{3,2,0,1:T(8,128)(2,1)}), bf16[1,128,128,128]{3,2,0,1:T(8,128)(2,1)}, u32[]{:S(2)}, u32[]{:S(2)}) async-start(bf16[1,128,128,128]{3,2,0,1:T(8,128)(2,1)} %bitcast_select_fusion), calls=%async_computation.1 | async-start | bytes 8388608 | tf_op jit(solution)/shard_map/all_to_all | solution.py:214
  46.1 1.0 convert_element_type.194
  47.2 1.0 convert_element_type.198
  48.2 1.0 convert_element_type.201
  49.9 1.0 convert_element_type.187
  50.9 1.0 convert_element_type.189
  52.6 1.1 pad_maximum_fusion.tab_ref
  55.0 41.1 %all-to-all-done.1 = bf16[1,128,128,128]{3,2,0,1:T(8,128)(2,1)} async-done(((bf16[1,128,128,128]{3,2,0,1:T(8,128)(2,1)}), bf16[1,128,128,128]{3,2,0,1:T(8,128)(2,1)}, u32[]{:S(2)}, u32[]{:S(2)}) %all-to-all-start.1) | async-done | bytes 4194336 | tf_op jit(solution)/shard_map/all_to_all | solution.py:214
  96.1 4.7 %copy.21 = bf16[1,32,4,128,128]{4,3,1,2,0:T(8,128)(2,1)} copy(bf16[1,32,4,128,128]{4,3,2,1,0:T(8,128)(2,1)} %bitcast.10) | data formatting | bytes 8388608 | tf_op jit(solution)/shard_map/all_to_all | solution.py:214
  100.8 47.3 %shard_map.46 = bf16[32,4,2,64,128]{4,3,2,1,0:T(8,128)(2,1)} custom-call(s32[4]{0:T(128)} %and_select_fusion.counts_ref, f32[8]{0:T(128)} %power_multiply_fusion.scales_ref, bf16[4,16,256,128]{3,2,1,0:T(8,128)(2,1)} %bitcast.62, bf16[4,256,512]{2,1,0:T(8,128)(2,1)} %pad_maximum_fusion.tab_ref), custom_call_target="tpu_custom_call" | custom-call | tf_op jit(solution)/shard_map/pallas_call | solution.py:173
  148.1 8.3 %all-to-all-start.2 = ((bf16[32,4,2,64,128]{4,3,2,1,0:T(8,128)(2,1)}), bf16[32,4,2,64,128]{4,3,2,1,0:T(8,128)(2,1)}, u32[]{:S(2)}, u32[]{:S(2)}) async-start(bf16[32,4,2,64,128]{4,3,2,1,0:T(8,128)(2,1)} %shard_map.46), calls=%async_computation.2 | async-start | bytes 8388608 | tf_op jit(solution)/shard_map/all_to_all | solution.py:222
  156.5 1.0 scatter_custom_fusion
  157.5 49.6 %all-to-all-done.2 = bf16[32,4,2,64,128]{4,3,2,1,0:T(8,128)(2,1)} async-done(((bf16[32,4,2,64,128]{4,3,2,1,0:T(8,128)(2,1)}), bf16[32,4,2,64,128]{4,3,2,1,0:T(8,128)(2,1)}, u32[]{:S(2)}, u32[]{:S(2)}) %all-to-all-start.2) | async-done | bytes 4194336 | tf_op jit(solution)/shard_map/all_to_all | solution.py:222
  207.2 5.2 %gather_fusion.3 = bf16[128,2,64,128]{3,2,1,0:T(8,128)(2,1)} fusion(bf16[128,2,64,128]{3,2,1,0:T(8,128)(2,1)} %bitcast.17, s32[1024]{0:T(1024)S(1)} %pad_clamp_fusion), kind=kCustom, calls=%fused_computation.3 | custom fusion | bytes 8389120 | tf_op jit(solution)/shard_map/jit(_take)/gather | solution.py:223
  212.4 2.6 %broadcast_select_fusion = bf16[128,2,64,128]{3,2,1,0:T(8,128)(2,1)S(1)} fusion(bf16[128,2,64,128]{3,2,1,0:T(8,128)(2,1)} %gather_fusion.3, pred[128]{0:T(512)(128)(4,1)S(1)} %compare_and_fusion.1), kind=kLoop, calls=%fused_computation.10 | loop fusion | flops 2097152 | bytes 8388736 | tf_op jit(solution)/shard_map/jit(_take)/select_n | solution.py:223
  215.2 2.3 %fusion.2 = bf16[1,128,64,128]{3,2,1,0:T(8,128)(2,1)} fusion(bf16[128,2,64,128]{3,2,1,0:T(8,128)(2,1)S(1)} %broadcast_select_fusion, bf16[127,64,128]{2,1,0:T(8,128)(2,1)S(1)} %slice_bitcast_fusion.1, f32[]{:T(128)S(6)} %sub.15, f32[]{:T(128)S(6)} %div.14), kind=kLoop, calls=%fused_computation.11 | loop fusion | flops 6291456 | bytes 6275080 | tf_op jit(solution)/shard_map/broadcast_in_dim | solution.py:230
  (33 shorter events, 5.8 us)
Async XLA Ops:
  2.3 16.7 %all-to-all-start = ((bf16[1,4,32,136]{3,1,0,2:T(4,128)(2,1)}), bf16[1,4,32,136]{3,1,0,2:T(4,128)(2,1)S(1)}, u32[]{:S(2)}, u32[]{:S(2)}) async-start(bf16[1,4,32,136]{3,1,0,2:T(4,128)(2,1)} %copy.18), calls=%async_computation | async-start | bytes 131072 | tf_op jit(solution)/shard_map/all_to_all | solution.py:202
  40.5 55.5 %all-to-all-start.1 = ((bf16[1,128,128,128]{3,2,0,1:T(8,128)(2,1)}), bf16[1,128,128,128]{3,2,0,1:T(8,128)(2,1)}, u32[]{:S(2)}, u32[]{:S(2)}) async-start(bf16[1,128,128,128]{3,2,0,1:T(8,128)(2,1)} %bitcast_select_fusion), calls=%async_computation.1 | async-start | bytes 8388608 | tf_op jit(solution)/shard_map/all_to_all | solution.py:214
  148.1 59.0 %all-to-all-start.2 = ((bf16[32,4,2,64,128]{4,3,2,1,0:T(8,128)(2,1)}), bf16[32,4,2,64,128]{4,3,2,1,0:T(8,128)(2,1)}, u32[]{:S(2)}, u32[]{:S(2)}) async-start(bf16[32,4,2,64,128]{4,3,2,1,0:T(8,128)(2,1)} %shard_map.46), calls=%async_computation.2 | async-start | bytes 8388608 | tf_op jit(solution)/shard_map/all_to_all | solution.py:222

commit v6 on v5

--- a/solution.py
+++ b/solution.py
@@ -178,56 +178,29 @@
     )(sweeps, scales, observed, tables)
 
 
-def snake_slots(devices, per_device):
-    ranks = []
-    for d in range(devices):
-        for i in range(per_device):
-            ranks.append(i * devices + (d if i % 2 == 0 else devices - 1 - d))
-    return jnp.array(ranks, jnp.int32)
-
-
 def shards(spectra, sampled_mask, counts):
-    devices = lax.axis_size("shot")
-    me = lax.axis_index("shot")
-    owned_count = counts.shape[1]
-    total = devices * owned_count
     extent = sampled_mask.shape[2]
     plane = extent * extent
     lane_count = spectra.shape[3]
     halfway = extent // 2
-
-    mask_rows = (sampled_mask[0] > 0).astype(jnp.bfloat16).reshape(owned_count, devices, -1)
-    count_cols = jnp.broadcast_to(counts[0].astype(jnp.bfloat16)[:, None, None], (owned_count, devices, 8))
-    packed = jnp.concatenate([mask_rows, count_cols], axis=2)[None]
-    arrived = lax.all_to_all(packed, "shot", split_axis=2, concat_axis=1, tiled=True)[0, :, 0]
-    local_traces = spectra.shape[2]
-    local_mask = arrived[:, :local_traces]
-    all_counts = arrived[:, local_traces].astype(jnp.int32)
-
-    order = jnp.argsort(-all_counts, stable=True).astype(jnp.int32)
-    perm = order[snake_slots(devices, owned_count)]
-    inverse = jnp.zeros((total,), jnp.int32).at[perm].set(jnp.arange(total, dtype=jnp.int32))
-    mine = lax.dynamic_slice(perm, (me * owned_count,), (owned_count,))
-
-    marked = jnp.where(local_mask[None, :, :, None] > 0, spectra, jnp.nan).astype(spectra.dtype)
-    routed = jnp.take(marked, perm, axis=1)
-    regrouped = lax.all_to_all(routed, "shot", split_axis=1, concat_axis=2, tiled=True)
+    regrouped = lax.all_to_all(spectra, "shot", split_axis=1, concat_axis=2, tiled=True)
+    owned_count = regrouped.shape[1]
     observed = regrouped.reshape(owned_count, extent, plane, lane_count)
-    sweeps = jnp.take(all_counts, mine)
+    marked = jnp.where(sampled_mask[0][..., None] > 0, observed, jnp.nan).astype(observed.dtype)
     tables = kernel_tables(extent)
     steps = jnp.arange(8, dtype=jnp.float32)
     scales = 0.5 * jnp.power(jnp.float32(0.6), steps)
 
-    result = run_patches(observed, sweeps, scales, tables)
-    back = lax.all_to_all(result, "shot", split_axis=0, concat_axis=1, tiled=True)[0]
-    back = jnp.take(back, inverse, axis=0)
-    own_half = back[:, 0].astype(jnp.float32)
-    top_half = back[:, 1].astype(jnp.float32)
-    earlier = jnp.concatenate([jnp.zeros_like(top_half[:1]), top_half[:-1]], axis=0)
-    h = (me // (devices // halfway)).astype(jnp.float32)
-    weight = (h + 0.5) / halfway
-    mixed = weight * own_half + (1.0 - weight) * earlier
-    return mixed.astype(jnp.bfloat16)[None]
+    result = run_patches(marked, counts[0], scales, tables)
+    dests = result.shape[0]
+    top = result[:, :, 1]
+    arrived = passed_along(top[:, -1], "shot", 1)
+    earlier = jnp.concatenate([arrived[:, None], top[:, :-1]], axis=1).astype(jnp.float32)
+    h = (jnp.arange(dests, dtype=jnp.int32) // (dests // halfway)).astype(jnp.float32)
+    weight = ((h + 0.5) / halfway)[:, None, None, None]
+    mixed = weight * result[:, :, 0].astype(jnp.float32) + (1.0 - weight) * earlier
+    mixed = mixed.astype(jnp.bfloat16)
+    return lax.all_to_all(mixed, "shot", split_axis=0, concat_axis=1, tiled=True)
 
 
 def solution(mesh):

time: 220 us -> 204 us (0.927); the launches traced: 218 us -> 204 us
  blocking collectives: 0 us -> 31.2 us
  waiting for transfers between devices: 97.4 us -> 80.3 us
  other arithmetic: 25.8 us -> 9.37 us
  local copies, waits for them, and re-layouts: 24.1 us -> 10.7 us
  starting transfers between devices: 22.6 us -> 35.6 us
  Pallas kernels: 47.3 us -> 36.7 us
    all_to_all x3 -> x1, waiting for transfers between devices: 97.4 us -> 42.5 us  [shards(): lax.all_to_all(spectra, 'shot', split_axis=1, concat_axis=2, tiled=True)]
    ppermute x0 -> x1, waiting for transfers between devices: none -> 37.8 us  [passed_along(): return lax.ppermute(block, axis, route)]
    all_to_all x0 -> x1, blocking collectives: none -> 31.2 us  [shards(): lax.all_to_all(mixed, 'shot', split_axis=0, concat_axis=1, tiled=True)]
    ppermute x0 -> x1, starting transfers between devices: none -> 26.1 us  [passed_along(): return lax.ppermute(block, axis, route)]
    all_to_all x3 -> x1, starting transfers between devices: 22.6 us -> 9.47 us  [shards(): lax.all_to_all(spectra, 'shot', split_axis=1, concat_axis=2, tiled=True)]
    gather x4 -> x0, local copies, waits for them, and re-layouts: 12.3 us -> none  [the longest x1 5.24 us: shards(): routed = jnp.take(marked, perm, axis=1)]
    pallas_call x1, Pallas kernels: 47.3 us -> 36.7 us  [run_patches(): pl.pallas_call(pocs_kernel, grid_spec=grid_spec, out_shape=jax.ShapeDtype...]
    select_n x7 -> x1, other arithmetic: 15.5 us -> 4.94 us  [shards(): jnp.where(sampled_mask[0][..., None] > 0, observed, jnp.nan)]
  transfers between devices with their start and end apart: 3 -> 2, of which waited for: 3 -> 2; matrix products, arithmetic and copies ran while one was open for 5% -> 4% of each run, Pallas kernels for 0% -> 0%
where the time goes in v6:
time: 204 us
  waiting for transfers between devices  80.3 us (39%)
  Pallas kernels  36.7 us (18%)
  starting transfers between devices  35.6 us (17%)
  blocking collectives  31.2 us (15%)
  local copies, waits for them, and re-layouts  10.7 us (5%)
  other arithmetic  9.37 us (5%)
    all_to_all x1, waiting for transfers between devices, shards(): lax.all_to_all(spectra, 'shot', split_axis=1, concat_axis=2, tiled=True)  42.5 us
    ppermute x1, waiting for transfers between devices, passed_along(): return lax.ppermute(block, axis, route)  37.8 us
    pallas_call x1, Pallas kernels, run_patches(): pl.pallas_call(pocs_kernel, grid_spec=grid_spec, out_shape=jax.ShapeDtype...  36.7 us
    all_to_all x1, blocking collectives, shards(): lax.all_to_all(mixed, 'shot', split_axis=0, concat_axis=1, tiled=True)  31.2 us
    ppermute x1, starting transfers between devices, passed_along(): return lax.ppermute(block, axis, route)  26.1 us
    all_to_all x1, starting transfers between devices, shards(): lax.all_to_all(spectra, 'shot', split_axis=1, concat_axis=2, tiled=True)  9.47 us
    select_n x1, other arithmetic, shards(): jnp.where(sampled_mask[0][..., None] > 0, observed, jnp.nan)  4.94 us
  transfers between devices with their start and end apart: 2, of which 2 were waited for; matrix products, arithmetic and copies ran while one was open for 4% of the time, Pallas kernels for 0%

profile of v6, /device:TPU:1, one launch (start us, length us, event | category | flops | bytes accessed | tf_op | source)
XLA Modules:
  0.0 204.1 jit_solution(4254781670402700727)
XLA Ops:
  0.0 9.5 %all-to-all-start = ((bf16[1,128,128,128]{3,2,0,1:T(8,128)(2,1)}), bf16[1,128,128,128]{3,2,0,1:T(8,128)(2,1)}, u32[]{:S(2)}, u32[]{:S(2)}) async-start(bf16[1,128,128,128]{3,2,0,1:T(8,128)(2,1)} %bitcast.43), calls=%async_computation | async-start | bytes 8388608 | tf_op jit(solution)/shard_map/all_to_all | solution.py:186
  9.5 0.1 negate_convert_fusion
  9.6 0.1 convert_convert_fusion
  9.6 0.6 multiply_convert_fusion.1
  10.2 1.0 convert_element_type.177
  11.2 1.0 convert_element_type.181
  12.2 1.0 convert_element_type.184
  13.2 0.1 negate_multiply_fusion
  13.3 0.6 add_convert_fusion
  13.9 1.0 convert_element_type.170
  14.9 1.0 convert_element_type.172
  15.9 0.5 power_multiply_fusion.scales_ref
  16.5 1.1 pad_maximum_fusion.tab_ref
  17.7 42.5 %all-to-all-done = bf16[1,128,128,128]{3,2,0,1:T(8,128)(2,1)} async-done(((bf16[1,128,128,128]{3,2,0,1:T(8,128)(2,1)}), bf16[1,128,128,128]{3,2,0,1:T(8,128)(2,1)}, u32[]{:S(2)}, u32[]{:S(2)}) %all-to-all-start) | async-done | bytes 4194336 | tf_op jit(solution)/shard_map/all_to_all | solution.py:186
  60.2 2.5 %copy.8 = bf16[1,32,4,128,128]{4,3,1,2,0:T(8,128)(2,1)S(1)} copy(bf16[1,32,4,128,128]{4,3,2,1,0:T(8,128)(2,1)} %bitcast.3) | data formatting | bytes 8388608 | tf_op jit(solution)/shard_map/all_to_all | solution.py:186
  62.7 4.9 %broadcast_select_fusion.obs_ref = bf16[4,16,256,128]{3,2,1,0:T(8,128)(2,1)} fusion(bf16[4,16,256,128]{3,2,1,0:T(8,128)(2,1)S(1)} %bitcast.41, pred[4,16,256]{2,1,0:T(8,128)(4,1)S(1)} %compare_bitcast_fusion), kind=kLoop, calls=%fused_computation.3 | loop fusion | flops 2097152 | bytes 8404992 | tf_op jit(solution)/shard_map/jit(_where)/select_n | solution.py:189
  67.6 36.7 %shard_map.37 = bf16[32,4,2,64,128]{4,3,2,1,0:T(8,128)(2,1)} custom-call(s32[4]{0:T(128)} %bitcast.45, f32[8]{0:T(128)} %power_multiply_fusion.scales_ref, bf16[4,16,256,128]{3,2,1,0:T(8,128)(2,1)} %broadcast_select_fusion.obs_ref, bf16[4,256,512]{2,1,0:T(8,128)(2,1)} %pad_maximum_fusion.tab_ref), custom_call_target="tpu_custom_call" | custom-call | tf_op jit(solution)/shard_map/pallas_call | solution.py:173
  104.3 1.8 slice_bitcast_fusion
  106.2 26.1 %collective-permute-start = (bf16[32,64,128]{2,1,0:T(8,128)(2,1)S(1)}, bf16[32,64,128]{2,1,0:T(8,128)(2,1)S(1)}, u32[]{:S(2)}, u32[]{:S(2)}) collective-permute-start(bf16[32,64,128]{2,1,0:T(8,128)(2,1)S(1)} %slice_bitcast_fusion.2), channel_id=1, source_target_pairs={{0,4},{4,8},{8,12},{12,16},{16,20},{20,24},{24,28},{28,32},{32,36}... | collective-permute-start | bytes 1572872 | tf_op jit(solution)/shard_map/ppermute | solution.py:12
  132.3 0.1 slice.19
  132.4 37.8 %collective-permute-done = bf16[32,64,128]{2,1,0:T(8,128)(2,1)S(1)} collective-permute-done((bf16[32,64,128]{2,1,0:T(8,128)(2,1)S(1)}, bf16[32,64,128]{2,1,0:T(8,128)(2,1)S(1)}, u32[]{:S(2)}, u32[]{:S(2)}) %collective-permute-start) | collective-permute-done | bytes 524320 | tf_op jit(solution)/shard_map/ppermute | solution.py:12
  170.3 1.3 fusion.1
  171.5 31.2 %all_to_all.27 = bf16[32,4,64,128]{3,2,1,0:T(8,128)(2,1)S(1)} all-to-all(bf16[32,4,64,128]{3,2,1,0:T(8,128)(2,1)S(1)} %fusion.1), channel_id=1, replica_groups=mesh['shot'=32,'az'=4] {'shot'}, dimensions={0} | all-to-all | bytes 4194304 | tf_op jit(solution)/shard_map/all_to_all | solution.py:203
  202.8 1.3 copy.14
  (11 shorter events, 0.2 us)
Async XLA Ops:
  0.0 60.2 %all-to-all-start = ((bf16[1,128,128,128]{3,2,0,1:T(8,128)(2,1)}), bf16[1,128,128,128]{3,2,0,1:T(8,128)(2,1)}, u32[]{:S(2)}, u32[]{:S(2)}) async-start(bf16[1,128,128,128]{3,2,0,1:T(8,128)(2,1)} %bitcast.43), calls=%async_computation | async-start | bytes 8388608 | tf_op jit(solution)/shard_map/all_to_all | solution.py:186
  15.9 1.8 copy-start.1
  106.1 64.1 %copy-start = (bf16[32,4,2,64,128]{4,3,2,1,0:T(8,128)(2,1)S(1)}, bf16[32,4,2,64,128]{4,3,2,1,0:T(8,128)(2,1)}, u32[]{:S(2)}) copy-start(bf16[32,4,2,64,128]{4,3,2,1,0:T(8,128)(2,1)} %shard_map.37) | copy-start | bytes 12582916
  106.2 64.1 %collective-permute-start = (bf16[32,64,128]{2,1,0:T(8,128)(2,1)S(1)}, bf16[32,64,128]{2,1,0:T(8,128)(2,1)S(1)}, u32[]{:S(2)}, u32[]{:S(2)}) collective-permute-start(bf16[32,64,128]{2,1,0:T(8,128)(2,1)S(1)} %slice_bitcast_fusion.2), channel_id=1, source_target_pairs={{0,4},{4,8},{8,12},{12,16},{16,20},{20,24},{24,28},{28,32},{32,36}... | collective-permute-start | bytes 1572872 | tf_op jit(solution)/shard_map/ppermute | solution.py:12

commit v7 on v6

--- a/solution.py
+++ b/solution.py
@@ -183,24 +183,34 @@
     plane = extent * extent
     lane_count = spectra.shape[3]
     halfway = extent // 2
-    regrouped = lax.all_to_all(spectra, "shot", split_axis=1, concat_axis=2, tiled=True)
-    owned_count = regrouped.shape[1]
-    observed = regrouped.reshape(owned_count, extent, plane, lane_count)
-    marked = jnp.where(sampled_mask[0][..., None] > 0, observed, jnp.nan).astype(observed.dtype)
+    owned_count = counts.shape[1]
     tables = kernel_tables(extent)
     steps = jnp.arange(8, dtype=jnp.float32)
     scales = 0.5 * jnp.power(jnp.float32(0.6), steps)
 
-    result = run_patches(marked, counts[0], scales, tables)
-    dests = result.shape[0]
-    top = result[:, :, 1]
-    arrived = passed_along(top[:, -1], "shot", 1)
-    earlier = jnp.concatenate([arrived[:, None], top[:, :-1]], axis=1).astype(jnp.float32)
+    results = []
+    for slot in range(owned_count):
+        regrouped = lax.all_to_all(spectra[:, slot::owned_count], "shot", split_axis=1, concat_axis=2, tiled=True)
+        observed = regrouped.reshape(1, extent, plane, lane_count)
+        marked = jnp.where(sampled_mask[0, slot][None, ..., None] > 0, observed, jnp.nan).astype(observed.dtype)
+        results.append(run_patches(marked, counts[0, slot:slot + 1], scales, tables)[:, 0])
+
+    dests = results[0].shape[0]
     h = (jnp.arange(dests, dtype=jnp.int32) // (dests // halfway)).astype(jnp.float32)
-    weight = ((h + 0.5) / halfway)[:, None, None, None]
-    mixed = weight * result[:, :, 0].astype(jnp.float32) + (1.0 - weight) * earlier
-    mixed = mixed.astype(jnp.bfloat16)
-    return lax.all_to_all(mixed, "shot", split_axis=0, concat_axis=1, tiled=True)
+    weight = ((h + 0.5) / halfway)[:, None, None]
+
+    def blended(slot, earlier):
+        mixed = weight * results[slot][:, 0].astype(jnp.float32) + (1.0 - weight) * earlier.astype(jnp.float32)
+        mixed = mixed.astype(jnp.bfloat16)[:, None]
+        return lax.all_to_all(mixed, "shot", split_axis=0, concat_axis=1, tiled=True)
+
+    returned = [None] * owned_count
+    for slot in range(1, owned_count):
+        returned[slot] = blended(slot, results[slot - 1][:, 1])
+    arrived = passed_along(results[-1][:, 1], "shot", 1)
+    returned[0] = blended(0, arrived)
+    stacked = jnp.stack(returned, axis=2)
+    return stacked.reshape(1, -1, plane // 4, lane_count)
 
 
 def solution(mesh):

time: 204 us -> 256 us (1.25)
  starting transfers between devices: 35.6 us -> 75.5 us
  waiting for transfers between devices: 80.3 us -> 45.8 us
  Pallas kernels: 36.7 us -> 60 us
  blocking collectives: 31.2 us -> 41.4 us
  other arithmetic: 9.37 us -> 16 us
  local copies, waits for them, and re-layouts: 10.7 us -> 14.8 us
    all_to_all x1 -> x6, starting transfers between devices: 9.47 us -> 72 us  [the longest x3 59.4 us: blended(): lax.all_to_all(mixed, 'shot', split_axis=0, concat_axis=1, tiled=True)]
    ppermute x1, waiting for transfers between devices: 37.8 us -> 0.01 us  [passed_along(): return lax.ppermute(block, axis, route)]
    pallas_call x1 -> x4, Pallas kernels: 36.7 us -> 60 us  [run_patches(): pl.pallas_call(pocs_kernel, grid_spec=grid_spec, out_shape=jax.ShapeDtype...]
    ppermute x1, starting transfers between devices: 26.1 us -> 3.55 us  [passed_along(): return lax.ppermute(block, axis, route)]
    all_to_all x1 -> x2, blocking collectives: 31.2 us -> 41.4 us  [the longest x1 26.4 us: shards(): lax.all_to_all(spectra[:, slot::owned_count], 'shot', split_axis=1, conca...]
    slice x1 -> x2, local copies, waits for them, and re-layouts: 0.12 us -> 4.69 us  [the longest x1 4.02 us: shards(): spectra[:, slot::owned_count]]
    all_to_all x1 -> x6, waiting for transfers between devices: 42.5 us -> 45.8 us  [the longest x3 26.6 us: shards(): lax.all_to_all(spectra[:, slot::owned_count], 'shot', split_axis=1, conca...]
    pallas_call x0 -> x2, local copies, waits for them, and re-layouts: none -> 2.6 us  [run_patches(): pl.pallas_call(pocs_kernel, grid_spec=grid_spec, out_shape=jax.ShapeDtype...]
  transfers between devices with their start and end apart: 2 -> 7, of which waited for: 2 -> 4; matrix products, arithmetic and copies ran while one was open for 4% -> 7% of each run, Pallas kernels for 0% -> 16%
where the time goes in v7:
time: 256 us; the launch traced here: 254 us
  starting transfers between devices  75.5 us (29%)
  Pallas kernels  60 us (23%)
  waiting for transfers between devices  45.8 us (18%)
  blocking collectives  41.4 us (16%)
  other arithmetic  16 us (6%)
  local copies, waits for them, and re-layouts  14.8 us (6%)
    pallas_call x4, Pallas kernels, run_patches(): pl.pallas_call(pocs_kernel, grid_spec=grid_spec, out_shape=jax.ShapeDtype...  60 us
    all_to_all x3, starting transfers between devices, blended(): lax.all_to_all(mixed, 'shot', split_axis=0, concat_axis=1, tiled=True)  59.4 us
    all_to_all x3, waiting for transfers between devices, shards(): lax.all_to_all(spectra[:, slot::owned_count], 'shot', split_axis=1, conca...  26.6 us
    all_to_all x1, blocking collectives, shards(): lax.all_to_all(spectra[:, slot::owned_count], 'shot', split_axis=1, conca...  26.4 us
    all_to_all x3, waiting for transfers between devices, blended(): lax.all_to_all(mixed, 'shot', split_axis=0, concat_axis=1, tiled=True)  19.2 us
    all_to_all x1, blocking collectives, blended(): lax.all_to_all(mixed, 'shot', split_axis=0, concat_axis=1, tiled=True)  15 us
    all_to_all x3, starting transfers between devices, shards(): lax.all_to_all(spectra[:, slot::owned_count], 'shot', split_axis=1, conca...  12.6 us
    select_n x2, other arithmetic, shards(): jnp.where(sampled_mask[0, slot][None, ..., None] > 0, observed, jnp.nan)  6.89 us
  transfers between devices with their start and end apart: 7, of which 4 were waited for; matrix products, arithmetic and copies ran while one was open for 7% of the time, Pallas kernels for 16%

profile of v7, /device:TPU:1, one launch (start us, length us, event | category | flops | bytes accessed | tf_op | source)
XLA Modules:
  0.0 253.8 jit_solution(4567547737109084451)
XLA Ops:
  0.0 4.0 %fusion.27 = (bf16[1,32,128,128]{3,2,0,1:T(8,128)(2,1)S(1)}, bf16[1,32,128,128]{3,2,0,1:T(8,128)(2,1)}, bf16[1,32,128,128]{3,2,0,1:T(8,128)(2,1)}, bf16[1,32,128,128]{3,2,0,1:T(8,128)(2,1)}) fusion(bf16[1,128,128,128]{3,2,0,1:T(8,128)(2,1)} %bitcast.77), kind=kLoop, calls=%fused_computation.70 | loop fusion | bytes 8388608 | tf_op jit(solution)/shard_map/slice | solution.py:193
  4.0 26.4 %all_to_all.32 = bf16[1,32,128,128]{3,2,0,1:T(8,128)(2,1)} all-to-all(bf16[1,32,128,128]{3,2,0,1:T(8,128)(2,1)S(1)} %get-tuple-element.5), channel_id=1, replica_groups=mesh['shot'=32,'az'=4] {'shot'}, dimensions={1} | all-to-all | bytes 2097152 | tf_op jit(solution)/shard_map/all_to_all | solution.py:193
  30.4 4.0 %all-to-all-start.5 = ((bf16[1,32,128,128]{3,2,0,1:T(8,128)(2,1)}), bf16[1,32,128,128]{3,2,0,1:T(8,128)(2,1)S(1)}, u32[]{:S(2)}, u32[]{:S(2)}) async-start(bf16[1,32,128,128]{3,2,0,1:T(8,128)(2,1)} %get-tuple-element.6), calls=%async_computation.5 | async-start | bytes 2097152 | tf_op jit(solution)/shard_map/all_to_all | solution.py:193
  34.4 17.1 %all-to-all-done.5 = bf16[1,32,128,128]{3,2,0,1:T(8,128)(2,1)S(1)} async-done(((bf16[1,32,128,128]{3,2,0,1:T(8,128)(2,1)}), bf16[1,32,128,128]{3,2,0,1:T(8,128)(2,1)S(1)}, u32[]{:S(2)}, u32[]{:S(2)}) %all-to-all-start.5) | async-done | bytes 1048608 | tf_op jit(solution)/shard_map/all_to_all | solution.py:193
  51.5 4.6 %all-to-all-start.3 = ((bf16[1,32,128,128]{3,2,0,1:T(8,128)(2,1)}), bf16[1,32,128,128]{3,2,0,1:T(8,128)(2,1)}, u32[]{:S(2)}, u32[]{:S(2)}) async-start(bf16[1,32,128,128]{3,2,0,1:T(8,128)(2,1)} %get-tuple-element.7), calls=%async_computation.3 | async-start | bytes 2097152 | tf_op jit(solution)/shard_map/all_to_all | solution.py:193
  63.9 9.5 %all-to-all-done.3 = bf16[1,32,128,128]{3,2,0,1:T(8,128)(2,1)} async-done(((bf16[1,32,128,128]{3,2,0,1:T(8,128)(2,1)}), bf16[1,32,128,128]{3,2,0,1:T(8,128)(2,1)}, u32[]{:S(2)}, u32[]{:S(2)}) %all-to-all-start.3) | async-done | bytes 1048608 | tf_op jit(solution)/shard_map/all_to_all | solution.py:193
  73.4 4.0 %all-to-all-start.1 = ((bf16[1,32,128,128]{3,2,0,1:T(8,128)(2,1)}), bf16[1,32,128,128]{3,2,0,1:T(8,128)(2,1)S(1)}, u32[]{:S(2)}, u32[]{:S(2)}) async-start(bf16[1,32,128,128]{3,2,0,1:T(8,128)(2,1)} %get-tuple-element.8), calls=%async_computation.1 | async-start | bytes 2097152 | tf_op jit(solution)/shard_map/all_to_all | solution.py:193
  79.2 4.2 %broadcast_select_fusion = (bf16[1,16,256,128]{3,2,1,0:T(8,128)(2,1)}, bf16[1,16,256,128]{3,2,1,0:T(8,128)(2,1)}) fusion(bf16[1,16,256,128]{3,2,1,0:T(8,128)(2,1)S(1)} %bitcast.82, pred[16,256]{1,0:T(8,128)(4,1)S(1)} %get-tuple-element.17, bf16[1,16,256,128]{3,2,1,0:T(8,128)(2,1)} %bitcast.20, pred[16,256]{1,0:T(8,128)(4,1)S(1)} %get-tuple-element.18), kind=kLoop, calls=%fused_computation.18 | loop fusion | flops 1048576 | bytes 4202496 | tf_op jit(solution)/shard_map/jit(_where)/select_n | solution.py:195
  83.4 19.7 %shard_map.40 = bf16[32,1,2,64,128]{4,3,2,1,0:T(8,128)(2,1)} custom-call(s32[1]{0:T(128)} %bitcast.24.counts_ref, f32[8]{0:T(128)} %power_multiply_fusion.scales_ref, bf16[1,16,256,128]{3,2,1,0:T(8,128)(2,1)} %get-tuple-element.28.obs_ref, bf16[4,256,512]{2,1,0:T(8,128)(2,1)} %pad_maximum_fusion.1.tab_ref), custom_call_target="tpu_custom_call" | custom-call | tf_op jit(solution)/shard_map/pallas_call | solution.py:173
  103.2 2.7 %broadcast_select_fusion.2 = (bf16[1,16,256,128]{3,2,1,0:T(8,128)(2,1)}, bf16[1,16,256,128]{3,2,1,0:T(8,128)(2,1)}) fusion(bf16[1,16,256,128]{3,2,1,0:T(8,128)(2,1)S(1)} %bitcast.83, pred[16,256]{1,0:T(8,128)(4,1)S(1)} %get-tuple-element.16, bf16[1,16,256,128]{3,2,1,0:T(8,128)(2,1)S(1)} %bitcast.81, pred[16,256]{1,0:T(8,128)(4,1)S(1)} %get-tuple-element.15), kind=kLoop, calls=%fused_computation.20 | loop fusion | flops 1048576 | bytes 4202496 | tf_op jit(solution)/shard_map/jit(_where)/select_n | solution.py:195
  105.9 19.4 %shard_map.38 = bf16[32,1,2,64,128]{4,3,2,1,0:T(8,128)(2,1)} custom-call(s32[1]{0:T(128)} %bitcast.10.counts_ref, f32[8]{0:T(128)} %power_multiply_fusion.scales_ref, bf16[1,16,256,128]{3,2,1,0:T(8,128)(2,1)} %get-tuple-element.30.obs_ref, bf16[4,256,512]{2,1,0:T(8,128)(2,1)} %pad_maximum_fusion.1.tab_ref), custom_call_target="tpu_custom_call" | custom-call | tf_op jit(solution)/shard_map/pallas_call | solution.py:173
  125.2 2.1 fusion.3
  127.4 19.0 %all-to-all-start.7 = ((bf16[32,1,64,128]{3,2,1,0:T(8,128)(2,1)}), bf16[32,1,64,128]{3,2,1,0:T(8,128)(2,1)}, u32[]{:S(2)}, u32[]{:S(2)}) async-start(bf16[32,1,64,128]{3,2,1,0:T(8,128)(2,1)} %fusion.3), calls=%async_computation.7 | async-start | bytes 1048576 | tf_op jit(solution)/shard_map/all_to_all | solution.py:205
  146.3 8.8 %shard_map.39 = bf16[32,1,2,64,128]{4,3,2,1,0:T(8,128)(2,1)} custom-call(s32[1]{0:T(128)} %bitcast.18.counts_ref, f32[8]{0:T(128)} %power_multiply_fusion.scales_ref, bf16[1,16,256,128]{3,2,1,0:T(8,128)(2,1)} %get-tuple-element.29.obs_ref, bf16[4,256,512]{2,1,0:T(8,128)(2,1)} %pad_maximum_fusion.1.tab_ref), custom_call_target="tpu_custom_call" | custom-call | tf_op jit(solution)/shard_map/pallas_call | solution.py:173
  156.4 12.1 %shard_map.37 = bf16[32,1,2,64,128]{4,3,2,1,0:T(8,128)(2,1)} custom-call(s32[1]{0:T(128)} %bitcast.counts_ref, f32[8]{0:T(128)} %power_multiply_fusion.scales_ref, bf16[1,16,256,128]{3,2,1,0:T(8,128)(2,1)} %get-tuple-element.31.obs_ref, bf16[4,256,512]{2,1,0:T(8,128)(2,1)} %pad_maximum_fusion.1.tab_ref), custom_call_target="tpu_custom_call" | custom-call | tf_op jit(solution)/shard_map/pallas_call | solution.py:173
  170.8 1.5 fusion.4
  172.3 36.5 %all-to-all-start.4 = ((bf16[32,1,64,128]{3,2,1,0:T(8,128)(2,1)}), bf16[32,1,64,128]{3,2,1,0:T(8,128)(2,1)S(1)}, u32[]{:S(2)}, u32[]{:S(2)}) async-start(bf16[32,1,64,128]{3,2,1,0:T(8,128)(2,1)} %get-tuple-element.9), calls=%async_computation.4 | async-start | bytes 1048576 | tf_op jit(solution)/shard_map/all_to_all | solution.py:205
  208.9 3.5 %collective-permute-start = (bf16[32,64,128]{2,1,0:T(8,128)(2,1)S(1)}, bf16[32,64,128]{2,1,0:T(8,128)(2,1)S(1)}, u32[]{:S(2)}, u32[]{:S(2)}) collective-permute-start(bf16[32,64,128]{2,1,0:T(8,128)(2,1)S(1)} %slice_bitcast_fusion.1), channel_id=1, source_target_pairs={{0,4},{4,8},{8,12},{12,16},{16,20},{20,24},{24,28},{28,32},{32,36}... | collective-permute-start | bytes 1572872 | tf_op jit(solution)/shard_map/ppermute | solution.py:12
  212.5 8.0 %all-to-all-done.4 = bf16[32,1,64,128]{3,2,1,0:T(8,128)(2,1)S(1)} async-done(((bf16[32,1,64,128]{3,2,1,0:T(8,128)(2,1)}), bf16[32,1,64,128]{3,2,1,0:T(8,128)(2,1)S(1)}, u32[]{:S(2)}, u32[]{:S(2)}) %all-to-all-start.4) | async-done | bytes 524320 | tf_op jit(solution)/shard_map/all_to_all | solution.py:205
  220.4 3.9 %all-to-all-start.6 = ((bf16[32,1,64,128]{3,2,1,0:T(8,128)(2,1)}), bf16[32,1,64,128]{3,2,1,0:T(8,128)(2,1)S(1)}, u32[]{:S(2)}, u32[]{:S(2)}) async-start(bf16[32,1,64,128]{3,2,1,0:T(8,128)(2,1)} %get-tuple-element.10), calls=%async_computation.6 | async-start | bytes 1048576 | tf_op jit(solution)/shard_map/all_to_all | solution.py:205
  224.7 11.2 %all-to-all-done.6 = bf16[32,1,64,128]{3,2,1,0:T(8,128)(2,1)S(1)} async-done(((bf16[32,1,64,128]{3,2,1,0:T(8,128)(2,1)}), bf16[32,1,64,128]{3,2,1,0:T(8,128)(2,1)S(1)}, u32[]{:S(2)}, u32[]{:S(2)}) %all-to-all-start.6) | async-done | bytes 524320 | tf_op jit(solution)/shard_map/all_to_all | solution.py:205
  235.9 15.0 %all_to_all.33 = bf16[32,1,64,128]{3,2,1,0:T(8,128)(2,1)S(1)} all-to-all(bf16[32,1,64,128]{3,2,1,0:T(8,128)(2,1)S(1)} %fusion.6), channel_id=1, replica_groups=mesh['shot'=32,'az'=4] {'shot'}, dimensions={0} | all-to-all | bytes 1048576 | tf_op jit(solution)/shard_map/all_to_all | solution.py:205
  251.0 1.3 pad_maximum_fusion
  252.3 1.5 copy.29
  (46 shorter events, 13.4 us)
Async XLA Ops:
  30.4 21.1 %all-to-all-start.5 = ((bf16[1,32,128,128]{3,2,0,1:T(8,128)(2,1)}), bf16[1,32,128,128]{3,2,0,1:T(8,128)(2,1)S(1)}, u32[]{:S(2)}, u32[]{:S(2)}) async-start(bf16[1,32,128,128]{3,2,0,1:T(8,128)(2,1)} %get-tuple-element.6), calls=%async_computation.5 | async-start | bytes 2097152 | tf_op jit(solution)/shard_map/all_to_all | solution.py:193
  51.5 4.6 %copy-start.2 = (bf16[1,32,128,128]{3,2,0,1:T(8,128)(2,1)}, bf16[1,32,128,128]{3,2,0,1:T(8,128)(2,1)S(1)}, u32[]{:S(2)}) copy-start(bf16[1,32,128,128]{3,2,0,1:T(8,128)(2,1)S(1)} %all-to-all-done.5) | copy-start | bytes 3145732
  51.5 21.9 %all-to-all-start.3 = ((bf16[1,32,128,128]{3,2,0,1:T(8,128)(2,1)}), bf16[1,32,128,128]{3,2,0,1:T(8,128)(2,1)}, u32[]{:S(2)}, u32[]{:S(2)}) async-start(bf16[1,32,128,128]{3,2,0,1:T(8,128)(2,1)} %get-tuple-element.7), calls=%async_computation.3 | async-start | bytes 2097152 | tf_op jit(solution)/shard_map/all_to_all | solution.py:193
  60.2 3.0 %copy-start.9 = (s32[1,4]{1,0:T(1,128)S(1)}, s32[1,4]{1,0:T(1,128)}, u32[]{:S(2)}) copy-start(s32[1,4]{1,0:T(1,128)} %param.5) | copy-start | bytes 52
  61.2 16.8 %copy-start.7 = (bf16[256,256]{1,0:T(8,128)(2,1)S(1)}, bf16[256,256]{1,0:T(8,128)(2,1)}, u32[]{:S(2)}) copy-start(bf16[256,256]{1,0:T(8,128)(2,1)} %neg.38) | copy-start | bytes 393220
  73.4 29.8 %all-to-all-start.1 = ((bf16[1,32,128,128]{3,2,0,1:T(8,128)(2,1)}), bf16[1,32,128,128]{3,2,0,1:T(8,128)(2,1)S(1)}, u32[]{:S(2)}, u32[]{:S(2)}) async-start(bf16[1,32,128,128]{3,2,0,1:T(8,128)(2,1)} %get-tuple-element.8), calls=%async_computation.1 | async-start | bytes 2097152 | tf_op jit(solution)/shard_map/all_to_all | solution.py:193
  77.4 1.8 copy-start.8
  77.4 1.8 copy-start.3
  83.4 19.7 %copy-start.1 = (bf16[1,32,128,128]{3,2,0,1:T(8,128)(2,1)S(1)}, bf16[1,32,128,128]{3,2,0,1:T(8,128)(2,1)}, u32[]{:S(2)}) copy-start(bf16[1,32,128,128]{3,2,0,1:T(8,128)(2,1)} %all_to_all.32) | copy-start | bytes 3145732
  105.9 19.4 %copy-start.4 = (bf16[32,1,2,64,128]{4,3,2,1,0:T(8,128)(2,1)S(1)}, bf16[32,1,2,64,128]{4,3,2,1,0:T(8,128)(2,1)}, u32[]{:S(2)}) copy-start(bf16[32,1,2,64,128]{4,3,2,1,0:T(8,128)(2,1)} %shard_map.40) | copy-start | bytes 3145732
  127.4 45.0 %all-to-all-start.7 = ((bf16[32,1,64,128]{3,2,1,0:T(8,128)(2,1)}), bf16[32,1,64,128]{3,2,1,0:T(8,128)(2,1)}, u32[]{:S(2)}, u32[]{:S(2)}) async-start(bf16[32,1,64,128]{3,2,1,0:T(8,128)(2,1)} %fusion.3), calls=%async_computation.7 | async-start | bytes 1048576 | tf_op jit(solution)/shard_map/all_to_all | solution.py:205
  169.8 1.0 copy-start.5
  170.8 38.1 %copy-start = (bf16[32,1,2,64,128]{4,3,2,1,0:T(8,128)(2,1)S(1)}, bf16[32,1,2,64,128]{4,3,2,1,0:T(8,128)(2,1)}, u32[]{:S(2)}) copy-start(bf16[32,1,2,64,128]{4,3,2,1,0:T(8,128)(2,1)} %shard_map.38) | copy-start | bytes 3145732
  172.3 52.0 %copy-start.6 = (bf16[32,1,2,64,128]{4,3,0,2,1:T(8,128)(2,1)S(1)}, bf16[32,1,2,64,128]{4,3,0,2,1:T(8,128)(2,1)}, u32[]{:S(2)}) copy-start(bf16[32,1,2,64,128]{4,3,0,2,1:T(8,128)(2,1)} %copy-done.5) | copy-start | bytes 3145732
  172.3 48.1 %all-to-all-start.4 = ((bf16[32,1,64,128]{3,2,1,0:T(8,128)(2,1)}), bf16[32,1,64,128]{3,2,1,0:T(8,128)(2,1)S(1)}, u32[]{:S(2)}, u32[]{:S(2)}) async-start(bf16[32,1,64,128]{3,2,1,0:T(8,128)(2,1)} %get-tuple-element.9), calls=%async_computation.4 | async-start | bytes 1048576 | tf_op jit(solution)/shard_map/all_to_all | solution.py:205
  208.9 15.4 %collective-permute-start = (bf16[32,64,128]{2,1,0:T(8,128)(2,1)S(1)}, bf16[32,64,128]{2,1,0:T(8,128)(2,1)S(1)}, u32[]{:S(2)}, u32[]{:S(2)}) collective-permute-start(bf16[32,64,128]{2,1,0:T(8,128)(2,1)S(1)} %slice_bitcast_fusion.1), channel_id=1, source_target_pairs={{0,4},{4,8},{8,12},{12,16},{16,20},{20,24},{24,28},{28,32},{32,36}... | collective-permute-start | bytes 1572872 | tf_op jit(solution)/shard_map/ppermute | solution.py:12
  220.4 15.5 %all-to-all-start.6 = ((bf16[32,1,64,128]{3,2,1,0:T(8,128)(2,1)}), bf16[32,1,64,128]{3,2,1,0:T(8,128)(2,1)S(1)}, u32[]{:S(2)}, u32[]{:S(2)}) async-start(bf16[32,1,64,128]{3,2,1,0:T(8,128)(2,1)} %get-tuple-element.10), calls=%async_computation.6 | async-start | bytes 1048576 | tf_op jit(solution)/shard_map/all_to_all | solution.py:205

commit v8 on v6

--- a/solution.py
+++ b/solution.py
@@ -47,7 +47,7 @@
 GROUP = 16
 
 
-def pocs_kernel(counts_ref, scales_ref, obs_ref, tab_ref, out_ref, y_ref, v_ref):
+def pocs_kernel(counts_ref, scales_ref, obs_ref, mask_ref, tab_ref, out_ref, y_ref, v_ref):
     p = pl.program_id(0)
     extent = obs_ref.shape[1]
     lanes = obs_ref.shape[3]
@@ -84,10 +84,6 @@
         for quarter in range(4):
             out_ref[(a % half_axis) * 4 + quarter, 0, a // half_axis] = value[quarter * rows:(quarter + 1) * rows]
 
-    def recorded(v):
-        wide = v.astype(jnp.float32)
-        return wide == wide
-
     def magnitude(c):
         return jnp.sqrt(c * c + pltpu.roll(c, half, 1) ** 2)
 
@@ -96,7 +92,7 @@
         initial = []
         for g in range(group):
             observed = obs_ref[0, a0 + g]
-            value = jnp.where(recorded(observed), observed, jnp.zeros_like(observed))
+            value = jnp.where(mask_ref[0, a0 + g] > 0, observed, jnp.zeros_like(observed))
             write_out(a0 + g, value)
             initial.append(value)
         stage_one(a0, initial)
@@ -139,7 +135,7 @@
             updated = []
             for g in range(group):
                 observed = obs_ref[0, a0 + g].astype(jnp.float32)
-                value = jnp.where(observed == observed, observed, returned[g]).astype(jnp.bfloat16)
+                value = jnp.where(mask_ref[0, a0 + g] > 0, observed, returned[g]).astype(jnp.bfloat16)
                 write_out(a0 + g, value)
                 updated.append(value)
 
@@ -155,7 +151,7 @@
     lax.fori_loop(0, sweeps, sweep_step, 0)
 
 
-def run_patches(observed, sweeps, scales, tables):
+def run_patches(observed, maskb, sweeps, scales, tables):
     count, extent, plane, lanes = observed.shape
     block = pl.BlockSpec((1, extent, plane, lanes), lambda p, c, s: (p, 0, 0, 0))
     dests = extent // 2 * 4
@@ -163,7 +159,7 @@
     grid_spec = pltpu.PrefetchScalarGridSpec(
         num_scalar_prefetch=2,
         grid=(count,),
-        in_specs=[block, pl.BlockSpec(tables.shape, lambda p, c, s: (0, 0, 0))],
+        in_specs=[block, block, pl.BlockSpec(tables.shape, lambda p, c, s: (0, 0, 0))],
         out_specs=out_block,
         scratch_shapes=[
             pltpu.VMEM((extent, extent, extent, lanes), jnp.bfloat16),
@@ -175,7 +171,7 @@
         grid_spec=grid_spec,
         out_shape=jax.ShapeDtypeStruct((dests, count, 2, plane // 4, lanes), jnp.bfloat16),
         compiler_params=pltpu.CompilerParams(dimension_semantics=("arbitrary",)),
-    )(sweeps, scales, observed, tables)
+    )(sweeps, scales, observed, maskb, tables)
 
 
 def shards(spectra, sampled_mask, counts):
@@ -183,15 +179,23 @@
     plane = extent * extent
     lane_count = spectra.shape[3]
     halfway = extent // 2
-    regrouped = lax.all_to_all(spectra, "shot", split_axis=1, concat_axis=2, tiled=True)
-    owned_count = regrouped.shape[1]
-    observed = regrouped.reshape(owned_count, extent, plane, lane_count)
-    marked = jnp.where(sampled_mask[0][..., None] > 0, observed, jnp.nan).astype(observed.dtype)
+    devices = lax.axis_size("shot")
+    owned_count = counts.shape[1]
+    chunk = owned_count // 2
     tables = kernel_tables(extent)
     steps = jnp.arange(8, dtype=jnp.float32)
     scales = 0.5 * jnp.power(jnp.float32(0.6), steps)
-
-    result = run_patches(marked, counts[0], scales, tables)
+    by_owner = spectra.reshape((1, devices, owned_count) + spectra.shape[2:])
+
+    pieces = []
+    for first in range(0, owned_count, chunk):
+        part = by_owner[:, :, first:first + chunk].reshape((1, devices * chunk) + spectra.shape[2:])
+        regrouped = lax.all_to_all(part, "shot", split_axis=1, concat_axis=2, tiled=True)
+        observed = regrouped.reshape(chunk, extent, plane, lane_count)
+        recorded = (sampled_mask[0, first:first + chunk] > 0).astype(jnp.bfloat16)
+        maskb = jnp.broadcast_to(recorded[..., None], observed.shape)
+        pieces.append(run_patches(observed, maskb, counts[0, first:first + chunk], scales, tables))
+    result = jnp.concatenate(pieces, axis=1)
     dests = result.shape[0]
     top = result[:, :, 1]
     arrived = passed_along(top[:, -1], "shot", 1)

time: 204 us -> 222 us (1.088)
  blocking collectives: 31.2 us -> 68.8 us
  starting transfers between devices: 35.6 us -> 6.11 us
  waiting for transfers between devices: 80.3 us -> 59.2 us
  Pallas kernels: 36.7 us -> 53.1 us
  local copies, waits for them, and re-layouts: 10.7 us -> 23.7 us
    all_to_all x0 -> x1, blocking collectives: none -> 37.6 us  [shards(): lax.all_to_all(part, 'shot', split_axis=1, concat_axis=2, tiled=True)]
    all_to_all x1, waiting for transfers between devices: 42.5 us -> 8.12 us  [shards(): lax.all_to_all(part, 'shot', split_axis=1, concat_axis=2, tiled=True)]
    ppermute x1, starting transfers between devices: 26.1 us -> 2.05 us  [passed_along(): return lax.ppermute(block, axis, route)]
    pallas_call x1 -> x2, Pallas kernels: 36.7 us -> 53.1 us  [run_patches(): pl.pallas_call(pocs_kernel, grid_spec=grid_spec, out_shape=jax.ShapeDtype...]
    ppermute x1, waiting for transfers between devices: 37.8 us -> 51.1 us  [passed_along(): return lax.ppermute(block, axis, route)]
    all_to_all x1, starting transfers between devices: 9.47 us -> 4.06 us  [shards(): lax.all_to_all(part, 'shot', split_axis=1, concat_axis=2, tiled=True)]
    select_n x1 -> x0, other arithmetic: 4.94 us -> none  [shards(): jnp.where(sampled_mask[0][..., None] > 0, observed, jnp.nan)]
    broadcast_in_dim x0 -> x2, local copies, waits for them, and re-layouts: none -> 4.47 us  [shards(): maskb = jnp.broadcast_to(recorded[..., None], observed.shape)]
  transfers between devices with their start and end apart: 2 -> 2, of which waited for: 2 -> 2; matrix products, arithmetic and copies ran while one was open for 4% -> 9% of each run, Pallas kernels for 0% -> 0%
where the time goes in v8:
time: 222 us
  blocking collectives  68.8 us (31%)
  waiting for transfers between devices  59.2 us (27%)
  Pallas kernels  53.1 us (24%)
  local copies, waits for them, and re-layouts  23.7 us (11%)
  other arithmetic  10.7 us (5%)
  starting transfers between devices  6.11 us (3%)
    pallas_call x2, Pallas kernels, run_patches(): pl.pallas_call(pocs_kernel, grid_spec=grid_spec, out_shape=jax.ShapeDtype...  53.1 us
    ppermute x1, waiting for transfers between devices, passed_along(): return lax.ppermute(block, axis, route)  51.1 us
    all_to_all x1, blocking collectives, shards(): lax.all_to_all(part, 'shot', split_axis=1, concat_axis=2, tiled=True)  37.6 us
    all_to_all x1, blocking collectives, shards(): lax.all_to_all(mixed, 'shot', split_axis=0, concat_axis=1, tiled=True)  31.2 us
    all_to_all x1, waiting for transfers between devices, shards(): lax.all_to_all(part, 'shot', split_axis=1, concat_axis=2, tiled=True)  8.12 us
    convert_element_type x3, local copies, waits for them, and re-layouts, spread(): return jnp.kron(table.astype(jnp.float32), eye).astype(jnp.bfloat16)  6.09 us
    broadcast_in_dim x2, local copies, waits for them, and re-layouts, shards(): maskb = jnp.broadcast_to(recorded[..., None], observed.shape)  4.47 us
  transfers between devices with their start and end apart: 2, of which 2 were waited for; matrix products, arithmetic and copies ran while one was open for 9% of the time, Pallas kernels for 0%

profile of v8, /device:TPU:1, one launch (start us, length us, event | category | flops | bytes accessed | tf_op | source)
XLA Modules:
  0.0 221.8 jit_solution(18321554809911306372)
XLA Ops:
  0.0 4.1 %fusion.25 = (bf16[1,32,2,128,128]{4,3,2,1,0:T(8,128)(2,1)S(1)}, bf16[1,32,2,128,128]{4,3,2,1,0:T(8,128)(2,1)}) fusion(bf16[1,32,4,128,128]{4,3,2,1,0:T(8,128)(2,1)} %bitcast.59), kind=kLoop, calls=%fused_computation.58 | loop fusion | bytes 8388608 | tf_op jit(solution)/shard_map/slice | solution.py:192
  4.1 37.6 %all_to_all.42 = bf16[1,64,128,128]{3,2,0,1:T(8,128)(2,1)} all-to-all(bf16[1,64,128,128]{3,2,0,1:T(8,128)(2,1)S(1)} %bitcast.58), channel_id=1, replica_groups=mesh['shot'=32,'az'=4] {'shot'}, dimensions={1} | all-to-all | bytes 4194304 | tf_op jit(solution)/shard_map/all_to_all | solution.py:193
  41.7 4.1 %all-to-all-start = ((bf16[1,64,128,128]{3,2,0,1:T(8,128)(2,1)}), bf16[1,64,128,128]{3,2,0,1:T(8,128)(2,1)S(1)}, u32[]{:S(2)}, u32[]{:S(2)}) async-start(bf16[1,64,128,128]{3,2,0,1:T(8,128)(2,1)} %bitcast.55), calls=%async_computation | async-start | bytes 4194304 | tf_op jit(solution)/shard_map/all_to_all | solution.py:193
  45.9 1.8 multiply_convert_fusion.1
  47.8 2.2 convert_element_type.197
  50.0 2.2 %convert_element_type.201 = bf16[256,256]{1,0:T(8,128)(2,1)S(1)} reshape(bf16[16,16,16,16]{3,2,1,0:T(8,128)(2,1)} %get-tuple-element.15) | data formatting | bytes 262144 | tf_op jit(solution)/shard_map/convert_element_type | solution.py:37
  52.2 1.7 convert_element_type.204
  54.0 1.6 add_convert_fusion
  55.5 2.2 convert_element_type.192
  58.5 1.6 convert_element_type.190
  62.7 1.1 pad_maximum_fusion.1.tab_ref
  64.5 1.5 copy.11
  66.0 8.1 %all-to-all-done = bf16[1,64,128,128]{3,2,0,1:T(8,128)(2,1)S(1)} async-done(((bf16[1,64,128,128]{3,2,0,1:T(8,128)(2,1)}), bf16[1,64,128,128]{3,2,0,1:T(8,128)(2,1)S(1)}, u32[]{:S(2)}, u32[]{:S(2)}) %all-to-all-start) | async-done | bytes 2097184 | tf_op jit(solution)/shard_map/all_to_all | solution.py:193
  74.1 1.6 copy.10
  75.7 2.2 %broadcast_in_dim.37.mask_ref = bf16[2,16,256,128]{3,2,1,0:T(8,128)(2,1)} broadcast(bf16[2,16,256]{2,1,0:T(8,128)(2,1)S(1)} %get-tuple-element.11), dimensions={0,1,2} | broadcast | bytes 2113536 | tf_op jit(solution)/shard_map/broadcast_in_dim | solution.py:196
  77.9 35.9 %shard_map.38 = bf16[32,2,2,64,128]{4,3,2,1,0:T(8,128)(2,1)} custom-call(s32[2]{0:T(128)} %get-tuple-element.18.counts_ref, f32[8]{0:T(128)} %power_multiply_fusion.scales_ref, bf16[2,16,256,128]{3,2,1,0:T(8,128)(2,1)} %bitcast.57, bf16[2,16,256,128]{3,2,1,0:T(8,128)(2,1)} %broadcast_in_dim.37.mask_ref, bf16[4,256,512]{2,1,0:T(8,128)(2,1)} %pad_maximum_fusion.1.tab_ref), custom_call_target="tpu_custom_call" | custom-call | tf_op jit(solution)/shard_map/pallas_call | solution.py:169
  113.8 2.2 %broadcast_in_dim.36.mask_ref = bf16[2,16,256,128]{3,2,1,0:T(8,128)(2,1)} broadcast(bf16[2,16,256]{2,1,0:T(8,128)(2,1)S(1)} %get-tuple-element.12), dimensions={0,1,2} | broadcast | bytes 2113536 | tf_op jit(solution)/shard_map/broadcast_in_dim | solution.py:196
  116.0 17.3 %shard_map.37 = bf16[32,2,2,64,128]{4,3,2,1,0:T(8,128)(2,1)} custom-call(s32[2]{0:T(128)} %get-tuple-element.19.counts_ref, f32[8]{0:T(128)} %power_multiply_fusion.scales_ref, bf16[2,16,256,128]{3,2,1,0:T(8,128)(2,1)} %bitcast.56, bf16[2,16,256,128]{3,2,1,0:T(8,128)(2,1)} %broadcast_in_dim.36.mask_ref, bf16[4,256,512]{2,1,0:T(8,128)(2,1)} %pad_maximum_fusion.1.tab_ref), custom_call_target="tpu_custom_call" | custom-call | tf_op jit(solution)/shard_map/pallas_call | solution.py:169
  133.3 1.4 fusion.4
  134.8 2.1 collective-permute-start
  137.0 51.1 %collective-permute-done = bf16[32,64,128]{2,1,0:T(8,128)(2,1)S(1)} collective-permute-done((bf16[32,64,128]{2,1,0:T(8,128)(2,1)S(1)}, bf16[32,64,128]{2,1,0:T(8,128)(2,1)S(1)}, u32[]{:S(2)}, u32[]{:S(2)}) %collective-permute-start) | collective-permute-done | bytes 524320 | tf_op jit(solution)/shard_map/ppermute | solution.py:12
  188.1 1.2 fusion.1
  189.3 31.2 %all_to_all.43 = bf16[32,4,64,128]{3,2,1,0:T(8,128)(2,1)S(1)} all-to-all(bf16[32,4,64,128]{3,2,1,0:T(8,128)(2,1)S(1)} %fusion.1), channel_id=1, replica_groups=mesh['shot'=32,'az'=4] {'shot'}, dimensions={0} | all-to-all | bytes 4194304 | tf_op jit(solution)/shard_map/all_to_all | solution.py:207
  220.5 1.3 copy.17
  (23 shorter events, 4.4 us)
Async XLA Ops:
  41.7 32.4 %all-to-all-start = ((bf16[1,64,128,128]{3,2,0,1:T(8,128)(2,1)}), bf16[1,64,128,128]{3,2,0,1:T(8,128)(2,1)S(1)}, u32[]{:S(2)}, u32[]{:S(2)}) async-start(bf16[1,64,128,128]{3,2,0,1:T(8,128)(2,1)} %bitcast.55), calls=%async_computation | async-start | bytes 4194304 | tf_op jit(solution)/shard_map/all_to_all | solution.py:193
  60.1 3.8 %copy-start.4 = (s32[1,4]{1,0:T(1,128)S(1)}, s32[1,4]{1,0:T(1,128)}, u32[]{:S(2)}) copy-start(s32[1,4]{1,0:T(1,128)} %param.5) | copy-start | bytes 52
  60.1 4.4 %copy-start.3 = (s32[1,4,16,256]{3,2,1,0:T(8,128)S(1)}, s32[1,4,16,256]{3,2,1,0:T(8,128)}, u32[]{:S(2)}) copy-start(s32[1,4,16,256]{3,2,1,0:T(8,128)} %param.4) | copy-start | bytes 196612
  60.1 4.4 %copy-start.2 = (bf16[1,64,128,128]{3,2,0,1:T(8,128)(2,1)S(1)}, bf16[1,64,128,128]{3,2,0,1:T(8,128)(2,1)}, u32[]{:S(2)}) copy-start(bf16[1,64,128,128]{3,2,0,1:T(8,128)(2,1)} %all_to_all.42) | copy-start | bytes 6291460
  116.0 17.3 %copy-start = (bf16[32,2,2,64,128]{4,3,2,1,0:T(8,128)(2,1)S(1)}, bf16[32,2,2,64,128]{4,3,2,1,0:T(8,128)(2,1)}, u32[]{:S(2)}) copy-start(bf16[32,2,2,64,128]{4,3,2,1,0:T(8,128)(2,1)} %shard_map.38) | copy-start | bytes 6291460
  134.7 53.4 %copy-start.1 = (bf16[32,2,2,64,128]{4,3,2,1,0:T(8,128)(2,1)S(1)}, bf16[32,2,2,64,128]{4,3,2,1,0:T(8,128)(2,1)}, u32[]{:S(2)}) copy-start(bf16[32,2,2,64,128]{4,3,2,1,0:T(8,128)(2,1)} %shard_map.37) | copy-start | bytes 6291460
  134.8 53.3 %collective-permute-start = (bf16[32,64,128]{2,1,0:T(8,128)(2,1)S(1)}, bf16[32,64,128]{2,1,0:T(8,128)(2,1)S(1)}, u32[]{:S(2)}, u32[]{:S(2)}) collective-permute-start(bf16[32,64,128]{2,1,0:T(8,128)(2,1)S(1)} %slice_bitcast_fusion), channel_id=1, source_target_pairs={{0,4},{4,8},{8,12},{12,16},{16,20},{20,24},{24,28},{28,32},{32,36}... | collective-permute-start | bytes 1572872 | tf_op jit(solution)/shard_map/ppermute | solution.py:12

commit v9 on v8

--- a/solution.py
+++ b/solution.py
@@ -1,3 +1,6 @@
+import ml_dtypes
+import numpy as np
+
 import jax
 import jax.numpy as jnp
 from jax import lax
@@ -12,36 +15,29 @@
     return lax.ppermute(block, axis, route)
 
 
-def dft_tables(extent):
-    indices = jnp.arange(extent, dtype=jnp.int32)
+def kernel_tables(extent):
+    indices = np.arange(extent, dtype=np.int32)
     product = indices[:, None] * indices[None, :] % extent
-    phase = product.astype(jnp.float32) * (2.0 * jnp.pi / extent)
-    scale = extent ** (-0.5)
-    cos_table = jnp.cos(phase) * scale
-    sin_table = -jnp.sin(phase) * scale
-    kron_real = jnp.kron(cos_table, cos_table) - jnp.kron(sin_table, sin_table)
-    kron_imag = jnp.kron(cos_table, sin_table) + jnp.kron(sin_table, cos_table)
-    return (
-        cos_table.astype(jnp.bfloat16),
-        sin_table.astype(jnp.bfloat16),
-        kron_real.astype(jnp.bfloat16),
-        kron_imag.astype(jnp.bfloat16),
-    )
-
-
-def kernel_tables(extent):
-    cos_table, sin_table, kron_real, kron_imag = dft_tables(extent)
-    eye = jnp.eye(extent, dtype=jnp.float32)
+    phase = product.astype(np.float32) * np.float32(2.0 * np.pi / extent)
+    scale = np.float32(extent ** (-0.5))
+    cos_table = np.cos(phase) * scale
+    sin_table = -np.sin(phase) * scale
+    kron_real = np.kron(cos_table, cos_table) - np.kron(sin_table, sin_table)
+    kron_imag = np.kron(cos_table, sin_table) + np.kron(sin_table, cos_table)
+    bf16 = ml_dtypes.bfloat16
+    cos_b, sin_b = cos_table.astype(bf16), sin_table.astype(bf16)
+    real_b, imag_b = kron_real.astype(bf16), kron_imag.astype(bf16)
+    eye = np.eye(extent, dtype=np.float32)
 
     def spread(table):
-        return jnp.kron(table.astype(jnp.float32), eye).astype(jnp.bfloat16)
-
-    return jnp.stack([
-        jnp.concatenate([kron_real, kron_imag], axis=1),
-        jnp.concatenate([kron_real, -kron_imag], axis=1),
-        jnp.concatenate([spread(cos_table), spread(sin_table)], axis=1),
-        jnp.concatenate([spread(cos_table), spread(-sin_table)], axis=1),
-    ])
+        return np.kron(table.astype(np.float32), eye).astype(bf16)
+
+    return jnp.asarray(np.stack([
+        np.concatenate([real_b, imag_b], axis=1),
+        np.concatenate([real_b, -imag_b], axis=1),
+        np.concatenate([spread(cos_b), spread(sin_b)], axis=1),
+        np.concatenate([spread(cos_b), spread(-sin_b)], axis=1),
+    ]))
 
 
 GROUP = 16

time: 222 us -> 222 us (level)
  waiting for transfers between devices: 59.2 us -> 75 us
  local copies, waits for them, and re-layouts: 23.7 us -> 15.3 us
  other arithmetic: 10.7 us -> 3.19 us
    all_to_all x1, waiting for transfers between devices: 8.12 us -> 23.9 us  [shards(): lax.all_to_all(part, 'shot', split_axis=1, concat_axis=2, tiled=True)]
    convert_element_type x5 -> x0, local copies, waits for them, and re-layouts: 9.94 us -> none  [the longest x3 6.09 us: spread(): return jnp.kron(table.astype(jnp.float32), eye).astype(jnp.bfloat16)]
    convert_element_type x5 -> x0, other arithmetic: 3.56 us -> none  [the longest x3 1.97 us: spread(): return jnp.kron(table.astype(jnp.float32), eye).astype(jnp.bfloat16)]
    another operation x3 -> x0, other arithmetic: 3.19 us -> none  [kernel_tables(): jnp.stack([jnp.concatenate([kron_real, kron_imag], axis=1), jnp.concatena...]
  transfers between devices with their start and end apart: 2 -> 2, of which waited for: 2 -> 2; matrix products, arithmetic and copies ran while one was open for 9% -> 2% of each run, Pallas kernels for 0% -> 0%
where the time goes in v9:
time: 222 us
  waiting for transfers between devices  75 us (34%)
  blocking collectives  68.8 us (31%)
  Pallas kernels  53.2 us (24%)
  local copies, waits for them, and re-layouts  15.3 us (7%)
  starting transfers between devices  6.25 us (3%)
  other arithmetic  3.19 us (1%)
    pallas_call x2, Pallas kernels, run_patches(): pl.pallas_call(pocs_kernel, grid_spec=grid_spec, out_shape=jax.ShapeDtype...  53.2 us
    ppermute x1, waiting for transfers between devices, passed_along(): return lax.ppermute(block, axis, route)  51.1 us
    all_to_all x1, blocking collectives, shards(): lax.all_to_all(part, 'shot', split_axis=1, concat_axis=2, tiled=True)  37.6 us
    all_to_all x1, blocking collectives, shards(): lax.all_to_all(mixed, 'shot', split_axis=0, concat_axis=1, tiled=True)  31.2 us
    all_to_all x1, waiting for transfers between devices, shards(): lax.all_to_all(part, 'shot', split_axis=1, concat_axis=2, tiled=True)  23.9 us
    all_to_all x2, local copies, waits for them, and re-layouts, shards(): lax.all_to_all(part, 'shot', split_axis=1, concat_axis=2, tiled=True)  4.63 us
  transfers between devices with their start and end apart: 2, of which 2 were waited for; matrix products, arithmetic and copies ran while one was open for 2% of the time, Pallas kernels for 0%

profile of v9, /device:TPU:1, one launch (start us, length us, event | category | flops | bytes accessed | tf_op | source)
XLA Modules:
  0.0 221.8 jit_solution(15764087680616186785)
XLA Ops:
  0.0 4.1 %fusion.12 = (bf16[1,32,2,128,128]{4,3,2,1,0:T(8,128)(2,1)}, bf16[1,32,2,128,128]{4,3,2,1,0:T(8,128)(2,1)S(1)}) fusion(bf16[1,32,4,128,128]{4,3,2,1,0:T(8,128)(2,1)} %bitcast.41), kind=kLoop, calls=%fused_computation.27 | loop fusion | bytes 8388608 | tf_op jit(solution)/shard_map/slice | solution.py:188
  4.1 37.6 %all_to_all.42 = bf16[1,64,128,128]{3,2,0,1:T(8,128)(2,1)} all-to-all(bf16[1,64,128,128]{3,2,0,1:T(8,128)(2,1)S(1)} %bitcast.40), channel_id=1, replica_groups=mesh['shot'=32,'az'=4] {'shot'}, dimensions={1} | all-to-all | bytes 4194304 | tf_op jit(solution)/shard_map/all_to_all | solution.py:189
  41.7 4.2 %all-to-all-start.1 = ((bf16[1,64,128,128]{3,2,0,1:T(8,128)(2,1)}), bf16[1,64,128,128]{3,2,0,1:T(8,128)(2,1)S(1)}, u32[]{:S(2)}, u32[]{:S(2)}) async-start(bf16[1,64,128,128]{3,2,0,1:T(8,128)(2,1)} %bitcast.37), calls=%async_computation.1 | async-start | bytes 4194304 | tf_op jit(solution)/shard_map/all_to_all | solution.py:189
  45.9 0.5 power_multiply_fusion.scales_ref
  46.4 0.0 copy-done.3
  46.4 0.7 slice_bitcast_fusion.1
  47.1 0.0 copy-done.2
  47.1 3.2 %copy.11 = bf16[1,2,32,128,128]{4,3,2,1,0:T(8,128)(2,1)} copy(bf16[1,2,32,128,128]{4,3,1,2,0:T(8,128)(2,1)} %bitcast.35) | data formatting | bytes 4194304 | tf_op jit(solution)/shard_map/all_to_all | solution.py:189
  50.3 23.9 %all-to-all-done.1 = bf16[1,64,128,128]{3,2,0,1:T(8,128)(2,1)S(1)} async-done(((bf16[1,64,128,128]{3,2,0,1:T(8,128)(2,1)}), bf16[1,64,128,128]{3,2,0,1:T(8,128)(2,1)S(1)}, u32[]{:S(2)}, u32[]{:S(2)}) %all-to-all-start.1) | async-done | bytes 2097184 | tf_op jit(solution)/shard_map/all_to_all | solution.py:189
  74.2 1.5 copy.12
  75.7 2.2 broadcast_in_dim.6.mask_ref
  77.8 17.2 %shard_map.46 = bf16[32,2,2,64,128]{4,3,2,1,0:T(8,128)(2,1)} custom-call(s32[2]{0:T(128)} %get-tuple-element.10.counts_ref, f32[8]{0:T(128)} %power_multiply_fusion.scales_ref, bf16[2,16,256,128]{3,2,1,0:T(8,128)(2,1)} %bitcast.39, bf16[2,16,256,128]{3,2,1,0:T(8,128)(2,1)} %broadcast_in_dim.6.mask_ref, bf16[4,256,512]{2,1,0:T(8,128)(2,1)} %constant.33.clone.tab_ref), custom_call_target="tpu_custom_call" | custom-call | tf_op jit(solution)/shard_map/pallas_call | solution.py:165
  95.0 2.2 broadcast_in_dim.7.mask_ref
  97.2 36.1 %shard_map.47 = bf16[32,2,2,64,128]{4,3,2,1,0:T(8,128)(2,1)} custom-call(s32[2]{0:T(128)} %get-tuple-element.9.counts_ref, f32[8]{0:T(128)} %power_multiply_fusion.scales_ref, bf16[2,16,256,128]{3,2,1,0:T(8,128)(2,1)} %bitcast.38, bf16[2,16,256,128]{3,2,1,0:T(8,128)(2,1)} %broadcast_in_dim.7.mask_ref, bf16[4,256,512]{2,1,0:T(8,128)(2,1)} %constant.33.clone.tab_ref), custom_call_target="tpu_custom_call" | custom-call | tf_op jit(solution)/shard_map/pallas_call | solution.py:165
  133.3 0.0 copy-done
  133.3 1.4 fusion.4
  134.7 0.0 copy-start.1
  134.7 2.1 collective-permute-start
  136.8 0.2 slice.45
  137.0 51.1 %collective-permute-done = bf16[32,64,128]{2,1,0:T(8,128)(2,1)S(1)} collective-permute-done((bf16[32,64,128]{2,1,0:T(8,128)(2,1)S(1)}, bf16[32,64,128]{2,1,0:T(8,128)(2,1)S(1)}, u32[]{:S(2)}, u32[]{:S(2)}) %collective-permute-start) | collective-permute-done | bytes 524320 | tf_op jit(solution)/shard_map/ppermute | solution.py:15
  188.0 0.0 copy-done.1
  188.0 1.2 fusion.1
  189.3 31.2 %all_to_all.43 = bf16[32,4,64,128]{3,2,1,0:T(8,128)(2,1)S(1)} all-to-all(bf16[32,4,64,128]{3,2,1,0:T(8,128)(2,1)S(1)} %fusion.1), channel_id=1, replica_groups=mesh['shot'=32,'az'=4] {'shot'}, dimensions={0} | all-to-all | bytes 4194304 | tf_op jit(solution)/shard_map/all_to_all | solution.py:203
  220.5 1.3 copy.18
  (6 shorter events, 0.1 us)
Async XLA Ops:
  41.7 4.7 %copy-start.3 = (s32[1,4]{1,0:T(1,128)S(1)}, s32[1,4]{1,0:T(1,128)}, u32[]{:S(2)}) copy-start(s32[1,4]{1,0:T(1,128)} %param.6) | copy-start | bytes 52
  41.7 5.4 %copy-start.2 = (s32[1,4,16,256]{3,2,1,0:T(8,128)S(1)}, s32[1,4,16,256]{3,2,1,0:T(8,128)}, u32[]{:S(2)}) copy-start(s32[1,4,16,256]{3,2,1,0:T(8,128)} %param.5) | copy-start | bytes 196612
  41.7 32.5 %all-to-all-start.1 = ((bf16[1,64,128,128]{3,2,0,1:T(8,128)(2,1)}), bf16[1,64,128,128]{3,2,0,1:T(8,128)(2,1)S(1)}, u32[]{:S(2)}, u32[]{:S(2)}) async-start(bf16[1,64,128,128]{3,2,0,1:T(8,128)(2,1)} %bitcast.37), calls=%async_computation.1 | async-start | bytes 4194304 | tf_op jit(solution)/shard_map/all_to_all | solution.py:189
  97.2 36.1 %copy-start = (bf16[32,2,2,64,128]{4,3,2,1,0:T(8,128)(2,1)S(1)}, bf16[32,2,2,64,128]{4,3,2,1,0:T(8,128)(2,1)}, u32[]{:S(2)}) copy-start(bf16[32,2,2,64,128]{4,3,2,1,0:T(8,128)(2,1)} %shard_map.46) | copy-start | bytes 6291460
  134.7 53.3 %copy-start.1 = (bf16[32,2,2,64,128]{4,3,2,1,0:T(8,128)(2,1)S(1)}, bf16[32,2,2,64,128]{4,3,2,1,0:T(8,128)(2,1)}, u32[]{:S(2)}) copy-start(bf16[32,2,2,64,128]{4,3,2,1,0:T(8,128)(2,1)} %shard_map.47) | copy-start | bytes 6291460
  134.7 53.3 %collective-permute-start = (bf16[32,64,128]{2,1,0:T(8,128)(2,1)S(1)}, bf16[32,64,128]{2,1,0:T(8,128)(2,1)S(1)}, u32[]{:S(2)}, u32[]{:S(2)}) collective-permute-start(bf16[32,64,128]{2,1,0:T(8,128)(2,1)S(1)} %slice_bitcast_fusion), channel_id=1, source_target_pairs={{0,4},{4,8},{8,12},{12,16},{16,20},{20,24},{24,28},{28,32},{32,36}... | collective-permute-start | bytes 1572872 | tf_op jit(solution)/shard_map/ppermute | solution.py:15

commit v10 on v9

--- a/solution.py
+++ b/solution.py
@@ -80,9 +80,6 @@
         for quarter in range(4):
             out_ref[(a % half_axis) * 4 + quarter, 0, a // half_axis] = value[quarter * rows:(quarter + 1) * rows]
 
-    def magnitude(c):
-        return jnp.sqrt(c * c + pltpu.roll(c, half, 1) ** 2)
-
     def init_group(i, carry):
         a0 = group * i
         initial = []
@@ -102,20 +99,28 @@
 
     def init_hi(i, running):
         for coeffs in coeff_group(i):
-            running = jnp.maximum(running, jnp.max(magnitude(coeffs), axis=0, keepdims=True))
+            square = coeffs * coeffs
+            running = jnp.maximum(running, jnp.max(square + pltpu.roll(square, half, 1), axis=0, keepdims=True))
         return running
 
-    largest = lax.fori_loop(0, groups, init_hi, jnp.zeros((1, lanes), jnp.float32), unroll=groups)
+    largest = jnp.sqrt(lax.fori_loop(0, groups, init_hi, jnp.zeros((1, lanes), jnp.float32), unroll=groups))
 
     def sweep_step(k, carry):
         cutoff = largest * scales_ref[k]
 
         def thin_group(i, c2):
             thinned = []
-            for coeffs in coeff_group(i):
-                size_now = magnitude(coeffs)
+            blocks = coeff_group(i)
+            for b in range(0, len(blocks), 2):
+                first, second = blocks[b], blocks[b + 1]
+                sq0 = first * first
+                sq1 = second * second
+                packed = jnp.where(lower, sq0 + pltpu.roll(sq0, half, 1), sq1 + pltpu.roll(sq1, half, 1))
+                size_now = jnp.sqrt(packed)
                 factor = jnp.maximum(size_now - cutoff, 0.0) / (jnp.maximum(size_now, cutoff) + 1e-06)
-                thinned.append((coeffs * factor).astype(jnp.bfloat16))
+                swapped = pltpu.roll(factor, half, 1)
+                thinned.append((first * jnp.where(lower, factor, swapped)).astype(jnp.bfloat16))
+                thinned.append((second * jnp.where(lower, swapped, factor)).astype(jnp.bfloat16))
             hi0 = group * i
             for g, back_mid in enumerate(apply(3, thinned)):
                 back_mid = back_mid.astype(jnp.bfloat16)

time: 222 us -> 215 us (0.968)
  Pallas kernels: 53.2 us -> 49.1 us
  waiting for transfers between devices: 75 us -> 71.4 us
    pallas_call x2, Pallas kernels: 53.2 us -> 49.1 us  [run_patches(): pl.pallas_call(pocs_kernel, grid_spec=grid_spec, out_shape=jax.ShapeDtype...]
    ppermute x1, waiting for transfers between devices: 51.1 us -> 47.5 us  [passed_along(): return lax.ppermute(block, axis, route)]
where the time goes in v10:
time: 215 us; the launch traced here: 214 us
  waiting for transfers between devices  71.4 us (33%)
  blocking collectives  68.8 us (32%)
  Pallas kernels  49.1 us (23%)
  local copies, waits for them, and re-layouts  15.3 us (7%)
  starting transfers between devices  6.25 us (3%)
  other arithmetic  3.19 us (1%)
    pallas_call x2, Pallas kernels, run_patches(): pl.pallas_call(pocs_kernel, grid_spec=grid_spec, out_shape=jax.ShapeDtype...  49.1 us
    ppermute x1, waiting for transfers between devices, passed_along(): return lax.ppermute(block, axis, route)  47.5 us
    all_to_all x1, blocking collectives, shards(): lax.all_to_all(part, 'shot', split_axis=1, concat_axis=2, tiled=True)  37.6 us
    all_to_all x1, blocking collectives, shards(): lax.all_to_all(mixed, 'shot', split_axis=0, concat_axis=1, tiled=True)  31.2 us
    all_to_all x1, waiting for transfers between devices, shards(): lax.all_to_all(part, 'shot', split_axis=1, concat_axis=2, tiled=True)  23.9 us
    all_to_all x2, local copies, waits for them, and re-layouts, shards(): lax.all_to_all(part, 'shot', split_axis=1, concat_axis=2, tiled=True)  4.63 us
    broadcast_in_dim x2, local copies, waits for them, and re-layouts, shards(): maskb = jnp.broadcast_to(recorded[..., None], observed.shape)  4.38 us
  transfers between devices with their start and end apart: 2, of which 2 were waited for; matrix products, arithmetic and copies ran while one was open for 2% of the time, Pallas kernels for 0%

profile of v10, /device:TPU:1, one launch (start us, length us, event | category | flops | bytes accessed | tf_op | source)
XLA Modules:
  0.0 214.1 jit_solution(1808821217348950976)
XLA Ops:
  0.0 4.1 %fusion.12 = (bf16[1,32,2,128,128]{4,3,2,1,0:T(8,128)(2,1)}, bf16[1,32,2,128,128]{4,3,2,1,0:T(8,128)(2,1)S(1)}) fusion(bf16[1,32,4,128,128]{4,3,2,1,0:T(8,128)(2,1)} %bitcast.41), kind=kLoop, calls=%fused_computation.27 | loop fusion | bytes 8388608 | tf_op jit(solution)/shard_map/slice | solution.py:193
  4.1 37.6 %all_to_all.42 = bf16[1,64,128,128]{3,2,0,1:T(8,128)(2,1)} all-to-all(bf16[1,64,128,128]{3,2,0,1:T(8,128)(2,1)S(1)} %bitcast.40), channel_id=1, replica_groups=mesh['shot'=32,'az'=4] {'shot'}, dimensions={1} | all-to-all | bytes 4194304 | tf_op jit(solution)/shard_map/all_to_all | solution.py:194
  41.7 4.2 %all-to-all-start.1 = ((bf16[1,64,128,128]{3,2,0,1:T(8,128)(2,1)}), bf16[1,64,128,128]{3,2,0,1:T(8,128)(2,1)S(1)}, u32[]{:S(2)}, u32[]{:S(2)}) async-start(bf16[1,64,128,128]{3,2,0,1:T(8,128)(2,1)} %bitcast.37), calls=%async_computation.1 | async-start | bytes 4194304 | tf_op jit(solution)/shard_map/all_to_all | solution.py:194
  45.9 0.5 power_multiply_fusion.scales_ref
  46.4 0.0 copy-done.3
  46.4 0.7 slice_bitcast_fusion.1
  47.1 0.0 copy-done.2
  47.1 3.2 %copy.11 = bf16[1,2,32,128,128]{4,3,2,1,0:T(8,128)(2,1)} copy(bf16[1,2,32,128,128]{4,3,1,2,0:T(8,128)(2,1)} %bitcast.35) | data formatting | bytes 4194304 | tf_op jit(solution)/shard_map/all_to_all | solution.py:194
  50.3 23.9 %all-to-all-done.1 = bf16[1,64,128,128]{3,2,0,1:T(8,128)(2,1)S(1)} async-done(((bf16[1,64,128,128]{3,2,0,1:T(8,128)(2,1)}), bf16[1,64,128,128]{3,2,0,1:T(8,128)(2,1)S(1)}, u32[]{:S(2)}, u32[]{:S(2)}) %all-to-all-start.1) | async-done | bytes 2097184 | tf_op jit(solution)/shard_map/all_to_all | solution.py:194
  74.2 1.5 copy.12
  75.7 2.2 %broadcast_in_dim.6.mask_ref = bf16[2,16,256,128]{3,2,1,0:T(8,128)(2,1)} broadcast(bf16[2,16,256]{2,1,0:T(8,128)(2,1)S(1)} %get-tuple-element.8), dimensions={0,1,2} | broadcast | bytes 2113536 | tf_op jit(solution)/shard_map/broadcast_in_dim | solution.py:197
  77.8 15.9 %shard_map.46 = bf16[32,2,2,64,128]{4,3,2,1,0:T(8,128)(2,1)} custom-call(s32[2]{0:T(128)} %get-tuple-element.10.counts_ref, f32[8]{0:T(128)} %power_multiply_fusion.scales_ref, bf16[2,16,256,128]{3,2,1,0:T(8,128)(2,1)} %bitcast.39, bf16[2,16,256,128]{3,2,1,0:T(8,128)(2,1)} %broadcast_in_dim.6.mask_ref, bf16[4,256,512]{2,1,0:T(8,128)(2,1)} %constant.33.clone.tab_ref), custom_call_target="tpu_custom_call" | custom-call | tf_op jit(solution)/shard_map/pallas_call | solution.py:170
  93.7 2.2 %broadcast_in_dim.7.mask_ref = bf16[2,16,256,128]{3,2,1,0:T(8,128)(2,1)} broadcast(bf16[2,16,256]{2,1,0:T(8,128)(2,1)S(1)} %get-tuple-element.7), dimensions={0,1,2} | broadcast | bytes 2113536 | tf_op jit(solution)/shard_map/broadcast_in_dim | solution.py:197
  95.9 33.2 %shard_map.47 = bf16[32,2,2,64,128]{4,3,2,1,0:T(8,128)(2,1)} custom-call(s32[2]{0:T(128)} %get-tuple-element.9.counts_ref, f32[8]{0:T(128)} %power_multiply_fusion.scales_ref, bf16[2,16,256,128]{3,2,1,0:T(8,128)(2,1)} %bitcast.38, bf16[2,16,256,128]{3,2,1,0:T(8,128)(2,1)} %broadcast_in_dim.7.mask_ref, bf16[4,256,512]{2,1,0:T(8,128)(2,1)} %constant.33.clone.tab_ref), custom_call_target="tpu_custom_call" | custom-call | tf_op jit(solution)/shard_map/pallas_call | solution.py:170
  129.1 0.0 copy-done
  129.1 1.4 fusion.4
  130.6 0.0 copy-start.1
  130.6 2.1 collective-permute-start
  132.7 0.2 slice.45
  132.9 47.5 %collective-permute-done = bf16[32,64,128]{2,1,0:T(8,128)(2,1)S(1)} collective-permute-done((bf16[32,64,128]{2,1,0:T(8,128)(2,1)S(1)}, bf16[32,64,128]{2,1,0:T(8,128)(2,1)S(1)}, u32[]{:S(2)}, u32[]{:S(2)}) %collective-permute-start) | collective-permute-done | bytes 524320 | tf_op jit(solution)/shard_map/ppermute | solution.py:15
  180.3 0.0 copy-done.1
  180.3 1.2 fusion.1
  181.6 31.2 %all_to_all.43 = bf16[32,4,64,128]{3,2,1,0:T(8,128)(2,1)S(1)} all-to-all(bf16[32,4,64,128]{3,2,1,0:T(8,128)(2,1)S(1)} %fusion.1), channel_id=1, replica_groups=mesh['shot'=32,'az'=4] {'shot'}, dimensions={0} | all-to-all | bytes 4194304 | tf_op jit(solution)/shard_map/all_to_all | solution.py:208
  212.8 1.3 copy.18
  (6 shorter events, 0.1 us)
Async XLA Ops:
  41.7 4.7 %copy-start.3 = (s32[1,4]{1,0:T(1,128)S(1)}, s32[1,4]{1,0:T(1,128)}, u32[]{:S(2)}) copy-start(s32[1,4]{1,0:T(1,128)} %param.6) | copy-start | bytes 52
  41.7 5.4 %copy-start.2 = (s32[1,4,16,256]{3,2,1,0:T(8,128)S(1)}, s32[1,4,16,256]{3,2,1,0:T(8,128)}, u32[]{:S(2)}) copy-start(s32[1,4,16,256]{3,2,1,0:T(8,128)} %param.5) | copy-start | bytes 196612
  41.7 32.5 %all-to-all-start.1 = ((bf16[1,64,128,128]{3,2,0,1:T(8,128)(2,1)}), bf16[1,64,128,128]{3,2,0,1:T(8,128)(2,1)S(1)}, u32[]{:S(2)}, u32[]{:S(2)}) async-start(bf16[1,64,128,128]{3,2,0,1:T(8,128)(2,1)} %bitcast.37), calls=%async_computation.1 | async-start | bytes 4194304 | tf_op jit(solution)/shard_map/all_to_all | solution.py:194
  95.9 33.2 %copy-start = (bf16[32,2,2,64,128]{4,3,2,1,0:T(8,128)(2,1)S(1)}, bf16[32,2,2,64,128]{4,3,2,1,0:T(8,128)(2,1)}, u32[]{:S(2)}) copy-start(bf16[32,2,2,64,128]{4,3,2,1,0:T(8,128)(2,1)} %shard_map.46) | copy-start | bytes 6291460
  130.6 49.8 %copy-start.1 = (bf16[32,2,2,64,128]{4,3,2,1,0:T(8,128)(2,1)S(1)}, bf16[32,2,2,64,128]{4,3,2,1,0:T(8,128)(2,1)}, u32[]{:S(2)}) copy-start(bf16[32,2,2,64,128]{4,3,2,1,0:T(8,128)(2,1)} %shard_map.47) | copy-start | bytes 6291460
  130.6 49.7 %collective-permute-start = (bf16[32,64,128]{2,1,0:T(8,128)(2,1)S(1)}, bf16[32,64,128]{2,1,0:T(8,128)(2,1)S(1)}, u32[]{:S(2)}, u32[]{:S(2)}) collective-permute-start(bf16[32,64,128]{2,1,0:T(8,128)(2,1)S(1)} %slice_bitcast_fusion), channel_id=1, source_target_pairs={{0,4},{4,8},{8,12},{12,16},{16,20},{20,24},{24,28},{28,32},{32,36}... | collective-permute-start | bytes 1572872 | tf_op jit(solution)/shard_map/ppermute | solution.py:15

commit v11 on v10

--- a/solution.py
+++ b/solution.py
@@ -43,7 +43,7 @@
 GROUP = 16
 
 
-def pocs_kernel(counts_ref, scales_ref, obs_ref, mask_ref, tab_ref, out_ref, y_ref, v_ref):
+def pocs_kernel(counts_ref, scales_ref, obs_ref, mask_ref, tab_ref, out_ref, y_ref, v_ref, m_ref):
     p = pl.program_id(0)
     extent = obs_ref.shape[1]
     lanes = obs_ref.shape[3]
@@ -55,6 +55,12 @@
     groups = extent // group
     sweeps = counts_ref[p]
     lower = lax.broadcasted_iota(jnp.int32, (1, lanes), 1) < half
+    columns = jnp.transpose(mask_ref[0].astype(jnp.float32))
+    for a in range(extent):
+        m_ref[a] = jnp.broadcast_to(columns[:, a:a + 1], (plane, lanes)).astype(jnp.bfloat16)
+
+    def sampled(a):
+        return m_ref[a] > 0
 
     def rot(block):
         rolled = pltpu.roll(block, half, 1)
@@ -85,13 +91,14 @@
         initial = []
         for g in range(group):
             observed = obs_ref[0, a0 + g]
-            value = jnp.where(mask_ref[0, a0 + g] > 0, observed, jnp.zeros_like(observed))
+            value = jnp.where(sampled(a0 + g), observed, jnp.zeros_like(observed))
             write_out(a0 + g, value)
             initial.append(value)
         stage_one(a0, initial)
         return carry
 
-    lax.fori_loop(0, groups, init_group, 0, unroll=groups)
+    for i in range(groups):
+        init_group(i, 0)
 
     def coeff_group(i):
         hi0 = group * i
@@ -103,7 +110,10 @@
             running = jnp.maximum(running, jnp.max(square + pltpu.roll(square, half, 1), axis=0, keepdims=True))
         return running
 
-    largest = jnp.sqrt(lax.fori_loop(0, groups, init_hi, jnp.zeros((1, lanes), jnp.float32), unroll=groups))
+    running = jnp.zeros((1, lanes), jnp.float32)
+    for i in range(groups):
+        running = init_hi(i, running)
+    largest = jnp.sqrt(running)
 
     def sweep_step(k, carry):
         cutoff = largest * scales_ref[k]
@@ -128,7 +138,8 @@
                     v_ref[a, hi0 + g] = back_mid[a * extent:(a + 1) * extent]
             return c2
 
-        lax.fori_loop(0, groups, thin_group, 0, unroll=groups)
+        for i in range(groups):
+            thin_group(i, 0)
 
         def back_group(i, c2):
             a0 = group * i
@@ -136,7 +147,7 @@
             updated = []
             for g in range(group):
                 observed = obs_ref[0, a0 + g].astype(jnp.float32)
-                value = jnp.where(mask_ref[0, a0 + g] > 0, observed, returned[g]).astype(jnp.bfloat16)
+                value = jnp.where(sampled(a0 + g), observed, returned[g]).astype(jnp.bfloat16)
                 write_out(a0 + g, value)
                 updated.append(value)
 
@@ -146,7 +157,8 @@
 
             return c2
 
-        lax.fori_loop(0, groups, back_group, 0, unroll=groups)
+        for i in range(groups):
+            back_group(i, 0)
         return carry
 
     lax.fori_loop(0, sweeps, sweep_step, 0)
@@ -160,11 +172,12 @@
     grid_spec = pltpu.PrefetchScalarGridSpec(
         num_scalar_prefetch=2,
         grid=(count,),
-        in_specs=[block, block, pl.BlockSpec(tables.shape, lambda p, c, s: (0, 0, 0))],
+        in_specs=[block, pl.BlockSpec((1, extent, plane), lambda p, c, s: (p, 0, 0)), pl.BlockSpec(tables.shape, lambda p, c, s: (0, 0, 0))],
         out_specs=out_block,
         scratch_shapes=[
             pltpu.VMEM((extent, extent, extent, lanes), jnp.bfloat16),
             pltpu.VMEM((extent, extent, extent, lanes), jnp.bfloat16),
+            pltpu.VMEM((extent, plane, lanes), jnp.bfloat16),
         ],
     )
     return pl.pallas_call(
@@ -193,8 +206,7 @@
         part = by_owner[:, :, first:first + chunk].reshape((1, devices * chunk) + spectra.shape[2:])
         regrouped = lax.all_to_all(part, "shot", split_axis=1, concat_axis=2, tiled=True)
         observed = regrouped.reshape(chunk, extent, plane, lane_count)
-        recorded = (sampled_mask[0, first:first + chunk] > 0).astype(jnp.bfloat16)
-        maskb = jnp.broadcast_to(recorded[..., None], observed.shape)
+        maskb = sampled_mask[0, first:first + chunk]
         pieces.append(run_patches(observed, maskb, counts[0, first:first + chunk], scales, tables))
     result = jnp.concatenate(pieces, axis=1)
     dests = result.shape[0]

time: 215 us -> 211 us (0.981)
  local copies, waits for them, and re-layouts: 15.3 us -> 11.5 us
    broadcast_in_dim x2 -> x0, local copies, waits for them, and re-layouts: 4.38 us -> none  [shards(): maskb = jnp.broadcast_to(recorded[..., None], observed.shape)]
where the time goes in v11:
time: 211 us; the launch traced here: 210 us
  waiting for transfers between devices  70.8 us (34%)
  blocking collectives  68.8 us (33%)
  Pallas kernels  49.8 us (24%)
  local copies, waits for them, and re-layouts  11.5 us (5%)
  starting transfers between devices  6.25 us (3%)
  other arithmetic  3.14 us (1%)
    pallas_call x2, Pallas kernels, run_patches(): pl.pallas_call(pocs_kernel, grid_spec=grid_spec, out_shape=jax.ShapeDtype...  49.8 us
    ppermute x1, waiting for transfers between devices, passed_along(): return lax.ppermute(block, axis, route)  47.4 us
    all_to_all x1, blocking collectives, shards(): lax.all_to_all(part, 'shot', split_axis=1, concat_axis=2, tiled=True)  37.6 us
    all_to_all x1, blocking collectives, shards(): lax.all_to_all(mixed, 'shot', split_axis=0, concat_axis=1, tiled=True)  31.2 us
    all_to_all x1, waiting for transfers between devices, shards(): lax.all_to_all(part, 'shot', split_axis=1, concat_axis=2, tiled=True)  23.4 us
    all_to_all x2, local copies, waits for them, and re-layouts, shards(): lax.all_to_all(part, 'shot', split_axis=1, concat_axis=2, tiled=True)  4.63 us
  transfers between devices with their start and end apart: 2, of which 2 were waited for; matrix products, arithmetic and copies ran while one was open for 2% of the time, Pallas kernels for 0%

profile of v11, /device:TPU:1, one launch (start us, length us, event | category | flops | bytes accessed | tf_op | source)
XLA Modules:
  0.0 210.3 jit_solution(2424772757110479553)
XLA Ops:
  0.0 4.1 %fusion.8 = (bf16[1,32,2,128,128]{4,3,2,1,0:T(8,128)(2,1)}, bf16[1,32,2,128,128]{4,3,2,1,0:T(8,128)(2,1)S(1)}) fusion(bf16[1,32,4,128,128]{4,3,2,1,0:T(8,128)(2,1)} %bitcast.41), kind=kLoop, calls=%fused_computation.23 | loop fusion | bytes 8388608 | tf_op jit(solution)/shard_map/slice | solution.py:206
  4.1 37.6 %all_to_all.42 = bf16[1,64,128,128]{3,2,0,1:T(8,128)(2,1)} all-to-all(bf16[1,64,128,128]{3,2,0,1:T(8,128)(2,1)S(1)} %bitcast.40), channel_id=1, replica_groups=mesh['shot'=32,'az'=4] {'shot'}, dimensions={1} | all-to-all | bytes 4194304 | tf_op jit(solution)/shard_map/all_to_all | solution.py:207
  41.7 0.0 copy-start.3
  41.7 4.2 %all-to-all-start.1 = ((bf16[1,64,128,128]{3,2,0,1:T(8,128)(2,1)}), bf16[1,64,128,128]{3,2,0,1:T(8,128)(2,1)S(1)}, u32[]{:S(2)}, u32[]{:S(2)}) async-start(bf16[1,64,128,128]{3,2,0,1:T(8,128)(2,1)} %bitcast.39), calls=%async_computation.1 | async-start | bytes 4194304 | tf_op jit(solution)/shard_map/all_to_all | solution.py:207
  45.9 0.5 power_multiply_fusion.scales_ref
  46.4 0.0 copy-done.3
  46.4 0.6 slice_bitcast_fusion.3
  47.0 0.0 copy-done.2
  47.0 0.6 slice_bitcast_fusion.1
  47.6 3.2 %copy.11 = bf16[1,2,32,128,128]{4,3,2,1,0:T(8,128)(2,1)} copy(bf16[1,2,32,128,128]{4,3,1,2,0:T(8,128)(2,1)} %bitcast.35) | data formatting | bytes 4194304 | tf_op jit(solution)/shard_map/all_to_all | solution.py:207
  50.8 23.4 %all-to-all-done.1 = bf16[1,64,128,128]{3,2,0,1:T(8,128)(2,1)S(1)} async-done(((bf16[1,64,128,128]{3,2,0,1:T(8,128)(2,1)}), bf16[1,64,128,128]{3,2,0,1:T(8,128)(2,1)S(1)}, u32[]{:S(2)}, u32[]{:S(2)}) %all-to-all-start.1) | async-done | bytes 2097184 | tf_op jit(solution)/shard_map/all_to_all | solution.py:207
  74.2 1.5 copy.12
  75.7 16.2 %shard_map.46 = bf16[32,2,2,64,128]{4,3,2,1,0:T(8,128)(2,1)} custom-call(s32[2]{0:T(128)} %get-tuple-element.10.counts_ref, f32[8]{0:T(128)} %power_multiply_fusion.scales_ref, bf16[2,16,256,128]{3,2,1,0:T(8,128)(2,1)} %bitcast.37, s32[2,16,256]{2,1,0:T(8,128)} %get-tuple-element.8.mask_ref, bf16[4,256,512]{2,1,0:T(8,128)(2,1)} %constant.32.clone.tab_ref), custom_call_target="tpu_custom_call" | custom-call | tf_op jit(solution)/shard_map/pallas_call | solution.py:183
  91.9 33.6 %shard_map.47 = bf16[32,2,2,64,128]{4,3,2,1,0:T(8,128)(2,1)} custom-call(s32[2]{0:T(128)} %get-tuple-element.9.counts_ref, f32[8]{0:T(128)} %power_multiply_fusion.scales_ref, bf16[2,16,256,128]{3,2,1,0:T(8,128)(2,1)} %bitcast.36, s32[2,16,256]{2,1,0:T(8,128)} %get-tuple-element.7.mask_ref, bf16[4,256,512]{2,1,0:T(8,128)(2,1)} %constant.32.clone.tab_ref), custom_call_target="tpu_custom_call" | custom-call | tf_op jit(solution)/shard_map/pallas_call | solution.py:183
  125.5 0.0 copy-done
  125.5 1.4 fusion.4
  126.9 0.0 copy-start.1
  127.0 2.1 collective-permute-start
  129.0 0.2 slice.45
  129.2 47.4 %collective-permute-done = bf16[32,64,128]{2,1,0:T(8,128)(2,1)S(1)} collective-permute-done((bf16[32,64,128]{2,1,0:T(8,128)(2,1)S(1)}, bf16[32,64,128]{2,1,0:T(8,128)(2,1)S(1)}, u32[]{:S(2)}, u32[]{:S(2)}) %collective-permute-start) | collective-permute-done | bytes 524320 | tf_op jit(solution)/shard_map/ppermute | solution.py:15
  176.6 0.0 copy-done.1
  176.6 1.2 fusion.1
  177.8 31.2 %all_to_all.43 = bf16[32,4,64,128]{3,2,1,0:T(8,128)(2,1)S(1)} all-to-all(bf16[32,4,64,128]{3,2,1,0:T(8,128)(2,1)S(1)} %fusion.1), channel_id=1, replica_groups=mesh['shot'=32,'az'=4] {'shot'}, dimensions={0} | all-to-all | bytes 4194304 | tf_op jit(solution)/shard_map/all_to_all | solution.py:220
  209.0 1.3 copy.18
  (4 shorter events, 0.1 us)
Async XLA Ops:
  41.7 4.7 %copy-start.3 = (s32[1,4]{1,0:T(1,128)S(1)}, s32[1,4]{1,0:T(1,128)}, u32[]{:S(2)}) copy-start(s32[1,4]{1,0:T(1,128)} %param.6) | copy-start | bytes 52
  41.7 5.3 %copy-start.2 = (s32[1,4,16,256]{3,2,1,0:T(8,128)S(1)}, s32[1,4,16,256]{3,2,1,0:T(8,128)}, u32[]{:S(2)}) copy-start(s32[1,4,16,256]{3,2,1,0:T(8,128)} %param.5) | copy-start | bytes 196612
  41.7 32.5 %all-to-all-start.1 = ((bf16[1,64,128,128]{3,2,0,1:T(8,128)(2,1)}), bf16[1,64,128,128]{3,2,0,1:T(8,128)(2,1)S(1)}, u32[]{:S(2)}, u32[]{:S(2)}) async-start(bf16[1,64,128,128]{3,2,0,1:T(8,128)(2,1)} %bitcast.39), calls=%async_computation.1 | async-start | bytes 4194304 | tf_op jit(solution)/shard_map/all_to_all | solution.py:207
  91.9 33.6 %copy-start = (bf16[32,2,2,64,128]{4,3,2,1,0:T(8,128)(2,1)S(1)}, bf16[32,2,2,64,128]{4,3,2,1,0:T(8,128)(2,1)}, u32[]{:S(2)}) copy-start(bf16[32,2,2,64,128]{4,3,2,1,0:T(8,128)(2,1)} %shard_map.46) | copy-start | bytes 6291460
  126.9 49.7 %copy-start.1 = (bf16[32,2,2,64,128]{4,3,2,1,0:T(8,128)(2,1)S(1)}, bf16[32,2,2,64,128]{4,3,2,1,0:T(8,128)(2,1)}, u32[]{:S(2)}) copy-start(bf16[32,2,2,64,128]{4,3,2,1,0:T(8,128)(2,1)} %shard_map.47) | copy-start | bytes 6291460
  127.0 49.6 %collective-permute-start = (bf16[32,64,128]{2,1,0:T(8,128)(2,1)S(1)}, bf16[32,64,128]{2,1,0:T(8,128)(2,1)S(1)}, u32[]{:S(2)}, u32[]{:S(2)}) collective-permute-start(bf16[32,64,128]{2,1,0:T(8,128)(2,1)S(1)} %slice_bitcast_fusion), channel_id=1, source_target_pairs={{0,4},{4,8},{8,12},{12,16},{16,20},{20,24},{24,28},{28,32},{32,36}... | collective-permute-start | bytes 1572872 | tf_op jit(solution)/shard_map/ppermute | solution.py:15

commit v12 on v10

--- a/solution.py
+++ b/solution.py
@@ -45,10 +45,15 @@
 
 def pocs_kernel(counts_ref, scales_ref, obs_ref, mask_ref, tab_ref, out_ref, y_ref, v_ref):
     p = pl.program_id(0)
-    extent = obs_ref.shape[1]
-    lanes = obs_ref.shape[3]
+    extent = mask_ref.shape[1]
+    lanes = mask_ref.shape[3]
     half = lanes // 2
-    plane = obs_ref.shape[2]
+    plane = mask_ref.shape[2]
+    sources = obs_ref.shape[0] // extent
+
+    def obs(a):
+        return obs_ref[pl.ds(a * sources, sources), 0].reshape(plane, lanes)
+
     half_axis = extent // 2
     rows = plane // 4
     group = GROUP
@@ -84,7 +89,7 @@
         a0 = group * i
         initial = []
         for g in range(group):
-            observed = obs_ref[0, a0 + g]
+            observed = obs(a0 + g)
             value = jnp.where(mask_ref[0, a0 + g] > 0, observed, jnp.zeros_like(observed))
             write_out(a0 + g, value)
             initial.append(value)
@@ -135,7 +140,7 @@
             returned = apply(1, [v_ref[a0 + g].reshape(plane, lanes) for g in range(group)])
             updated = []
             for g in range(group):
-                observed = obs_ref[0, a0 + g].astype(jnp.float32)
+                observed = obs(a0 + g).astype(jnp.float32)
                 value = jnp.where(mask_ref[0, a0 + g] > 0, observed, returned[g]).astype(jnp.bfloat16)
                 write_out(a0 + g, value)
                 updated.append(value)
@@ -153,14 +158,16 @@
 
 
 def run_patches(observed, maskb, sweeps, scales, tables):
-    count, extent, plane, lanes = observed.shape
+    count, extent, plane, lanes = maskb.shape
     block = pl.BlockSpec((1, extent, plane, lanes), lambda p, c, s: (p, 0, 0, 0))
+    sources = observed.shape[0]
+    obs_block = pl.BlockSpec((sources, 1) + observed.shape[2:], lambda p, c, s: (0, p, 0, 0))
     dests = extent // 2 * 4
     out_block = pl.BlockSpec((dests, 1, 2, plane // 4, lanes), lambda p, c, s: (0, p, 0, 0, 0))
     grid_spec = pltpu.PrefetchScalarGridSpec(
         num_scalar_prefetch=2,
         grid=(count,),
-        in_specs=[block, block, pl.BlockSpec(tables.shape, lambda p, c, s: (0, 0, 0))],
+        in_specs=[obs_block, block, pl.BlockSpec(tables.shape, lambda p, c, s: (0, 0, 0))],
         out_specs=out_block,
         scratch_shapes=[
             pltpu.VMEM((extent, extent, extent, lanes), jnp.bfloat16),
@@ -190,11 +197,10 @@
 
     pieces = []
     for first in range(0, owned_count, chunk):
-        part = by_owner[:, :, first:first + chunk].reshape((1, devices * chunk) + spectra.shape[2:])
-        regrouped = lax.all_to_all(part, "shot", split_axis=1, concat_axis=2, tiled=True)
-        observed = regrouped.reshape(chunk, extent, plane, lane_count)
+        part = by_owner[:, :, first:first + chunk]
+        observed = lax.all_to_all(part, "shot", split_axis=1, concat_axis=1, tiled=True)[0]
         recorded = (sampled_mask[0, first:first + chunk] > 0).astype(jnp.bfloat16)
-        maskb = jnp.broadcast_to(recorded[..., None], observed.shape)
+        maskb = jnp.broadcast_to(recorded[..., None], (chunk, extent, plane, lane_count))
         pieces.append(run_patches(observed, maskb, counts[0, first:first + chunk], scales, tables))
     result = jnp.concatenate(pieces, axis=1)
     dests = result.shape[0]

time: 215 us -> 184 us (0.86)
  waiting for transfers between devices: 71.4 us -> 45.7 us
  local copies, waits for them, and re-layouts: 15.3 us -> 10.7 us
    all_to_all x1, waiting for transfers between devices: 23.9 us -> 8.95 us  [shards(): lax.all_to_all(part, 'shot', split_axis=1, concat_axis=1, tiled=True)[0]]
    ppermute x1, waiting for transfers between devices: 47.5 us -> 36.8 us  [passed_along(): return lax.ppermute(block, axis, route)]
    all_to_all x2 -> x0, local copies, waits for them, and re-layouts: 4.63 us -> none  [shards(): lax.all_to_all(part, 'shot', split_axis=1, concat_axis=2, tiled=True)]
  transfers between devices with their start and end apart: 2 -> 2, of which waited for: 2 -> 2; matrix products, arithmetic and copies ran while one was open for 2% -> 2% of each run, Pallas kernels for 0% -> 9%
where the time goes in v12:
time: 184 us
  blocking collectives  68.8 us (37%)
  Pallas kernels  49.1 us (27%)
  waiting for transfers between devices  45.7 us (25%)
  local copies, waits for them, and re-layouts  10.7 us (6%)
  starting transfers between devices  6.25 us (3%)
  other arithmetic  3.24 us (2%)
    pallas_call x2, Pallas kernels, run_patches(): pl.pallas_call(pocs_kernel, grid_spec=grid_spec, out_shape=jax.ShapeDtype...  49.1 us
    all_to_all x1, blocking collectives, shards(): lax.all_to_all(part, 'shot', split_axis=1, concat_axis=1, tiled=True)[0]  37.6 us
    ppermute x1, waiting for transfers between devices, passed_along(): return lax.ppermute(block, axis, route)  36.8 us
    all_to_all x1, blocking collectives, shards(): lax.all_to_all(mixed, 'shot', split_axis=0, concat_axis=1, tiled=True)  31.2 us
    all_to_all x1, waiting for transfers between devices, shards(): lax.all_to_all(part, 'shot', split_axis=1, concat_axis=1, tiled=True)[0]  8.95 us
    broadcast_in_dim x2, local copies, waits for them, and re-layouts, shards(): jnp.broadcast_to(recorded[..., None], (chunk, extent, plane, lane_count))  4.45 us
    all_to_all x1, starting transfers between devices, shards(): lax.all_to_all(part, 'shot', split_axis=1, concat_axis=1, tiled=True)[0]  4.19 us
    slice x1, local copies, waits for them, and re-layouts, shards(): part = by_owner[:, :, first:first + chunk]  4.08 us
  transfers between devices with their start and end apart: 2, of which 2 were waited for; matrix products, arithmetic and copies ran while one was open for 2% of the time, Pallas kernels for 9%

profile of v12, /device:TPU:1, one launch (start us, length us, event | category | flops | bytes accessed | tf_op | source)
XLA Modules:
  0.0 183.9 jit_solution(7639949451506497403)
XLA Ops:
  0.0 4.1 %fusion.12 = (bf16[1,32,2,128,128]{4,3,2,0,1:T(8,128)(2,1)}, bf16[1,32,2,128,128]{4,3,2,0,1:T(8,128)(2,1)S(1)}) fusion(bf16[1,32,4,128,128]{4,3,2,0,1:T(8,128)(2,1)} %bitcast.29), kind=kLoop, calls=%fused_computation.27 | loop fusion | bytes 8388608 | tf_op jit(solution)/shard_map/slice | solution.py:200
  4.1 37.6 %all_to_all.22 = bf16[1,32,2,128,128]{4,3,2,0,1:T(8,128)(2,1)} all-to-all(bf16[1,32,2,128,128]{4,3,2,0,1:T(8,128)(2,1)S(1)} %get-tuple-element.6), channel_id=1, replica_groups=mesh['shot'=32,'az'=4] {'shot'}, dimensions={1} | all-to-all | bytes 4194304 | tf_op jit(solution)/shard_map/all_to_all | solution.py:201
  41.7 0.0 copy-start.4
  41.7 4.2 %all-to-all-start.1 = ((bf16[1,32,2,128,128]{4,3,2,0,1:T(8,128)(2,1)}), bf16[1,32,2,128,128]{4,3,2,0,1:T(8,128)(2,1)S(1)}, u32[]{:S(2)}, u32[]{:S(2)}) async-start(bf16[1,32,2,128,128]{4,3,2,0,1:T(8,128)(2,1)} %get-tuple-element.5), calls=%async_computation.1 | async-start | bytes 4194304 | tf_op jit(solution)/shard_map/all_to_all | solution.py:201
  45.9 0.6 power_multiply_fusion.scales_ref
  46.5 0.0 copy-done.4
  46.5 0.6 slice_bitcast_fusion.1
  47.1 0.0 copy-done.3
  47.1 2.2 %broadcast_in_dim.6.mask_ref = bf16[2,16,256,128]{3,2,1,0:T(8,128)(2,1)} broadcast(bf16[2,16,256]{2,1,0:T(8,128)(2,1)S(1)} %get-tuple-element.8), dimensions={0,1,2} | broadcast | bytes 2113536 | tf_op jit(solution)/shard_map/broadcast_in_dim | solution.py:203
  49.4 15.9 %shard_map.46 = bf16[32,2,2,64,128]{4,3,2,1,0:T(8,128)(2,1)} custom-call(s32[2]{0:T(128)} %get-tuple-element.10.counts_ref, f32[8]{0:T(128)} %power_multiply_fusion.scales_ref, bf16[32,2,128,128]{3,2,1,0:T(8,128)(2,1)} %bitcast.28, bf16[2,16,256,128]{3,2,1,0:T(8,128)(2,1)} %broadcast_in_dim.6.mask_ref, bf16[4,256,512]{2,1,0:T(8,128)(2,1)} %constant.33.clone.tab_ref), custom_call_target="tpu_custom_call" | custom-call | tf_op jit(solution)/shard_map/pallas_call | solution.py:177
  65.2 8.9 %all-to-all-done.1 = bf16[1,32,2,128,128]{4,3,2,0,1:T(8,128)(2,1)S(1)} async-done(((bf16[1,32,2,128,128]{4,3,2,0,1:T(8,128)(2,1)}), bf16[1,32,2,128,128]{4,3,2,0,1:T(8,128)(2,1)S(1)}, u32[]{:S(2)}, u32[]{:S(2)}) %all-to-all-start.1) | async-done | bytes 2097184 | tf_op jit(solution)/shard_map/all_to_all | solution.py:201
  74.2 2.2 %broadcast_in_dim.7.mask_ref = bf16[2,16,256,128]{3,2,1,0:T(8,128)(2,1)} broadcast(bf16[2,16,256]{2,1,0:T(8,128)(2,1)S(1)} %get-tuple-element.7), dimensions={0,1,2} | broadcast | bytes 2113536 | tf_op jit(solution)/shard_map/broadcast_in_dim | solution.py:203
  76.4 0.0 copy-done.2
  76.4 33.2 %shard_map.47 = bf16[32,2,2,64,128]{4,3,2,1,0:T(8,128)(2,1)} custom-call(s32[2]{0:T(128)} %get-tuple-element.9.counts_ref, f32[8]{0:T(128)} %power_multiply_fusion.scales_ref, bf16[32,2,128,128]{3,2,1,0:T(8,128)(2,1)} %bitcast.27, bf16[2,16,256,128]{3,2,1,0:T(8,128)(2,1)} %broadcast_in_dim.7.mask_ref, bf16[4,256,512]{2,1,0:T(8,128)(2,1)} %constant.33.clone.tab_ref), custom_call_target="tpu_custom_call" | custom-call | tf_op jit(solution)/shard_map/pallas_call | solution.py:177
  109.6 0.0 copy-done
  109.6 1.4 fusion.4
  111.0 0.0 copy-start.1
  111.1 2.1 %collective-permute-start = (bf16[32,64,128]{2,1,0:T(8,128)(2,1)S(1)}, bf16[32,64,128]{2,1,0:T(8,128)(2,1)S(1)}, u32[]{:S(2)}, u32[]{:S(2)}) collective-permute-start(bf16[32,64,128]{2,1,0:T(8,128)(2,1)S(1)} %slice_bitcast_fusion), channel_id=1, source_target_pairs={{0,4},{4,8},{8,12},{12,16},{16,20},{20,24},{24,28},{28,32},{32,36}... | collective-permute-start | bytes 1572872 | tf_op jit(solution)/shard_map/ppermute | solution.py:15
  113.2 0.2 slice.45
  113.3 36.8 %collective-permute-done = bf16[32,64,128]{2,1,0:T(8,128)(2,1)S(1)} collective-permute-done((bf16[32,64,128]{2,1,0:T(8,128)(2,1)S(1)}, bf16[32,64,128]{2,1,0:T(8,128)(2,1)S(1)}, u32[]{:S(2)}, u32[]{:S(2)}) %collective-permute-start) | collective-permute-done | bytes 524320 | tf_op jit(solution)/shard_map/ppermute | solution.py:15
  150.1 0.0 copy-done.1
  150.1 1.2 fusion.1
  151.3 31.2 %all_to_all.23 = bf16[32,4,64,128]{3,2,1,0:T(8,128)(2,1)S(1)} all-to-all(bf16[32,4,64,128]{3,2,1,0:T(8,128)(2,1)S(1)} %fusion.1), channel_id=1, replica_groups=mesh['shot'=32,'az'=4] {'shot'}, dimensions={0} | all-to-all | bytes 4194304 | tf_op jit(solution)/shard_map/all_to_all | solution.py:214
  182.5 1.3 copy.12
  (6 shorter events, 0.1 us)
Async XLA Ops:
  41.7 4.8 %copy-start.4 = (s32[1,4]{1,0:T(1,128)S(1)}, s32[1,4]{1,0:T(1,128)}, u32[]{:S(2)}) copy-start(s32[1,4]{1,0:T(1,128)} %param.6) | copy-start | bytes 52
  41.7 5.5 %copy-start.3 = (s32[1,4,16,256]{3,2,1,0:T(8,128)S(1)}, s32[1,4,16,256]{3,2,1,0:T(8,128)}, u32[]{:S(2)}) copy-start(s32[1,4,16,256]{3,2,1,0:T(8,128)} %param.5) | copy-start | bytes 196612
  41.7 32.5 %all-to-all-start.1 = ((bf16[1,32,2,128,128]{4,3,2,0,1:T(8,128)(2,1)}), bf16[1,32,2,128,128]{4,3,2,0,1:T(8,128)(2,1)S(1)}, u32[]{:S(2)}, u32[]{:S(2)}) async-start(bf16[1,32,2,128,128]{4,3,2,0,1:T(8,128)(2,1)} %get-tuple-element.5), calls=%async_computation.1 | async-start | bytes 4194304 | tf_op jit(solution)/shard_map/all_to_all | solution.py:201
  74.2 2.2 %copy-start.2 = (bf16[1,32,2,128,128]{4,3,2,0,1:T(8,128)(2,1)}, bf16[1,32,2,128,128]{4,3,2,0,1:T(8,128)(2,1)S(1)}, u32[]{:S(2)}) copy-start(bf16[1,32,2,128,128]{4,3,2,0,1:T(8,128)(2,1)S(1)} %all-to-all-done.1) | copy-start | bytes 6291460
  76.4 33.2 %copy-start = (bf16[32,2,2,64,128]{4,3,2,1,0:T(8,128)(2,1)S(1)}, bf16[32,2,2,64,128]{4,3,2,1,0:T(8,128)(2,1)}, u32[]{:S(2)}) copy-start(bf16[32,2,2,64,128]{4,3,2,1,0:T(8,128)(2,1)} %shard_map.46) | copy-start | bytes 6291460
  111.0 39.1 %copy-start.1 = (bf16[32,2,2,64,128]{4,3,2,1,0:T(8,128)(2,1)S(1)}, bf16[32,2,2,64,128]{4,3,2,1,0:T(8,128)(2,1)}, u32[]{:S(2)}) copy-start(bf16[32,2,2,64,128]{4,3,2,1,0:T(8,128)(2,1)} %shard_map.47) | copy-start | bytes 6291460
  111.1 39.0 %collective-permute-start = (bf16[32,64,128]{2,1,0:T(8,128)(2,1)S(1)}, bf16[32,64,128]{2,1,0:T(8,128)(2,1)S(1)}, u32[]{:S(2)}, u32[]{:S(2)}) collective-permute-start(bf16[32,64,128]{2,1,0:T(8,128)(2,1)S(1)} %slice_bitcast_fusion), channel_id=1, source_target_pairs={{0,4},{4,8},{8,12},{12,16},{16,20},{20,24},{24,28},{28,32},{32,36}... | collective-permute-start | bytes 1572872 | tf_op jit(solution)/shard_map/ppermute | solution.py:15
